TPU v7x, 256 devices: a whole 4x4x8 slice. The times are simulated.
256 devices in a mesh: dom: 32 (over y_hi, z, core), tp: 8 (over x, y_lo).
Axes of the slice: x: 4, y: 4 (y_hi: 2, y_lo: 2; y = y_hi * 2 + y_lo), z: 8, core: 2. Of those that a mesh axis runs over, the one named last changes fastest.
Arguments:
- hidden_in: bfloat16 [448, 64, 4096], P('dom', None, 'tp'), may hold values from -6 to 6
- query_weight: bfloat16 [4096, 4096], P('dom', 'tp'), may hold values from -0.09375 to 0.09375
- segment_keys: bfloat16 [448, 64, 1024], P('dom', None, 'tp'), may hold values from -6 to 6
- segment_values: bfloat16 [448, 64, 1024], P('dom', None, 'tp'), may hold values from -6 to 6
- prefix_keys: bfloat16 [32, 256, 1024], P('dom', None, 'tp'), may hold values from -80 to 80
- prefix_values: bfloat16 [32, 256, 1024], P('dom', None, 'tp'), may hold values from -6 to 6
- ancestors: int32 [448], P('dom'), may hold values from 0 to 31, as said below
- twist_weights: float32 [448], P('dom'), may hold values from 0.25 to 4
- out_grad: bfloat16 [448, 64, 4096], P('dom', None, 'tp'), may hold values from -24 to 24
Outputs:
- grad_query_weight: bfloat16 [4096, 4096], P('dom', 'tp')
- grad_segment_keys: bfloat16 [448, 64, 1024], P('dom', None, 'tp')
- grad_segment_values: bfloat16 [448, 64, 1024], P('dom', None, 'tp')
- grad_prefix_keys: float32 [32, 256, 1024], P('dom', None, 'tp')
- grad_prefix_values: float32 [32, 256, 1024], P('dom', None, 'tp')
Inputs may be any that keep to these rules, and one draw needn't show every extreme that they name: `ancestors`: among the 14 consecutive particles of one device, no ancestor is named more than 2 times, and one ancestor, the same for all devices, is named exactly 2 times on every device.
All inputs are finite; a program needn't handle non-finite values.
Results may differ from a plain program's by a relative error of at most 0.02.
The roundings to bfloat16 on the way count: a program that leaves them out, or rounds other values in their place, can miss the bound.
Values may be sent and summed in bfloat16 or wider, within the bound.
No kernel may reach another device: no remote copies, remote signals or barrier semaphores. Data moves between devices by JAX's collectives and lax.ppermute only.
A program may use at most 128 MiB of HBM per device.

v0:
```python
import math

import jax
import jax.numpy as jnp
from jax import lax
from jax.sharding import PartitionSpec as P

HD = 128


def attend(queries, scaled, seg_keys, seg_values, pre_keys, pre_values):
    factor = 1.0 / math.sqrt(queries.shape[-1])
    score_pre = (
        jnp.einsum("bikgd,bjkd->bkgij", queries, pre_keys, preferred_element_type=jnp.float32)
        * factor
    )
    score_seg = (
        jnp.einsum("bikgd,bjkd->bkgij", queries, seg_keys, preferred_element_type=jnp.float32)
        * factor
    )
    length = queries.shape[1]
    causal = lax.broadcasted_iota(jnp.int32, (length, length), 0) >= lax.broadcasted_iota(
        jnp.int32, (length, length), 1
    )
    score_seg = jnp.where(causal, score_seg, -jnp.inf)
    row_max = jnp.maximum(jnp.max(score_pre, -1), jnp.max(score_seg, -1))[..., None]
    exp_pre = jnp.exp(score_pre - row_max)
    exp_seg = jnp.exp(score_seg - row_max)
    denominator = (jnp.sum(exp_pre, -1) + jnp.sum(exp_seg, -1))[..., None]
    prob_pre = exp_pre / denominator
    prob_seg = exp_seg / denominator
    dprob_pre = jnp.einsum(
        "bikgd,bjkd->bkgij", scaled, pre_values, preferred_element_type=jnp.float32
    )
    dprob_seg = jnp.einsum(
        "bikgd,bjkd->bkgij", scaled, seg_values, preferred_element_type=jnp.float32
    )
    row_delta = (jnp.sum(prob_pre * dprob_pre, -1) + jnp.sum(prob_seg * dprob_seg, -1))[..., None]
    dscore_pre = (prob_pre * (dprob_pre - row_delta)).astype(jnp.bfloat16)
    dscore_seg = (prob_seg * (dprob_seg - row_delta)).astype(jnp.bfloat16)
    grad_q = (
        jnp.einsum("bkgij,bjkd->bikgd", dscore_pre, pre_keys, preferred_element_type=jnp.float32)
        + jnp.einsum("bkgij,bjkd->bikgd", dscore_seg, seg_keys, preferred_element_type=jnp.float32)
    ) * factor
    grad_pk = (
        jnp.einsum("bkgij,bikgd->bjkd", dscore_pre, queries, preferred_element_type=jnp.float32)
        * factor
    )
    grad_pv = jnp.einsum(
        "bkgij,bikgd->bjkd",
        prob_pre.astype(jnp.bfloat16),
        scaled,
        preferred_element_type=jnp.float32,
    )
    grad_sk = (
        jnp.einsum("bkgij,bikgd->bjkd", dscore_seg, queries, preferred_element_type=jnp.float32)
        * factor
    )
    grad_sv = jnp.einsum(
        "bkgij,bikgd->bjkd",
        prob_seg.astype(jnp.bfloat16),
        scaled,
        preferred_element_type=jnp.float32,
    )
    return (
        grad_q.astype(jnp.bfloat16),
        grad_sk.astype(jnp.bfloat16),
        grad_sv.astype(jnp.bfloat16),
        grad_pk,
        grad_pv,
    )


def local(
    hidden_in,
    query_weight,
    segment_keys,
    segment_values,
    prefix_keys,
    prefix_values,
    ancestors,
    twist_weights,
    out_grad,
):
    particles_here = hidden_in.shape[0]
    length = hidden_in.shape[1]
    features = lax.all_gather(hidden_in, "tp", axis=2, tiled=True)
    token_rows = features.reshape(particles_here * length, features.shape[2])
    width_q = query_weight.shape[1]
    width_kv = segment_keys.shape[2]
    kv_heads = width_kv // HD
    group_size = width_q // width_kv
    prefix = prefix_keys.shape[1]
    columns = token_rows
    queries = jnp.dot(
        columns,
        lax.all_gather(query_weight, "dom", axis=0, tiled=True),
        preferred_element_type=jnp.float32,
    ).astype(jnp.bfloat16)
    queries = queries.reshape(particles_here, length, width_q)
    scaled = (out_grad.astype(jnp.float32) * twist_weights[:, None, None]).astype(jnp.bfloat16)
    owners = lax.axis_size("dom")
    capacity = max(2, (2 * particles_here + owners - 1) // owners)
    positions = jnp.arange(particles_here, dtype=jnp.int32)
    shared = ancestors[:, None] == ancestors[None, :]
    slot_rank = jnp.sum(
        (shared & (positions[:, None] > positions[None, :])).astype(jnp.int32), axis=1
    )
    owner_ids = jnp.arange(owners, dtype=jnp.int32)
    slot_ids = jnp.arange(capacity, dtype=jnp.int32)
    slot_table = (
        (ancestors[None, None, :] == owner_ids[:, None, None])
        & (slot_rank[None, None, :] == slot_ids[None, :, None])
    ).astype(jnp.bfloat16)

    def to_slots(block):
        return jnp.einsum(
            "acp,piw->aciw", slot_table, block, preferred_element_type=jnp.float32
        ).astype(jnp.bfloat16)

    def from_slots(block):
        return jnp.einsum(
            "acp,aciw->piw", slot_table, block, preferred_element_type=jnp.float32
        ).astype(jnp.bfloat16)

    arrived = (
        lax.all_to_all(to_slots(queries), "dom", split_axis=0, concat_axis=0, tiled=True),
        lax.all_to_all(to_slots(scaled), "dom", split_axis=0, concat_axis=0, tiled=True),
        lax.all_to_all(to_slots(segment_keys), "dom", split_axis=0, concat_axis=0, tiled=True),
        lax.all_to_all(to_slots(segment_values), "dom", split_axis=0, concat_axis=0, tiled=True),
    )
    sources = max(
        (
            divisor
            for divisor in range(1, owners + 1)
            if owners % divisor == 0 and divisor * capacity <= max(particles_here, capacity)
        )
    )
    block_count = owners // sources
    slot_count = sources * capacity
    own_keys = jnp.broadcast_to(
        prefix_keys.reshape(1, prefix, kv_heads, HD), (slot_count, prefix, kv_heads, HD)
    )
    own_values = jnp.broadcast_to(
        prefix_values.reshape(1, prefix, kv_heads, HD), (slot_count, prefix, kv_heads, HD)
    )

    def handle(carried, entry):
        slot_q, slot_o, slot_k, slot_v = entry
        grad_q, grad_sk, grad_sv, grad_pk, grad_pv = attend(
            slot_q.reshape(slot_count, length, kv_heads, group_size, HD),
            slot_o.reshape(slot_count, length, kv_heads, group_size, HD),
            slot_k.reshape(slot_count, length, kv_heads, HD),
            slot_v.reshape(slot_count, length, kv_heads, HD),
            own_keys,
            own_values,
        )
        updated = (carried[0] + jnp.sum(grad_pk, 0), carried[1] + jnp.sum(grad_pv, 0))
        return (
            updated,
            (
                grad_q.reshape(slot_count, length, width_q),
                grad_sk.reshape(slot_count, length, width_kv),
                grad_sv.reshape(slot_count, length, width_kv),
            ),
        )

    blocks = tuple(
        (member.reshape(block_count, slot_count, length, member.shape[-1]) for member in arrived)
    )
    nothing = jnp.zeros((prefix, kv_heads, HD), jnp.float32)
    (sum_keys, sum_values), (out_q, out_k, out_v) = lax.scan(handle, (nothing, nothing), blocks)
    returned = (
        lax.all_to_all(
            out_q.reshape(owners, capacity, length, width_q),
            "dom",
            split_axis=0,
            concat_axis=0,
            tiled=True,
        ),
        lax.all_to_all(
            out_k.reshape(owners, capacity, length, width_kv),
            "dom",
            split_axis=0,
            concat_axis=0,
            tiled=True,
        ),
        lax.all_to_all(
            out_v.reshape(owners, capacity, length, width_kv),
            "dom",
            split_axis=0,
            concat_axis=0,
            tiled=True,
        ),
    )
    grad_queries = from_slots(returned[0])
    grad_seg_keys = from_slots(returned[1])
    grad_seg_values = from_slots(returned[2])
    grad_pre_keys = sum_keys.reshape(1, prefix, width_kv)
    grad_pre_values = sum_values.reshape(1, prefix, width_kv)
    grad_rows = grad_queries.reshape(particles_here * length, width_q)
    columns = token_rows
    grad_weight = lax.psum_scatter(
        jnp.einsum("tc,tq->cq", columns, grad_rows, preferred_element_type=jnp.float32).astype(
            jnp.bfloat16
        ),
        "dom",
        scatter_dimension=0,
        tiled=True,
    )
    return (grad_weight, grad_seg_keys, grad_seg_values, grad_pre_keys, grad_pre_values)


def solution(mesh):
    return jax.shard_map(
        local,
        mesh=mesh,
        in_specs=(
            P("dom", None, "tp"),
            P("dom", "tp"),
            P("dom", None, "tp"),
            P("dom", None, "tp"),
            P("dom", None, "tp"),
            P("dom", None, "tp"),
            P("dom"),
            P("dom"),
            P("dom", None, "tp"),
        ),
        out_specs=(
            P("dom", "tp"),
            P("dom", None, "tp"),
            P("dom", None, "tp"),
            P("dom", None, "tp"),
            P("dom", None, "tp"),
        ),
        check_vma=False,
    )
```

profile of v0, /device:TPU:2, one launch (start us, length us, event | category | flops | bytes accessed | tf_op | source)
XLA Modules:
  0.0 876.4 jit_solution(134274365021562520)
XLA Ops:
  13.3 11.6 %all-to-all-start.3 = ((bf16[32,2,64,128]{3,2,1,0:T(8,128)(2,1)}), bf16[32,2,64,128]{3,2,1,0:T(8,128)(2,1)S(1)}, u32[]{:S(2)}, u32[]{:S(2)}) async-start(bf16[32,2,64,128]{3,2,1,0:T(8,128)(2,1)} %copy.158), calls=%async_computation.3 | async-start | bytes 2097152 | tf_op jit(solution)/shard_map/all_to_all | solution.py:130
  26.9 32.4 %all-to-all-done.3 = bf16[32,2,64,128]{3,2,1,0:T(8,128)(2,1)S(1)} async-done(((bf16[32,2,64,128]{3,2,1,0:T(8,128)(2,1)}), bf16[32,2,64,128]{3,2,1,0:T(8,128)(2,1)S(1)}, u32[]{:S(2)}, u32[]{:S(2)}) %all-to-all-start.3) | async-done | bytes 1048608 | tf_op jit(solution)/shard_map/all_to_all | solution.py:130
  59.3 4.7 all-to-all-start.1
  65.6 4.4 copy.156
  70.0 27.1 %all-to-all-done.1 = bf16[32,2,64,128]{3,2,1,0:T(8,128)(2,1)} async-done(((bf16[32,2,64,128]{3,2,1,0:T(8,128)(2,1)}), bf16[32,2,64,128]{3,2,1,0:T(8,128)(2,1)}, u32[]{:S(2)}, u32[]{:S(2)}) %all-to-all-start.1) | async-done | bytes 1048608 | tf_op jit(solution)/shard_map/all_to_all | solution.py:129
  97.1 5.4 all-to-all-start.2
  102.6 21.5 %all-gather.5.cloned.1.call-done = bf16[4096,512]{1,0:T(8,128)(2,1)} async-done(((bf16[128,512]{1,0:T(8,128)(2,1)}), bf16[4096,512]{1,0:T(8,128)(2,1)}) %all-gather.5.cloned.1.call-update) | async-done | bytes 4194320 | tf_op jit(solution)/shard_map/all_gather | solution.py:97
  124.0 178.3 %all-gather.3.cloned.1.call-done = bf16[14,64,4096]{2,1,0:T(8,128)(2,1)} async-done(((bf16[14,64,512]{2,1,0:T(8,128)(2,1)}), bf16[14,64,4096]{2,1,0:T(8,128)(2,1)}) %all-gather.3.cloned.1.call-update) | async-done | bytes 7340048 | tf_op jit(solution)/shard_map/all_gather | solution.py:87
  302.3 8.2 convolution_convert_fusion.4
  311.9 4.4 copy.152
  316.3 8.2 all-to-all-start
  324.8 96.4 %all-to-all-done = bf16[32,2,64,512]{3,2,1,0:T(8,128)(2,1)} async-done(((bf16[32,2,64,512]{3,2,1,0:T(8,128)(2,1)}), bf16[32,2,64,512]{3,2,1,0:T(8,128)(2,1)}, u32[]{:S(2)}, u32[]{:S(2)}) %all-to-all-start) | async-done | bytes 4194336 | tf_op jit(solution)/shard_map/all_to_all | solution.py:127
  421.2 185.9 %while.19 = (s32[]{:T(128)}, f32[256,1,128]{0,2,1:T(8,128)S(1)}, f32[256,1,128]{0,2,1:T(8,128)S(1)}, bf16[8,8,64,512]{3,2,1,0:T(8,128)(2,1)}, bf16[8,8,64,128]{3...) while((s32[]{:T(128)}, f32[256,1,128]{0,2,1:T(8,128)S(1)}, ...), condition=%wide.region_9.10_spmd.clone, body=%wide.region_1.9_spmd.clone.sunk | while | flops 851605504 | bytes 65064360 | solution.py:172
  607.1 6.5 copy.159
  613.6 103.7 %all_to_all.35 = bf16[32,2,64,512]{3,1,2,0:T(2,128)(2,1)S(1)} all-to-all(bf16[32,2,64,512]{3,1,2,0:T(2,128)(2,1)S(1)} %copy.159), channel_id=1, replica_groups=mesh['dom'=32,'tp'=8] {'dom'}, dimensions={0} | all-to-all | bytes 8388608 | tf_op jit(solution)/shard_map/all_to_all | solution.py:174
  717.4 2.4 bitcast_convert_fusion.1
  719.8 9.5 %fusion.58 = bf16[4096,512]{0,1:T(8,128)(2,1)} fusion(bf16[14,64,4096]{2,1,0:T(8,128)(2,1)} %all-gather.3.cloned.1.call-done, bf16[14,64,512]{2,0,1:T(8,128)(2,1)S(1)} %bitcast_convert_fusion.1), kind=kOutput, calls=%fused_computation.77 | convolution fusion | flops 3760193536 | bytes 12451840 | tf_op jit(solution)/shard_map/tc,tq->cq/dot_general | solution.py:204
  729.3 6.5 copy.184
  739.0 3.9 all-to-all-start.5
  742.9 2.1 copy.164
  745.0 27.9 %all-to-all-done.5 = bf16[32,2,64,128]{3,1,2,0:T(2,128)(2,1)S(1)} async-done(((bf16[32,2,64,128]{3,1,2,0:T(2,128)(2,1)}), bf16[32,2,64,128]{3,1,2,0:T(2,128)(2,1)S(1)}, u32[]{:S(2)}, u32[]{:S(2)}) %all-to-all-start.5) | async-done | bytes 1048608 | tf_op jit(solution)/shard_map/all_to_all | solution.py:181
  772.9 4.0 all-to-all-start.6
  779.8 29.1 %all-to-all-done.6 = bf16[32,2,64,128]{3,1,2,0:T(2,128)(2,1)S(1)} async-done(((bf16[32,2,64,128]{3,1,2,0:T(2,128)(2,1)}), bf16[32,2,64,128]{3,1,2,0:T(2,128)(2,1)S(1)}, u32[]{:S(2)}, u32[]{:S(2)}) %all-to-all-start.6) | async-done | bytes 1048608 | tf_op jit(solution)/shard_map/all_to_all | solution.py:188
  810.4 59.2 %reduce-scatter.4.cloned.1.call-done = bf16[128,512]{1,0:T(8,128)(2,1)} async-done(((bf16[4096,512]{1,0:T(8,128)(2,1)}), bf16[128,512]{1,0:T(8,128)(2,1)}) %reduce-scatter.4.cloned.1.call-update) | async-done | bytes 131088
  (401 shorter events, 203.3 us)
Async XLA Ops:
  7.2 17.7 %copy-start.13 = (bf16[14,64,128]{2,1,0:T(8,128)(2,1)S(1)}, bf16[14,64,128]{2,1,0:T(8,128)(2,1)}, u32[]{:S(2)}) copy-start(bf16[14,64,128]{2,1,0:T(8,128)(2,1)} %param.13) | copy-start | bytes 688132
  7.2 116.9 %all-gather.5.cloned.1.call-start = ((), (), s32[]{:S(2)}) async-start(), calls=%async_computation.9 | async-start | bytes 4325376 | tf_op jit(solution)/shard_map/all_gather | solution.py:97
  7.9 294.4 %all-gather.3.cloned.1.call-start = ((), (), s32[]{:S(2)}) async-start(), calls=%async_computation.8 | async-start | bytes 8257536 | tf_op jit(solution)/shard_map/all_gather | solution.py:87
  13.3 50.7 %copy-start.12 = (bf16[14,64,512]{2,1,0:T(8,128)(2,1)S(1)}, bf16[14,64,512]{2,1,0:T(8,128)(2,1)}, u32[]{:S(2)}) copy-start(bf16[14,64,512]{2,1,0:T(8,128)(2,1)} %param.19) | copy-start | bytes 2752516
  13.3 50.7 %copy-start.14 = (f32[14]{0:T(128)S(1)}, f32[14]{0:T(128)}, u32[]{:S(2)}) copy-start(f32[14]{0:T(128)} %param.18) | copy-start | bytes 172
  13.3 46.0 %all-to-all-start.3 = ((bf16[32,2,64,128]{3,2,1,0:T(8,128)(2,1)}), bf16[32,2,64,128]{3,2,1,0:T(8,128)(2,1)S(1)}, u32[]{:S(2)}, u32[]{:S(2)}) async-start(bf16[32,2,64,128]{3,2,1,0:T(8,128)(2,1)} %copy.158), calls=%async_computation.3 | async-start | bytes 2097152 | tf_op jit(solution)/shard_map/all_to_all | solution.py:130
  59.3 37.8 %all-to-all-start.1 = ((bf16[32,2,64,128]{3,2,1,0:T(8,128)(2,1)}), bf16[32,2,64,128]{3,2,1,0:T(8,128)(2,1)}, u32[]{:S(2)}, u32[]{:S(2)}) async-start(bf16[32,2,64,128]{3,2,1,0:T(8,128)(2,1)} %copy.154), calls=%async_computation.1 | async-start | bytes 2097152 | tf_op jit(solution)/shard_map/all_to_all | solution.py:129
  97.1 219.2 %all-to-all-start.2 = ((bf16[32,2,64,512]{3,2,1,0:T(8,128)(2,1)}), bf16[32,2,64,512]{3,2,1,0:T(8,128)(2,1)}, u32[]{:S(2)}, u32[]{:S(2)}) async-start(bf16[32,2,64,512]{3,2,1,0:T(8,128)(2,1)} %copy.156), calls=%async_computation.2 | async-start | bytes 8388608 | tf_op jit(solution)/shard_map/all_to_all | solution.py:128
  316.3 104.9 %copy-start.7 = (bf16[1,256,128]{2,1,0:T(8,128)(2,1)S(1)}, bf16[1,256,128]{2,1,0:T(8,128)(2,1)}, u32[]{:S(2)}) copy-start(bf16[1,256,128]{2,1,0:T(8,128)(2,1)} %param.15) | copy-start | bytes 196612
  316.3 104.9 %all-to-all-start = ((bf16[32,2,64,512]{3,2,1,0:T(8,128)(2,1)}), bf16[32,2,64,512]{3,2,1,0:T(8,128)(2,1)}, u32[]{:S(2)}, u32[]{:S(2)}) async-start(bf16[32,2,64,512]{3,2,1,0:T(8,128)(2,1)} %copy.152), calls=%async_computation | async-start | bytes 8388608 | tf_op jit(solution)/shard_map/all_to_all | solution.py:127
  324.5 545.1 %reduce-scatter.4.cloned.1.call-start = ((), (), s32[]{:S(2)}) async-start(), calls=%async_computation.10 | async-start | bytes 4325376
  435.7 5.5 copy-start.6
  459.0 5.5 copy-start.6
  482.2 5.5 copy-start.6
  505.5 5.5 copy-start.6
  528.7 5.5 copy-start.6
  551.9 5.5 copy-start.6
  575.1 5.5 copy-start.6
  578.6 4.8 copy-start.3
  598.4 5.5 copy-start.6
  601.8 4.8 copy-start.3
  735.7 7.2 copy-start.11
  739.0 33.9 %all-to-all-start.5 = ((bf16[32,2,64,128]{3,1,2,0:T(2,128)(2,1)}), bf16[32,2,64,128]{3,1,2,0:T(2,128)(2,1)S(1)}, u32[]{:S(2)}, u32[]{:S(2)}) async-start(bf16[32,2,64,128]{3,1,2,0:T(2,128)(2,1)} %copy.162), calls=%async_computation.5 | async-start | bytes 2097152 | tf_op jit(solution)/shard_map/all_to_all | solution.py:181
  772.9 36.1 %all-to-all-start.6 = ((bf16[32,2,64,128]{3,1,2,0:T(2,128)(2,1)}), bf16[32,2,64,128]{3,1,2,0:T(2,128)(2,1)S(1)}, u32[]{:S(2)}, u32[]{:S(2)}) async-start(bf16[32,2,64,128]{3,1,2,0:T(2,128)(2,1)} %copy.164), calls=%async_computation.6 | async-start | bytes 2097152 | tf_op jit(solution)/shard_map/all_to_all | solution.py:188
  (71 other events, 159.4 us)
Sparse Core Ops, SparseCore 0:
  10.8 113.2 all-gather.4
  125.8 176.4 all-gather.2
  735.9 133.7 reduce-scatter.3
where the time goes:
time: 885 us; the launch traced here: 876 us
  waiting for transfers between devices  473 us (53%)
  matrix products  131 us (15%)
  blocking collectives  104 us (12%)
  local copies, waits for them, and re-layouts  86.7 us (10%)
  starting transfers between devices  38.1 us (4%)
  other arithmetic  27.5 us (3%)
  between operations  14.2 us (2%)
    all_gather x1, waiting for transfers between devices, local(): features = lax.all_gather(hidden_in, 'tp', axis=2, tiled=True)  178 us
    all_to_all x1, blocking collectives, local(): lax.all_to_all(out_q.reshape(owners, capacity, length, width_q), 'dom', s...  104 us
    all_to_all x1, waiting for transfers between devices, local(): lax.all_to_all(to_slots(queries), 'dom', split_axis=0, concat_axis=0, til...  96.4 us
    unnamed x4, waiting for transfers between devices  60.6 us
    all_to_all x1, waiting for transfers between devices, local(): lax.all_to_all(to_slots(segment_values), 'dom', split_axis=0, concat_axis...  32.4 us
    all_to_all x1, waiting for transfers between devices, local(): lax.all_to_all(out_v.reshape(owners, capacity, length, width_kv), 'dom',...  29.1 us
    all_to_all x1, waiting for transfers between devices, local(): lax.all_to_all(out_k.reshape(owners, capacity, length, width_kv), 'dom',...  27.9 us
    all_to_all x1, waiting for transfers between devices, local(): lax.all_to_all(to_slots(segment_keys), 'dom', split_axis=0, concat_axis=0...  27.1 us
  transfers between devices with their start and end apart: 9, of which 8 were waited for; matrix products, arithmetic and copies ran while one was open for 4% of the time, Pallas kernels for 0%

commit v1 on v0

v1 whole, which is shorter than its diff:
```python
import math

import jax
import jax.numpy as jnp
from jax import lax
from jax.sharding import PartitionSpec as P

HD = 128


def attend(queries, scaled, seg_keys, seg_values, pre_keys, pre_values):
    factor = 1.0 / math.sqrt(queries.shape[-1])
    score_pre = (
        jnp.einsum("bikgd,bjkd->bkgij", queries, pre_keys, preferred_element_type=jnp.float32)
        * factor
    )
    score_seg = (
        jnp.einsum("bikgd,bjkd->bkgij", queries, seg_keys, preferred_element_type=jnp.float32)
        * factor
    )
    length = queries.shape[1]
    causal = lax.broadcasted_iota(jnp.int32, (length, length), 0) >= lax.broadcasted_iota(
        jnp.int32, (length, length), 1
    )
    score_seg = jnp.where(causal, score_seg, -jnp.inf)
    row_max = jnp.maximum(jnp.max(score_pre, -1), jnp.max(score_seg, -1))[..., None]
    exp_pre = jnp.exp(score_pre - row_max)
    exp_seg = jnp.exp(score_seg - row_max)
    denominator = (jnp.sum(exp_pre, -1) + jnp.sum(exp_seg, -1))[..., None]
    prob_pre = exp_pre / denominator
    prob_seg = exp_seg / denominator
    dprob_pre = jnp.einsum(
        "bikgd,bjkd->bkgij", scaled, pre_values, preferred_element_type=jnp.float32
    )
    dprob_seg = jnp.einsum(
        "bikgd,bjkd->bkgij", scaled, seg_values, preferred_element_type=jnp.float32
    )
    row_delta = (jnp.sum(prob_pre * dprob_pre, -1) + jnp.sum(prob_seg * dprob_seg, -1))[..., None]
    dscore_pre = (prob_pre * (dprob_pre - row_delta)).astype(jnp.bfloat16)
    dscore_seg = (prob_seg * (dprob_seg - row_delta)).astype(jnp.bfloat16)
    grad_q = (
        jnp.einsum("bkgij,bjkd->bikgd", dscore_pre, pre_keys, preferred_element_type=jnp.float32)
        + jnp.einsum("bkgij,bjkd->bikgd", dscore_seg, seg_keys, preferred_element_type=jnp.float32)
    ) * factor
    grad_pk = (
        jnp.einsum("bkgij,bikgd->bjkd", dscore_pre, queries, preferred_element_type=jnp.float32)
        * factor
    )
    grad_pv = jnp.einsum(
        "bkgij,bikgd->bjkd",
        prob_pre.astype(jnp.bfloat16),
        scaled,
        preferred_element_type=jnp.float32,
    )
    grad_sk = (
        jnp.einsum("bkgij,bikgd->bjkd", dscore_seg, queries, preferred_element_type=jnp.float32)
        * factor
    )
    grad_sv = jnp.einsum(
        "bkgij,bikgd->bjkd",
        prob_seg.astype(jnp.bfloat16),
        scaled,
        preferred_element_type=jnp.float32,
    )
    return (
        grad_q.astype(jnp.bfloat16),
        grad_sk.astype(jnp.bfloat16),
        grad_sv.astype(jnp.bfloat16),
        grad_pk,
        grad_pv,
    )


def local(
    hidden_in,
    query_weight,
    segment_keys,
    segment_values,
    prefix_keys,
    prefix_values,
    ancestors,
    twist_weights,
    out_grad,
):
    particles_here = hidden_in.shape[0]
    length = hidden_in.shape[1]
    owners = lax.axis_size("dom")
    features = lax.all_gather(hidden_in, "tp", axis=2, tiled=True)
    token_rows = features.reshape(particles_here * length, features.shape[2])
    width_q = query_weight.shape[1]
    width_kv = segment_keys.shape[2]
    kv_heads = width_kv // HD
    group_size = width_q // width_kv
    prefix = prefix_keys.shape[1]
    queries = jnp.dot(
        token_rows,
        lax.all_gather(query_weight, "dom", axis=0, tiled=True),
        preferred_element_type=jnp.float32,
    ).astype(jnp.bfloat16)
    queries = queries.reshape(particles_here, length, width_q)
    scaled = (out_grad.astype(jnp.float32) * twist_weights[:, None, None]).astype(jnp.bfloat16)

    own_kv = jnp.concatenate([prefix_keys, prefix_values], axis=2)
    every_kv = lax.all_to_all(
        jnp.broadcast_to(own_kv, (owners,) + own_kv.shape[1:]),
        "dom",
        split_axis=0,
        concat_axis=0,
        tiled=True,
    )
    picked = jnp.take(every_kv, ancestors, axis=0)
    pre_keys = picked[:, :, :width_kv]
    pre_values = picked[:, :, width_kv:]

    grad_q, grad_sk, grad_sv, grad_pk, grad_pv = attend(
        queries.reshape(particles_here, length, kv_heads, group_size, HD),
        scaled.reshape(particles_here, length, kv_heads, group_size, HD),
        segment_keys.reshape(particles_here, length, kv_heads, HD),
        segment_values.reshape(particles_here, length, kv_heads, HD),
        pre_keys.reshape(particles_here, prefix, kv_heads, HD),
        pre_values.reshape(particles_here, prefix, kv_heads, HD),
    )
    grad_pkv = jnp.concatenate(
        [
            grad_pk.reshape(particles_here, prefix, width_kv),
            grad_pv.reshape(particles_here, prefix, width_kv),
        ],
        axis=2,
    )
    owner_ids = jnp.arange(owners, dtype=jnp.int32)
    onehot = (owner_ids[:, None] == ancestors[None, :]).astype(jnp.float32)
    outgoing = jnp.einsum(
        "ap,pjc->ajc", onehot, grad_pkv, precision=lax.Precision.HIGHEST
    )
    incoming = lax.all_to_all(outgoing, "dom", split_axis=0, concat_axis=0, tiled=True)
    summed = jnp.sum(incoming, axis=0)
    grad_pre_keys = summed[None, :, :width_kv]
    grad_pre_values = summed[None, :, width_kv:]

    grad_seg_keys = grad_sk.reshape(particles_here, length, width_kv)
    grad_seg_values = grad_sv.reshape(particles_here, length, width_kv)
    grad_rows = grad_q.reshape(particles_here * length, width_q)
    grad_weight = lax.psum_scatter(
        jnp.einsum("tc,tq->cq", token_rows, grad_rows, preferred_element_type=jnp.float32).astype(
            jnp.bfloat16
        ),
        "dom",
        scatter_dimension=0,
        tiled=True,
    )
    return (grad_weight, grad_seg_keys, grad_seg_values, grad_pre_keys, grad_pre_values)


def solution(mesh):
    return jax.shard_map(
        local,
        mesh=mesh,
        in_specs=(
            P("dom", None, "tp"),
            P("dom", "tp"),
            P("dom", None, "tp"),
            P("dom", None, "tp"),
            P("dom", None, "tp"),
            P("dom", None, "tp"),
            P("dom"),
            P("dom"),
            P("dom", None, "tp"),
        ),
        out_specs=(
            P("dom", "tp"),
            P("dom", None, "tp"),
            P("dom", None, "tp"),
            P("dom", None, "tp"),
            P("dom", None, "tp"),
        ),
        check_vma=False,
    )
```

time: 885 us -> 560 us (0.63)
  blocking collectives: 104 us -> 0 us
  matrix products: 131 us -> 38 us
  local copies, waits for them, and re-layouts: 86.7 us -> 34.3 us
  waiting for transfers between devices: 473 us -> 434 us
  starting transfers between devices: 38.1 us -> 21.6 us
  other arithmetic: 27.5 us -> 14.9 us
    all_to_all x1 -> x0, blocking collectives: 104 us -> none  [local(): lax.all_to_all(out_q.reshape(owners, capacity, length, width_q), 'dom', s...]
    all_to_all x6 -> x2, waiting for transfers between devices: 213 us -> 287 us  [the longest x1 176 us: local(): lax.all_to_all(outgoing, 'dom', split_axis=0, concat_axis=0, tiled=True)]
    unnamed x4, waiting for transfers between devices: 60.6 us -> 1.39 us
    all_gather x1, waiting for transfers between devices: 178 us -> 146 us  [local(): features = lax.all_gather(hidden_in, 'tp', axis=2, tiled=True)]
    all_gather x1, waiting for transfers between devices: 21.5 us -> 0.02 us  [local(): lax.all_gather(query_weight, 'dom', axis=0, tiled=True)]
    dynamic_slice x8 -> x0, local copies, waits for them, and re-layouts: 16.7 us -> none  [local(): lax.scan(handle, (nothing, nothing), blocks)]
    all_to_all x6 -> x2, starting transfers between devices: 37.8 us -> 21.4 us  [the longest x1 11.7 us: local(): lax.all_to_all(jnp.broadcast_to(own_kv, (owners,) + own_kv.shape[1:]), 'd...]
    dot_general x8 -> x1, matrix products: 16.5 us -> 1.08 us  [attend(): jnp.einsum('bkgij,bikgd->bjkd', dscore_seg, queries, preferred_element_ty...]
  transfers between devices with their start and end apart: 9 -> 5, of which waited for: 8 -> 3; matrix products, arithmetic and copies ran while one was open for 4% -> 7% of each run, Pallas kernels for 0% -> 0%
where the time goes in v1:
time: 560 us; the launch traced here: 557 us
  waiting for transfers between devices  434 us (78%)
  matrix products  38 us (7%)
  local copies, waits for them, and re-layouts  34.3 us (6%)
  starting transfers between devices  21.6 us (4%)
  other arithmetic  14.9 us (3%)
  between operations  14 us (2%)
    all_to_all x1, waiting for transfers between devices, local(): lax.all_to_all(outgoing, 'dom', split_axis=0, concat_axis=0, tiled=True)  176 us
    all_gather x1, waiting for transfers between devices, local(): features = lax.all_gather(hidden_in, 'tp', axis=2, tiled=True)  146 us
    all_to_all x1, waiting for transfers between devices, local(): lax.all_to_all(jnp.broadcast_to(own_kv, (owners,) + own_kv.shape[1:]), 'd...  111 us
    all_to_all x1, starting transfers between devices, local(): lax.all_to_all(jnp.broadcast_to(own_kv, (owners,) + own_kv.shape[1:]), 'd...  11.7 us
  transfers between devices with their start and end apart: 5, of which 3 were waited for; matrix products, arithmetic and copies ran while one was open for 7% of the time, Pallas kernels for 0%

profile of v1, /device:TPU:2, one launch (start us, length us, event | category | flops | bytes accessed | tf_op | source)
XLA Modules:
  0.0 556.5 jit_solution(17985210257255980945)
XLA Ops:
  9.6 2.4 broadcast_in_dim.41
  12.0 11.7 %all-to-all-start = ((bf16[32,256,256]{2,1,0:T(8,128)(2,1)}), bf16[32,256,256]{2,1,0:T(8,128)(2,1)}, u32[]{:S(2)}, u32[]{:S(2)}) async-start(bf16[32,256,256]{2,1,0:T(8,128)(2,1)} %broadcast_in_dim.41), calls=%async_computation | async-start | bytes 8388608 | tf_op jit(solution)/shard_map/all_to_all | solution.py:104
  23.8 111.2 %all-to-all-done = bf16[32,256,256]{2,1,0:T(8,128)(2,1)} async-done(((bf16[32,256,256]{2,1,0:T(8,128)(2,1)}), bf16[32,256,256]{2,1,0:T(8,128)(2,1)}, u32[]{:S(2)}, u32[]{:S(2)}) %all-to-all-start) | async-done | bytes 4194336 | tf_op jit(solution)/shard_map/all_to_all | solution.py:104
  135.1 4.2 gather_fusion
  139.2 1.7 broadcast_select_fusion
  141.0 145.5 %all-gather.3.cloned.1.call-done = bf16[14,64,4096]{2,1,0:T(8,128)(2,1)} async-done(((bf16[14,64,512]{2,1,0:T(8,128)(2,1)}), bf16[14,64,4096]{2,1,0:T(8,128)(2,1)}) %all-gather.3.cloned.1.call-update) | async-done | bytes 7340048 | tf_op jit(solution)/shard_map/all_gather | solution.py:88
  286.5 9.2 %convolution_convert_fusion.1 = bf16[896,512]{1,0:T(8,128)(2,1)} fusion(bf16[896,4096]{1,0:T(8,128)(2,1)} %bitcast.207, bf16[4096,512]{1,0:T(8,128)(2,1)} %all-gather.5.cloned.1.call-done), kind=kOutput, calls=%fused_computation.35 | convolution fusion | flops 3758555136 | bytes 12451840 | tf_op jit(solution)/shard_map/dot_general | solution.py:95
  295.7 1.9 reshape.161
  299.4 1.2 fusion.6
  301.8 2.6 fusion.1
  304.4 2.9 fusion.20
  307.4 2.4 fusion.13
  309.8 1.8 fusion.7
  312.0 2.2 pad_maximum_fusion
  314.2 5.4 copy.47
  319.6 5.7 %fusion.55 = f32[32,256,256]{2,0,1:T(8,128)S(1)} fusion(f32[14,256,256]{2,0,1:T(8,128)} %copy.47, s32[14]{0:T(128)S(1)} %copy-done.7), kind=kOutput, calls=%fused_computation.77 | convolution fusion | flops 352321984 | bytes 12058680 | tf_op jit(solution)/shard_map/ap,pjc->ajc/dot_general | solution.py:132
  325.3 8.1 %copy.48 = f32[32,256,256]{2,1,0:T(8,128)} copy(f32[32,256,256]{2,0,1:T(8,128)S(1)} %fusion.55) | data formatting | bytes 16777216 | tf_op jit(solution)/shard_map/ap,pjc->ajc/dot_general | solution.py:132
  333.4 9.7 %all-to-all-start.1 = ((f32[32,256,256]{2,1,0:T(8,128)}), f32[32,256,256]{2,1,0:T(8,128)}, u32[]{:S(2)}, u32[]{:S(2)}) async-start(f32[32,256,256]{2,1,0:T(8,128)} %copy.48), calls=%async_computation.1 | async-start | bytes 16777216 | tf_op jit(solution)/shard_map/all_to_all | solution.py:135
  343.1 2.7 fusion.30
  349.7 9.5 %fusion = bf16[4096,512]{0,1:T(8,128)(2,1)} fusion(bf16[896,4096]{1,0:T(8,128)(2,1)} %bitcast.208, bf16[112,8,4,128]{3,2,1,0:T(4,128)(2,1)S(1)} %bitcast.206), kind=kOutput, calls=%fused_computation.2 | convolution fusion | flops 3760193536 | bytes 12451840 | tf_op jit(solution)/shard_map/tc,tq->cq/dot_general | solution.py:144
  359.1 6.5 %copy.59 = bf16[4096,512]{1,0:T(8,128)(2,1)} copy(bf16[4096,512]{0,1:T(8,128)(2,1)} %fusion) | data formatting | bytes 8388608
  368.5 1.3 fusion.28
  369.8 175.5 %all-to-all-done.1 = f32[32,256,256]{2,1,0:T(8,128)} async-done(((f32[32,256,256]{2,1,0:T(8,128)}), f32[32,256,256]{2,1,0:T(8,128)}, u32[]{:S(2)}, u32[]{:S(2)}) %all-to-all-start.1) | async-done | bytes 8388640 | tf_op jit(solution)/shard_map/all_to_all | solution.py:135
  545.3 3.9 reduce_sum.49
  (49 shorter events, 13.2 us)
Async XLA Ops:
  7.2 291.1 %copy-start = (bf16[14,64,128]{2,1,0:T(8,128)(2,1)S(1)}, bf16[14,64,128]{2,1,0:T(8,128)(2,1)}, u32[]{:S(2)}) copy-start(bf16[14,64,128]{2,1,0:T(8,128)(2,1)} %param.11) | copy-start | bytes 688132
  7.2 133.8 %all-gather.5.cloned.1.call-start = ((), (), s32[]{:S(2)}) async-start(), calls=%async_computation.4 | async-start | bytes 4325376 | tf_op jit(solution)/shard_map/all_gather | solution.py:97
  7.9 278.6 %all-gather.3.cloned.1.call-start = ((), (), s32[]{:S(2)}) async-start(), calls=%async_computation.3 | async-start | bytes 8257536 | tf_op jit(solution)/shard_map/all_gather | solution.py:88
  12.0 11.8 %copy-start.7 = (s32[14]{0:T(128)S(1)}, s32[14]{0:T(128)}, u32[]{:S(2)}) copy-start(s32[14]{0:T(128)} %param.15) | copy-start | bytes 172
  12.0 123.0 %all-to-all-start = ((bf16[32,256,256]{2,1,0:T(8,128)(2,1)}), bf16[32,256,256]{2,1,0:T(8,128)(2,1)}, u32[]{:S(2)}, u32[]{:S(2)}) async-start(bf16[32,256,256]{2,1,0:T(8,128)(2,1)} %broadcast_in_dim.41), calls=%async_computation | async-start | bytes 8388608 | tf_op jit(solution)/shard_map/all_to_all | solution.py:104
  141.0 160.1 %copy-start.3 = (bf16[14,256,256]{2,1,0:T(8,128)(2,1)}, bf16[14,256,256]{2,1,0:T(8,128)(2,1)S(1)}, u32[]{:S(2)}) copy-start(bf16[14,256,256]{2,1,0:T(8,128)(2,1)S(1)} %broadcast_select_fusion) | copy-start | bytes 5505028
  299.3 8.0 %copy-start.1 = (f32[14,1,4,64,64]{3,4,2,0,1:T(8,128)}, f32[14,1,4,64,64]{3,4,2,0,1:T(8,128)S(1)}, u32[]{:S(2)}) copy-start(f32[14,1,4,64,64]{3,4,2,0,1:T(8,128)S(1)} %get-tuple-element.25) | copy-start | bytes 2752516
  300.6 1.2 copy-start.8
  300.6 1.2 copy-start.11
  304.4 3.0 copy-start.10
  333.4 212.0 %all-to-all-start.1 = ((f32[32,256,256]{2,1,0:T(8,128)}), f32[32,256,256]{2,1,0:T(8,128)}, u32[]{:S(2)}, u32[]{:S(2)}) async-start(f32[32,256,256]{2,1,0:T(8,128)} %copy.48), calls=%async_computation.1 | async-start | bytes 16777216 | tf_op jit(solution)/shard_map/all_to_all | solution.py:135
  343.1 206.9 %reduce-scatter.4.cloned.1.call-start = ((), (), s32[]{:S(2)}) async-start(), calls=%async_computation.5 | async-start | bytes 4325376
  345.8 0.9 copy-start.5
  346.7 1.5 copy-start.4
  365.6 1.2 copy-start.6
  365.6 2.3 copy-start.9
  366.8 1.7 copy-start.2
Sparse Core Ops, SparseCore 0:
  10.8 122.8 all-gather.4
  135.4 151.0 all-gather.2
  365.8 177.5 reduce-scatter.3

commit v2 on v1

--- a/solution.py
+++ b/solution.py
@@ -92,9 +92,16 @@
     kv_heads = width_kv // HD
     group_size = width_q // width_kv
     prefix = prefix_keys.shape[1]
+    every_weight = lax.all_to_all(
+        jnp.broadcast_to(query_weight[None], (owners,) + query_weight.shape),
+        "dom",
+        split_axis=0,
+        concat_axis=0,
+        tiled=True,
+    ).reshape(owners * query_weight.shape[0], width_q)
     queries = jnp.dot(
         token_rows,
-        lax.all_gather(query_weight, "dom", axis=0, tiled=True),
+        every_weight,
         preferred_element_type=jnp.float32,
     ).astype(jnp.bfloat16)
     queries = queries.reshape(particles_here, length, width_q)
@@ -132,8 +139,10 @@
     outgoing = jnp.einsum(
         "ap,pjc->ajc", onehot, grad_pkv, precision=lax.Precision.HIGHEST
     )
-    incoming = lax.all_to_all(outgoing, "dom", split_axis=0, concat_axis=0, tiled=True)
-    summed = jnp.sum(incoming, axis=0)
+    incoming = lax.all_to_all(
+        outgoing.astype(jnp.bfloat16), "dom", split_axis=0, concat_axis=0, tiled=True
+    )
+    summed = jnp.sum(incoming.astype(jnp.float32), axis=0)
     grad_pre_keys = summed[None, :, :width_kv]
     grad_pre_values = summed[None, :, width_kv:]
 

time: 560 us -> 478 us (0.85)
  waiting for transfers between devices: 434 us -> 345 us
  starting transfers between devices: 21.6 us -> 33.3 us
    all_gather x1, waiting for transfers between devices: 146 us -> 26.1 us  [local(): features = lax.all_gather(hidden_in, 'tp', axis=2, tiled=True)]
    unnamed x4 -> x3, waiting for transfers between devices: 1.39 us -> 57.6 us
    all_to_all x1, waiting for transfers between devices: 111 us -> 97.8 us  [local(): lax.all_to_all(jnp.broadcast_to(own_kv, (owners,) + own_kv.shape[1:]), 'd...]
    all_to_all x1 -> x2, waiting for transfers between devices: 176 us -> 164 us  [the longest x1 91 us: local(): lax.all_to_all(jnp.broadcast_to(query_weight[None], (owners,) + query_wei...]
    all_to_all x1 -> x2, starting transfers between devices: 9.69 us -> 21.4 us  [the longest x1 11.2 us: local(): lax.all_to_all(outgoing.astype(jnp.bfloat16), 'dom', split_axis=0, concat...]
    dot_general x1 -> x0, local copies, waits for them, and re-layouts: 8.08 us -> none  [local(): jnp.einsum('ap,pjc->ajc', onehot, grad_pkv, precision=lax.Precision.HIGHEST)]
  transfers between devices with their start and end apart: 5 -> 5, of which waited for: 3 -> 5; matrix products, arithmetic and copies ran while one was open for 7% -> 7% of each run, Pallas kernels for 0% -> 0%
where the time goes in v2:
time: 478 us
  waiting for transfers between devices  345 us (72%)
  matrix products  37.9 us (8%)
  starting transfers between devices  33.3 us (7%)
  local copies, waits for them, and re-layouts  33.2 us (7%)
  between operations  14.3 us (3%)
  other arithmetic  13.9 us (3%)
    all_to_all x1, waiting for transfers between devices, local(): lax.all_to_all(jnp.broadcast_to(own_kv, (owners,) + own_kv.shape[1:]), 'd...  97.8 us
    all_to_all x1, waiting for transfers between devices, local(): lax.all_to_all(jnp.broadcast_to(query_weight[None], (owners,) + query_wei...  91 us
    all_to_all x1, waiting for transfers between devices, local(): lax.all_to_all(outgoing.astype(jnp.bfloat16), 'dom', split_axis=0, concat...  72.5 us
    unnamed x3, waiting for transfers between devices  57.6 us
    all_gather x1, waiting for transfers between devices, local(): features = lax.all_gather(hidden_in, 'tp', axis=2, tiled=True)  26.1 us
    all_to_all x1, starting transfers between devices, local(): lax.all_to_all(jnp.broadcast_to(own_kv, (owners,) + own_kv.shape[1:]), 'd...  11.7 us
    all_to_all x1, starting transfers between devices, local(): lax.all_to_all(outgoing.astype(jnp.bfloat16), 'dom', split_axis=0, concat...  11.2 us
    unnamed x27, local copies, waits for them, and re-layouts  10.9 us
  transfers between devices with their start and end apart: 5, of which 5 were waited for; matrix products, arithmetic and copies ran while one was open for 7% of the time, Pallas kernels for 0%

profile of v2, /device:TPU:2, one launch (start us, length us, event | category | flops | bytes accessed | tf_op | source)
XLA Modules:
  0.0 477.5 jit_solution(17195037297653331596)
XLA Ops:
  8.1 2.6 broadcast_in_dim.47
  10.7 11.7 %all-to-all-start = ((bf16[32,256,256]{2,1,0:T(8,128)(2,1)}), bf16[32,256,256]{2,1,0:T(8,128)(2,1)}, u32[]{:S(2)}, u32[]{:S(2)}) async-start(bf16[32,256,256]{2,1,0:T(8,128)(2,1)} %broadcast_in_dim.47), calls=%async_computation | async-start | bytes 8388608 | tf_op jit(solution)/shard_map/all_to_all | solution.py:111
  23.2 97.8 %all-to-all-done = bf16[32,256,256]{2,1,0:T(8,128)(2,1)} async-done(((bf16[32,256,256]{2,1,0:T(8,128)(2,1)}), bf16[32,256,256]{2,1,0:T(8,128)(2,1)}, u32[]{:S(2)}, u32[]{:S(2)}) %all-to-all-start) | async-done | bytes 4194336 | tf_op jit(solution)/shard_map/all_to_all | solution.py:111
  120.9 2.4 broadcast_in_dim.50
  123.4 10.2 %all-to-all-start.1 = ((bf16[32,128,512]{2,1,0:T(8,128)(2,1)}), bf16[32,128,512]{2,1,0:T(8,128)(2,1)}, u32[]{:S(2)}, u32[]{:S(2)}) async-start(bf16[32,128,512]{2,1,0:T(8,128)(2,1)} %broadcast_in_dim.50), calls=%async_computation.1 | async-start | bytes 8388608 | tf_op jit(solution)/shard_map/all_to_all | solution.py:95
  133.7 4.1 gather_fusion
  139.6 91.0 %all-to-all-done.1 = bf16[32,128,512]{2,1,0:T(8,128)(2,1)} async-done(((bf16[32,128,512]{2,1,0:T(8,128)(2,1)}), bf16[32,128,512]{2,1,0:T(8,128)(2,1)}, u32[]{:S(2)}, u32[]{:S(2)}) %all-to-all-start.1) | async-done | bytes 4194336 | tf_op jit(solution)/shard_map/all_to_all | solution.py:95
  230.6 26.1 %all-gather.2.cloned.1.call-done = bf16[14,64,4096]{2,1,0:T(8,128)(2,1)} async-done(((bf16[14,64,512]{2,1,0:T(8,128)(2,1)}), bf16[14,64,4096]{2,1,0:T(8,128)(2,1)}) %all-gather.2.cloned.1.call-update) | async-done | bytes 7340048 | tf_op jit(solution)/shard_map/all_gather | solution.py:88
  256.7 9.2 %convolution_convert_fusion.2 = bf16[896,512]{1,0:T(8,128)(2,1)} fusion(bf16[896,4096]{1,0:T(8,128)(2,1)} %bitcast.208, bf16[4096,512]{1,0:T(8,128)(2,1)} %bitcast.5), kind=kOutput, calls=%fused_computation.37 | convolution fusion | flops 3758555136 | bytes 12451840 | tf_op jit(solution)/shard_map/dot_general | solution.py:102
  265.9 1.9 reshape.166
  272.0 2.6 fusion.1
  274.6 2.9 fusion.20
  277.6 2.3 fusion.13
  282.2 2.3 pad_maximum_fusion
  284.5 5.4 %copy.47 = f32[14,256,256]{2,0,1:T(8,128)} copy(f32[14,256,256]{1,2,0:T(8,128)} %pad_maximum_fusion) | data formatting | bytes 7340032 | tf_op jit(solution)/shard_map/concatenate | solution.py:130
  289.9 5.8 %convolution_convert_fusion.1 = bf16[32,256,256]{2,0,1:T(8,128)(2,1)S(1)} fusion(f32[14,256,256]{2,0,1:T(8,128)} %copy.47, s32[14]{0:T(128)S(1)} %copy-done.8), kind=kOutput, calls=%fused_computation.15 | convolution fusion | flops 354419136 | bytes 7864376 | tf_op jit(solution)/shard_map/ap,pjc->ajc/dot_general | solution.py:139
  295.7 4.5 copy.48
  300.1 11.2 %all-to-all-start.2 = ((bf16[32,256,256]{2,1,0:T(8,128)(2,1)}), bf16[32,256,256]{2,1,0:T(8,128)(2,1)}, u32[]{:S(2)}, u32[]{:S(2)}) async-start(bf16[32,256,256]{2,1,0:T(8,128)(2,1)} %copy.48), calls=%async_computation.2 | async-start | bytes 8388608 | tf_op jit(solution)/shard_map/all_to_all | solution.py:142
  311.4 2.7 fusion.30
  317.9 9.3 %fusion = bf16[4096,512]{0,1:T(8,128)(2,1)} fusion(bf16[896,4096]{1,0:T(8,128)(2,1)} %bitcast.209, bf16[112,8,4,128]{3,2,1,0:T(4,128)(2,1)S(1)} %bitcast.207), kind=kOutput, calls=%fused_computation.3 | convolution fusion | flops 3760193536 | bytes 12451840 | tf_op jit(solution)/shard_map/tc,tq->cq/dot_general | solution.py:153
  327.2 6.5 %copy.59 = bf16[4096,512]{1,0:T(8,128)(2,1)} copy(bf16[4096,512]{0,1:T(8,128)(2,1)} %fusion) | data formatting | bytes 8388608
  337.8 72.5 %all-to-all-done.2 = bf16[32,256,256]{2,1,0:T(8,128)(2,1)} async-done(((bf16[32,256,256]{2,1,0:T(8,128)(2,1)}), bf16[32,256,256]{2,1,0:T(8,128)(2,1)}, u32[]{:S(2)}, u32[]{:S(2)}) %all-to-all-start.2) | async-done | bytes 4194336 | tf_op jit(solution)/shard_map/all_to_all | solution.py:142
  410.3 2.8 convert_reduce_fusion
  413.8 56.9 %reduce-scatter.4.cloned.1.call-done = bf16[128,512]{1,0:T(8,128)(2,1)} async-done(((bf16[4096,512]{1,0:T(8,128)(2,1)}), bf16[128,512]{1,0:T(8,128)(2,1)}) %reduce-scatter.4.cloned.1.call-update) | async-done | bytes 131088
  (51 shorter events, 18.6 us)
Async XLA Ops:
  7.2 261.3 %copy-start = (bf16[14,64,128]{2,1,0:T(8,128)(2,1)S(1)}, bf16[14,64,128]{2,1,0:T(8,128)(2,1)}, u32[]{:S(2)}) copy-start(bf16[14,64,128]{2,1,0:T(8,128)(2,1)} %param.11) | copy-start | bytes 688132
  10.7 110.3 %copy-start.7 = (bf16[128,512]{1,0:T(8,128)(2,1)S(1)}, bf16[128,512]{1,0:T(8,128)(2,1)}, u32[]{:S(2)}) copy-start(bf16[128,512]{1,0:T(8,128)(2,1)} %param.10) | copy-start | bytes 393220
  10.7 110.2 %all-to-all-start = ((bf16[32,256,256]{2,1,0:T(8,128)(2,1)}), bf16[32,256,256]{2,1,0:T(8,128)(2,1)}, u32[]{:S(2)}, u32[]{:S(2)}) async-start(bf16[32,256,256]{2,1,0:T(8,128)(2,1)} %broadcast_in_dim.47), calls=%async_computation | async-start | bytes 8388608 | tf_op jit(solution)/shard_map/all_to_all | solution.py:111
  22.4 234.3 %all-gather.2.cloned.1.call-start = ((), (), s32[]{:S(2)}) async-start(), calls=%async_computation.4 | async-start | bytes 8257536 | tf_op jit(solution)/shard_map/all_gather | solution.py:88
  123.4 10.3 %copy-start.8 = (s32[14]{0:T(128)S(1)}, s32[14]{0:T(128)}, u32[]{:S(2)}) copy-start(s32[14]{0:T(128)} %param.15) | copy-start | bytes 172
  123.4 107.2 %all-to-all-start.1 = ((bf16[32,128,512]{2,1,0:T(8,128)(2,1)}), bf16[32,128,512]{2,1,0:T(8,128)(2,1)}, u32[]{:S(2)}, u32[]{:S(2)}) async-start(bf16[32,128,512]{2,1,0:T(8,128)(2,1)} %broadcast_in_dim.50), calls=%async_computation.1 | async-start | bytes 8388608 | tf_op jit(solution)/shard_map/all_to_all | solution.py:95
  139.6 131.7 %copy-start.3 = (bf16[14,256,256]{2,1,0:T(8,128)(2,1)}, bf16[14,256,256]{2,1,0:T(8,128)(2,1)S(1)}, u32[]{:S(2)}) copy-start(bf16[14,256,256]{2,1,0:T(8,128)(2,1)S(1)} %broadcast_select_fusion) | copy-start | bytes 5505028
  269.5 8.1 %copy-start.1 = (f32[14,1,4,64,64]{3,4,2,0,1:T(8,128)}, f32[14,1,4,64,64]{3,4,2,0,1:T(8,128)S(1)}, u32[]{:S(2)}) copy-start(f32[14,1,4,64,64]{3,4,2,0,1:T(8,128)S(1)} %get-tuple-element.25) | copy-start | bytes 2752516
  270.8 1.2 copy-start.9
  270.8 1.2 copy-start.12
  274.6 3.0 copy-start.11
  300.1 110.2 %all-to-all-start.2 = ((bf16[32,256,256]{2,1,0:T(8,128)(2,1)}), bf16[32,256,256]{2,1,0:T(8,128)(2,1)}, u32[]{:S(2)}, u32[]{:S(2)}) async-start(bf16[32,256,256]{2,1,0:T(8,128)(2,1)} %copy.48), calls=%async_computation.2 | async-start | bytes 8388608 | tf_op jit(solution)/shard_map/all_to_all | solution.py:142
  311.3 159.3 %reduce-scatter.4.cloned.1.call-start = ((), (), s32[]{:S(2)}) async-start(), calls=%async_computation.5 | async-start | bytes 4325376
  314.1 0.9 copy-start.5
  315.0 1.5 copy-start.4
  333.6 1.2 copy-start.6
  333.6 2.3 copy-start.10
  334.8 1.7 copy-start.2
Sparse Core Ops, SparseCore 0:
  25.0 231.6 all-gather.1
  333.8 136.8 reduce-scatter.3

commit v3 on v1

--- a/solution.py
+++ b/solution.py
@@ -69,6 +69,36 @@
         grad_pk,
         grad_pv,
     )
+
+
+TP_RING = (0, 2, 4, 6, 7, 5, 3, 1)
+
+
+def gather_ring(block):
+    size = len(TP_RING)
+    ahead = size // 2
+    behind = size - 1 - ahead
+    forward = [(TP_RING[i], TP_RING[(i + 1) % size]) for i in range(size)]
+    backward = [(TP_RING[(i + 1) % size], TP_RING[i]) for i in range(size)]
+    pieces = [block]
+    moving = block
+    for _ in range(ahead):
+        moving = lax.ppermute(moving, "tp", forward)
+        pieces.append(moving)
+    moving = block
+    for _ in range(behind):
+        moving = lax.ppermute(moving, "tp", backward)
+        pieces.append(moving)
+    offsets = [0] + [-(s + 1) for s in range(ahead)] + [s + 1 for s in range(behind)]
+    ring = jnp.array(TP_RING, jnp.int32)
+    place = jnp.zeros((size,), jnp.int32).at[ring].set(jnp.arange(size, dtype=jnp.int32))
+    here = place[lax.axis_index("tp")]
+    order = ring[(here + jnp.array(offsets, jnp.int32)) % size]
+    slot_of_offset = jnp.zeros((size,), jnp.int32).at[jnp.array(offsets, jnp.int32) % size].set(
+        jnp.arange(size, dtype=jnp.int32)
+    )
+    inverse = slot_of_offset[(place - here) % size]
+    return jnp.stack(pieces), order, inverse
 
 
 def local(
@@ -85,16 +115,21 @@
     particles_here = hidden_in.shape[0]
     length = hidden_in.shape[1]
     owners = lax.axis_size("dom")
-    features = lax.all_gather(hidden_in, "tp", axis=2, tiled=True)
-    token_rows = features.reshape(particles_here * length, features.shape[2])
+    features, order, inverse = gather_ring(hidden_in)
+    blocks = features.shape[0]
+    width_in = hidden_in.shape[2]
+    token_blocks = features.reshape(blocks, particles_here * length, width_in)
     width_q = query_weight.shape[1]
     width_kv = segment_keys.shape[2]
     kv_heads = width_kv // HD
     group_size = width_q // width_kv
     prefix = prefix_keys.shape[1]
-    queries = jnp.dot(
-        token_rows,
-        lax.all_gather(query_weight, "dom", axis=0, tiled=True),
+    every_weight = lax.all_gather(query_weight, "dom", axis=0, tiled=True)
+    weight_blocks = jnp.take(every_weight.reshape(blocks, width_in, width_q), order, axis=0)
+    queries = jnp.einsum(
+        "ktd,kdq->tq",
+        token_blocks,
+        weight_blocks,
         preferred_element_type=jnp.float32,
     ).astype(jnp.bfloat16)
     queries = queries.reshape(particles_here, length, width_q)
@@ -132,18 +167,22 @@
     outgoing = jnp.einsum(
         "ap,pjc->ajc", onehot, grad_pkv, precision=lax.Precision.HIGHEST
     )
-    incoming = lax.all_to_all(outgoing, "dom", split_axis=0, concat_axis=0, tiled=True)
-    summed = jnp.sum(incoming, axis=0)
+    incoming = lax.all_to_all(
+        outgoing.astype(jnp.bfloat16), "dom", split_axis=0, concat_axis=0, tiled=True
+    )
+    summed = jnp.sum(incoming.astype(jnp.float32), axis=0)
     grad_pre_keys = summed[None, :, :width_kv]
     grad_pre_values = summed[None, :, width_kv:]
 
     grad_seg_keys = grad_sk.reshape(particles_here, length, width_kv)
     grad_seg_values = grad_sv.reshape(particles_here, length, width_kv)
     grad_rows = grad_q.reshape(particles_here * length, width_q)
+    partial = jnp.einsum(
+        "ktd,tq->kdq", token_blocks, grad_rows, preferred_element_type=jnp.float32
+    ).astype(jnp.bfloat16)
+    partial = jnp.take(partial, inverse, axis=0).reshape(blocks * width_in, width_q)
     grad_weight = lax.psum_scatter(
-        jnp.einsum("tc,tq->cq", token_rows, grad_rows, preferred_element_type=jnp.float32).astype(
-            jnp.bfloat16
-        ),
+        partial,
         "dom",
         scatter_dimension=0,
         tiled=True,

time: 560 us -> 394 us (0.70)
  waiting for transfers between devices: 434 us -> 199 us
  starting transfers between devices: 21.6 us -> 82 us
  local copies, waits for them, and re-layouts: 34.3 us -> 40.5 us
    all_gather x2 -> x1, waiting for transfers between devices: 146 us -> 0.01 us  [local(): every_weight = lax.all_gather(query_weight, 'dom', axis=0, tiled=True)]
    all_to_all x1, waiting for transfers between devices: 111 us -> 0.01 us  [local(): lax.all_to_all(jnp.broadcast_to(own_kv, (owners,) + own_kv.shape[1:]), 'd...]
    all_to_all x1, waiting for transfers between devices: 176 us -> 68.9 us  [local(): lax.all_to_all(outgoing.astype(jnp.bfloat16), 'dom', split_axis=0, concat...]
    ppermute x0 -> x7, waiting for transfers between devices: none -> 73.8 us  [the longest x4 73.8 us: gather_ring(): moving = lax.ppermute(moving, 'tp', forward)]
    ppermute x0 -> x7, starting transfers between devices: none -> 59.8 us  [the longest x3 56.5 us: gather_ring(): moving = lax.ppermute(moving, 'tp', backward)]
    reduce_scatter x0 -> x1, waiting for transfers between devices: none -> 55.1 us  [local(): lax.psum_scatter(partial, 'dom', scatter_dimension=0, tiled=True)]
    gather x0 -> x4, local copies, waits for them, and re-layouts: none -> 11.2 us  [the longest x1 5 us: local(): jnp.take(every_weight.reshape(blocks, width_in, width_q), order, axis=0)]
    dot_general x1 -> x0, local copies, waits for them, and re-layouts: 8.08 us -> none  [local(): jnp.einsum('ap,pjc->ajc', onehot, grad_pkv, precision=lax.Precision.HIGHEST)]
  transfers between devices with their start and end apart: 5 -> 11, of which waited for: 3 -> 6; matrix products, arithmetic and copies ran while one was open for 7% -> 16% of each run, Pallas kernels for 0% -> 0%
where the time goes in v3:
time: 394 us; the launch traced here: 393 us
  waiting for transfers between devices  199 us (51%)
  starting transfers between devices  82 us (21%)
  local copies, waits for them, and re-layouts  40.5 us (10%)
  matrix products  39.6 us (10%)
  other arithmetic  18 us (5%)
  between operations  14.4 us (4%)
    ppermute x4, waiting for transfers between devices, gather_ring(): moving = lax.ppermute(moving, 'tp', forward)  73.8 us
    all_to_all x1, waiting for transfers between devices, local(): lax.all_to_all(outgoing.astype(jnp.bfloat16), 'dom', split_axis=0, concat...  68.9 us
    ppermute x3, starting transfers between devices, gather_ring(): moving = lax.ppermute(moving, 'tp', backward)  56.5 us
    reduce_scatter x1, waiting for transfers between devices, local(): lax.psum_scatter(partial, 'dom', scatter_dimension=0, tiled=True)  55.1 us
    all_to_all x1, starting transfers between devices, local(): lax.all_to_all(jnp.broadcast_to(own_kv, (owners,) + own_kv.shape[1:]), 'd...  11.8 us
    unnamed x37, local copies, waits for them, and re-layouts  10.4 us
    all_to_all x1, starting transfers between devices, local(): lax.all_to_all(outgoing.astype(jnp.bfloat16), 'dom', split_axis=0, concat...  10.4 us
    dot_general x1, matrix products, local(): jnp.einsum('ktd,tq->kdq', token_blocks, grad_rows, preferred_element_type...  9.48 us
  transfers between devices with their start and end apart: 11, of which 6 were waited for; matrix products, arithmetic and copies ran while one was open for 16% of the time, Pallas kernels for 0%

profile of v3, /device:TPU:2, one launch (start us, length us, event | category | flops | bytes accessed | tf_op | source)
XLA Modules:
  0.0 393.0 jit_solution(12212152473228883404)
XLA Ops:
  11.4 11.8 %all-to-all-start = ((bf16[32,256,256]{2,1,0:T(8,128)(2,1)}), bf16[32,256,256]{2,1,0:T(8,128)(2,1)}, u32[]{:S(2)}, u32[]{:S(2)}) async-start(bf16[32,256,256]{2,1,0:T(8,128)(2,1)} %broadcast_in_dim.62), calls=%async_computation | async-start | bytes 8388608 | tf_op jit(solution)/shard_map/all_to_all | solution.py:139
  24.7 21.0 %collective-permute-done = bf16[14,64,512]{2,1,0:T(8,128)(2,1)S(1)} collective-permute-done((bf16[14,64,512]{2,1,0:T(8,128)(2,1)S(1)}, bf16[14,64,512]{2,1,0:T(8,128)(2,1)S(1)}, u32[]{:S(2)}, u32[]{:S(2)}) %collective-permute-start) | collective-permute-done | bytes 917536 | tf_op jit(solution)/shard_map/ppermute | solution.py:86
  47.2 18.1 %collective-permute-start.4 = (bf16[14,64,512]{2,1,0:T(8,128)(2,1)S(1)}, bf16[14,64,512]{2,1,0:T(8,128)(2,1)S(1)}, u32[]{:S(2)}, u32[]{:S(2)}) collective-permute-start(bf16[14,64,512]{2,1,0:T(8,128)(2,1)S(1)} %copy-done.8), channel_id=1, source_target_pairs={{2,0},{4,2},{6,4},{7,6},{5,7},{3,5},{1,3},{0,1},{10,8},{12,10},{14... | collective-permute-start | bytes 2752520 | tf_op jit(solution)/shard_map/ppermute | solution.py:90
  67.2 18.4 %collective-permute-done.1 = bf16[14,64,512]{2,1,0:T(8,128)(2,1)} collective-permute-done((bf16[14,64,512]{2,1,0:T(8,128)(2,1)S(1)}, bf16[14,64,512]{2,1,0:T(8,128)(2,1)}, u32[]{:S(2)}, u32[]{:S(2)}) %collective-permute-start.1) | collective-permute-done | bytes 917536 | tf_op jit(solution)/shard_map/ppermute | solution.py:86
  86.3 35.5 %collective-permute-start.5 = (bf16[14,64,512]{2,1,0:T(8,128)(2,1)S(1)}, bf16[14,64,512]{2,1,0:T(8,128)(2,1)S(1)}, u32[]{:S(2)}, u32[]{:S(2)}) collective-permute-start(bf16[14,64,512]{2,1,0:T(8,128)(2,1)S(1)} %collective-permute-done.4), channel_id=1, source_target_pairs={{2,0},{4,2},{6,4},{7,6},{5,7},{3,5},{1,3},{0,1},{10,8},{12,10},{14... | collective-permute-start | bytes 2752520 | tf_op jit(solution)/shard_map/ppermute | solution.py:90
  121.8 20.2 %collective-permute-done.2 = bf16[14,64,512]{2,1,0:T(8,128)(2,1)} collective-permute-done((bf16[14,64,512]{2,1,0:T(8,128)(2,1)}, bf16[14,64,512]{2,1,0:T(8,128)(2,1)}, u32[]{:S(2)}, u32[]{:S(2)}) %collective-permute-start.2) | collective-permute-done | bytes 917536 | tf_op jit(solution)/shard_map/ppermute | solution.py:86
  143.2 2.9 collective-permute-start.6
  151.5 14.2 %collective-permute-done.3 = bf16[14,64,512]{2,1,0:T(8,128)(2,1)S(1)} collective-permute-done((bf16[14,64,512]{2,1,0:T(8,128)(2,1)}, bf16[14,64,512]{2,1,0:T(8,128)(2,1)S(1)}, u32[]{:S(2)}, u32[]{:S(2)}) %collective-permute-start.3) | collective-permute-done | bytes 917536 | tf_op jit(solution)/shard_map/ppermute | solution.py:86
  169.8 5.0 %gather_fusion.3 = bf16[8,512,512]{2,1,0:T(8,128)(2,1)} fusion(bf16[8,512,512]{2,1,0:T(8,128)(2,1)} %bitcast.228, s32[1024]{0:T(1024)S(1)} %pad_clamp_fusion.1), kind=kCustom, calls=%fused_computation.clone | custom fusion | bytes 8388640 | tf_op jit(solution)/shard_map/jit(_take)/gather | solution.py:128
  174.8 8.3 %bitcast_convert_fusion = bf16[896,512]{1,0:T(8,128)(2,1)S(1)} fusion(bf16[8,896,512]{2,1,0:T(8,128)(2,1)} %bitcast_dynamic-update-slice_fusion, bf16[8,512,512]{2,1,0:T(8,128)(2,1)} %gather_fusion.3, pred[8]{0:T(512)(128)(4,1)S(1)} %compare_and_fusion.1), kind=kOutput, calls=%fused_computation.38 | convolution fusion | flops 3760652288 | bytes 12451848 | tf_op jit(solution)/shard_map/ktd,kdq->tq/dot_general | solution.py:129
  183.3 2.9 gather_fusion
  190.2 2.7 fusion.3
  192.8 2.9 fusion.25
  202.7 5.4 %copy.51 = f32[14,256,256]{2,0,1:T(8,128)} copy(f32[14,256,256]{1,2,0:T(8,128)} %pad_maximum_fusion) | data formatting | bytes 7340032 | tf_op jit(solution)/shard_map/concatenate | solution.py:158
  208.1 5.6 %convolution_convert_fusion = bf16[32,256,256]{2,0,1:T(8,128)(2,1)S(1)} fusion(f32[14,256,256]{2,0,1:T(8,128)} %copy.51, s32[14]{0:T(128)S(1)} %copy-done.9), kind=kOutput, calls=%fused_computation.21 | convolution fusion | flops 354419136 | bytes 7864376 | tf_op jit(solution)/shard_map/ap,pjc->ajc/dot_general | solution.py:167
  213.7 4.5 %copy.52 = bf16[32,256,256]{2,1,0:T(8,128)(2,1)} copy(bf16[32,256,256]{2,0,1:T(8,128)(2,1)S(1)} %convolution_convert_fusion) | data formatting | bytes 8388608 | tf_op jit(solution)/shard_map/convert_element_type | solution.py:171
  218.2 10.4 %all-to-all-start.1 = ((bf16[32,256,256]{2,1,0:T(8,128)(2,1)}), bf16[32,256,256]{2,1,0:T(8,128)(2,1)}, u32[]{:S(2)}, u32[]{:S(2)}) async-start(bf16[32,256,256]{2,1,0:T(8,128)(2,1)} %copy.52), calls=%async_computation.2 | async-start | bytes 8388608 | tf_op jit(solution)/shard_map/all_to_all | solution.py:170
  228.6 2.8 fusion.35
  234.6 9.5 %convolution_convert_fusion.1 = bf16[8,512,512]{2,1,0:T(8,128)(2,1)} fusion(bf16[8,896,512]{2,1,0:T(8,128)(2,1)} %bitcast_dynamic-update-slice_fusion, bf16[896,512,1]{1,0,2:T(8,128)(2,1)S(1)} %reshape.252), kind=kOutput, calls=%fused_computation.22 | convolution fusion | flops 3760193536 | bytes 12451840 | tf_op jit(solution)/shard_map/ktd,tq->kdq/dot_general | solution.py:180
  244.1 4.9 %gather_fusion.4 = bf16[8,512,512]{2,1,0:T(8,128)(2,1)} fusion(bf16[8,512,512]{2,1,0:T(8,128)(2,1)} %convolution_convert_fusion.1, s32[1024]{0:T(1024)S(1)} %pad_clamp_fusion), kind=kCustom, calls=%fused_computation.1.clone | custom fusion | bytes 8388640 | tf_op jit(solution)/shard_map/jit(_take)/gather | solution.py:183
  249.1 4.6 %broadcast_select_fusion = bf16[8,512,512]{2,1,0:T(8,128)(2,1)} fusion(bf16[8,512,512]{2,1,0:T(8,128)(2,1)} %gather_fusion.4, pred[8]{0:T(512)(128)(4,1)S(1)} %compare_and_fusion), kind=kLoop, calls=%fused_computation.8 | loop fusion | flops 2097152 | bytes 8388616 | tf_op jit(solution)/shard_map/jit(_take)/select_n | solution.py:183
  258.6 68.9 %all-to-all-done.1 = bf16[32,256,256]{2,1,0:T(8,128)(2,1)} async-done(((bf16[32,256,256]{2,1,0:T(8,128)(2,1)}), bf16[32,256,256]{2,1,0:T(8,128)(2,1)}, u32[]{:S(2)}, u32[]{:S(2)}) %all-to-all-start.1) | async-done | bytes 4194336 | tf_op jit(solution)/shard_map/all_to_all | solution.py:170
  327.5 2.8 convert_reduce_fusion
  331.1 55.1 %reduce-scatter.2.cloned.1.call-done = bf16[128,512]{1,0:T(8,128)(2,1)} async-done(((bf16[4096,512]{1,0:T(8,128)(2,1)}), bf16[128,512]{1,0:T(8,128)(2,1)}) %reduce-scatter.2.cloned.1.call-update) | async-done | bytes 131088 | tf_op jit(solution)/shard_map/reduce_scatter | solution.py:184
  (89 shorter events, 40.2 us)
Async XLA Ops:
  7.2 180.0 %copy-start = (bf16[14,64,128]{2,1,0:T(8,128)(2,1)S(1)}, bf16[14,64,128]{2,1,0:T(8,128)(2,1)}, u32[]{:S(2)}) copy-start(bf16[14,64,128]{2,1,0:T(8,128)(2,1)} %param.16) | copy-start | bytes 688132
  7.2 162.6 %all-gather.2.cloned.1.call-start = ((), (), s32[]{:S(2)}) async-start(), calls=%async_computation.3 | async-start | bytes 4325376 | tf_op jit(solution)/shard_map/all_gather | solution.py:127
  11.3 11.8 %copy-start.8 = (bf16[14,64,512]{2,1,0:T(8,128)(2,1)S(1)}, bf16[14,64,512]{2,1,0:T(8,128)(2,1)}, u32[]{:S(2)}) copy-start(bf16[14,64,512]{2,1,0:T(8,128)(2,1)} %param.14) | copy-start | bytes 2752516
  11.3 53.9 %copy-start.10 = (s32[8]{0:T(128)S(1)}, s32[8]{0:T(128)}, u32[]{:S(2)}) copy-start(s32[8]{0:T(128)} %constant.88) | copy-start | bytes 100
  11.3 54.5 %copy-start.11 = (s32[8]{0:T(128)S(1)}, s32[8]{0:T(128)}, u32[]{:S(2)}) copy-start(s32[8]{0:T(128)} %constant.75.clone) | copy-start | bytes 100
  11.3 55.2 %copy-start.2 = (s32[8]{0:T(128)S(1)}, s32[8]{0:T(128)}, u32[]{:S(2)}) copy-start(s32[8]{0:T(128)} %constant.74.clone) | copy-start | bytes 100
  11.3 74.3 %copy-start.1 = (s32[8]{0:T(128)S(1)}, s32[8]{0:T(128)}, u32[]{:S(2)}) copy-start(s32[8]{0:T(128)} %constant.104) | copy-start | bytes 100
  11.3 75.0 %copy-start.9 = (s32[14]{0:T(128)S(1)}, s32[14]{0:T(128)}, u32[]{:S(2)}) copy-start(s32[14]{0:T(128)} %param.20) | copy-start | bytes 172
  11.4 172.0 %all-to-all-start = ((bf16[32,256,256]{2,1,0:T(8,128)(2,1)}), bf16[32,256,256]{2,1,0:T(8,128)(2,1)}, u32[]{:S(2)}, u32[]{:S(2)}) async-start(bf16[32,256,256]{2,1,0:T(8,128)(2,1)} %broadcast_in_dim.62), calls=%async_computation | async-start | bytes 8388608 | tf_op jit(solution)/shard_map/all_to_all | solution.py:139
  23.1 22.5 %collective-permute-start = (bf16[14,64,512]{2,1,0:T(8,128)(2,1)S(1)}, bf16[14,64,512]{2,1,0:T(8,128)(2,1)S(1)}, u32[]{:S(2)}, u32[]{:S(2)}) collective-permute-start(bf16[14,64,512]{2,1,0:T(8,128)(2,1)S(1)} %copy-done.8), channel_id=1, source_target_pairs={{0,2},{2,4},{4,6},{6,7},{7,5},{5,3},{3,1},{1,0},{8,10},{10,12},{12... | collective-permute-start | bytes 2752520 | tf_op jit(solution)/shard_map/ppermute | solution.py:86
  45.7 40.0 %collective-permute-start.1 = (bf16[14,64,512]{2,1,0:T(8,128)(2,1)S(1)}, bf16[14,64,512]{2,1,0:T(8,128)(2,1)}, u32[]{:S(2)}, u32[]{:S(2)}) collective-permute-start(bf16[14,64,512]{2,1,0:T(8,128)(2,1)S(1)} %collective-permute-done), channel_id=1, source_target_pairs={{0,2},{2,4},{4,6},{6,7},{7,5},{5,3},{3,1},{1,0},{8,10},{10,12},{12... | collective-permute-start | bytes 2752520 | tf_op jit(solution)/shard_map/ppermute | solution.py:86
  47.2 39.2 %collective-permute-start.4 = (bf16[14,64,512]{2,1,0:T(8,128)(2,1)S(1)}, bf16[14,64,512]{2,1,0:T(8,128)(2,1)S(1)}, u32[]{:S(2)}, u32[]{:S(2)}) collective-permute-start(bf16[14,64,512]{2,1,0:T(8,128)(2,1)S(1)} %copy-done.8), channel_id=1, source_target_pairs={{2,0},{4,2},{6,4},{7,6},{5,7},{3,5},{1,3},{0,1},{10,8},{12,10},{14... | collective-permute-start | bytes 2752520 | tf_op jit(solution)/shard_map/ppermute | solution.py:90
  85.6 56.4 %collective-permute-start.2 = (bf16[14,64,512]{2,1,0:T(8,128)(2,1)}, bf16[14,64,512]{2,1,0:T(8,128)(2,1)}, u32[]{:S(2)}, u32[]{:S(2)}) collective-permute-start(bf16[14,64,512]{2,1,0:T(8,128)(2,1)} %collective-permute-done.1), channel_id=1, source_target_pairs={{0,2},{2,4},{4,6},{6,7},{7,5},{5,3},{3,1},{1,0},{8,10},{10,12},{12... | collective-permute-start | bytes 2752520 | tf_op jit(solution)/shard_map/ppermute | solution.py:86
  86.3 56.9 %collective-permute-start.5 = (bf16[14,64,512]{2,1,0:T(8,128)(2,1)S(1)}, bf16[14,64,512]{2,1,0:T(8,128)(2,1)S(1)}, u32[]{:S(2)}, u32[]{:S(2)}) collective-permute-start(bf16[14,64,512]{2,1,0:T(8,128)(2,1)S(1)} %collective-permute-done.4), channel_id=1, source_target_pairs={{2,0},{4,2},{6,4},{7,6},{5,7},{3,5},{1,3},{0,1},{10,8},{12,10},{14... | collective-permute-start | bytes 2752520 | tf_op jit(solution)/shard_map/ppermute | solution.py:90
  142.0 23.8 %collective-permute-start.3 = (bf16[14,64,512]{2,1,0:T(8,128)(2,1)}, bf16[14,64,512]{2,1,0:T(8,128)(2,1)S(1)}, u32[]{:S(2)}, u32[]{:S(2)}) collective-permute-start(bf16[14,64,512]{2,1,0:T(8,128)(2,1)} %collective-permute-done.2), channel_id=1, source_target_pairs={{0,2},{2,4},{4,6},{6,7},{7,5},{5,3},{3,1},{1,0},{8,10},{10,12},{12... | collective-permute-start | bytes 2752520 | tf_op jit(solution)/shard_map/ppermute | solution.py:86
  143.2 25.6 %collective-permute-start.6 = (bf16[14,64,512]{2,1,0:T(8,128)(2,1)S(1)}, bf16[14,64,512]{2,1,0:T(8,128)(2,1)S(1)}, u32[]{:S(2)}, u32[]{:S(2)}) collective-permute-start(bf16[14,64,512]{2,1,0:T(8,128)(2,1)S(1)} %collective-permute-done.5), channel_id=1, source_target_pairs={{2,0},{4,2},{6,4},{7,6},{5,7},{3,5},{1,3},{0,1},{10,8},{12,10},{14... | collective-permute-start | bytes 2752520 | tf_op jit(solution)/shard_map/ppermute | solution.py:90
  186.4 3.7 copy-start.5
  188.2 7.6 %copy-start.3 = (f32[14,1,4,64,64]{3,4,2,0,1:T(8,128)}, f32[14,1,4,64,64]{3,4,2,0,1:T(8,128)S(1)}, u32[]{:S(2)}) copy-start(f32[14,1,4,64,64]{3,4,2,0,1:T(8,128)S(1)} %get-tuple-element.11) | copy-start | bytes 2752516
  188.2 1.9 copy-start.12
  192.8 3.0 copy-start.13
  218.2 109.3 %all-to-all-start.1 = ((bf16[32,256,256]{2,1,0:T(8,128)(2,1)}), bf16[32,256,256]{2,1,0:T(8,128)(2,1)}, u32[]{:S(2)}, u32[]{:S(2)}) async-start(bf16[32,256,256]{2,1,0:T(8,128)(2,1)} %copy.52), calls=%async_computation.2 | async-start | bytes 8388608 | tf_op jit(solution)/shard_map/all_to_all | solution.py:170
  228.6 157.6 %reduce-scatter.2.cloned.1.call-start = ((), (), s32[]{:S(2)}) async-start(), calls=%async_computation.4 | async-start | bytes 4325376 | tf_op jit(solution)/shard_map/reduce_scatter | solution.py:184
  228.6 4.2 %copy-start.6 = (bf16[14,256,256]{2,1,0:T(8,128)(2,1)S(1)}, bf16[14,256,256]{2,1,0:T(8,128)(2,1)}, u32[]{:S(2)}) copy-start(bf16[14,256,256]{2,1,0:T(8,128)(2,1)} %copy-done.5) | copy-start | bytes 5505028
  253.7 2.4 copy-start.4
  (2 other events, 2.9 us)
Sparse Core Ops, SparseCore 0:
  10.8 122.2 all-gather.1
  253.8 132.3 reduce-scatter.1

commit v4 on v3

--- a/solution.py
+++ b/solution.py
@@ -4,6 +4,7 @@
 import jax.numpy as jnp
 from jax import lax
 from jax.sharding import PartitionSpec as P
+
 
 HD = 128
 
@@ -62,13 +63,7 @@
         scaled,
         preferred_element_type=jnp.float32,
     )
-    return (
-        grad_q.astype(jnp.bfloat16),
-        grad_sk.astype(jnp.bfloat16),
-        grad_sv.astype(jnp.bfloat16),
-        grad_pk,
-        grad_pv,
-    )
+    return (grad_q.astype(jnp.bfloat16), grad_sk, grad_sv, grad_pk, grad_pv)
 
 
 TP_RING = (0, 2, 4, 6, 7, 5, 3, 1)
@@ -94,11 +89,10 @@
     place = jnp.zeros((size,), jnp.int32).at[ring].set(jnp.arange(size, dtype=jnp.int32))
     here = place[lax.axis_index("tp")]
     order = ring[(here + jnp.array(offsets, jnp.int32)) % size]
-    slot_of_offset = jnp.zeros((size,), jnp.int32).at[jnp.array(offsets, jnp.int32) % size].set(
-        jnp.arange(size, dtype=jnp.int32)
-    )
-    inverse = slot_of_offset[(place - here) % size]
-    return jnp.stack(pieces), order, inverse
+    stacked = jnp.zeros((size,) + block.shape, block.dtype)
+    for slot, piece in enumerate(pieces):
+        stacked = lax.dynamic_update_index_in_dim(stacked, piece, order[slot], 0)
+    return stacked
 
 
 def local(
@@ -115,7 +109,7 @@
     particles_here = hidden_in.shape[0]
     length = hidden_in.shape[1]
     owners = lax.axis_size("dom")
-    features, order, inverse = gather_ring(hidden_in)
+    features = gather_ring(hidden_in)
     blocks = features.shape[0]
     width_in = hidden_in.shape[2]
     token_blocks = features.reshape(blocks, particles_here * length, width_in)
@@ -125,15 +119,16 @@
     group_size = width_q // width_kv
     prefix = prefix_keys.shape[1]
     every_weight = lax.all_gather(query_weight, "dom", axis=0, tiled=True)
-    weight_blocks = jnp.take(every_weight.reshape(blocks, width_in, width_q), order, axis=0)
+    weight_blocks = every_weight.reshape(blocks, width_in, width_q)
     queries = jnp.einsum(
         "ktd,kdq->tq",
         token_blocks,
         weight_blocks,
         preferred_element_type=jnp.float32,
     ).astype(jnp.bfloat16)
-    queries = queries.reshape(particles_here, length, width_q)
+    queries = queries.reshape(particles_here, length, kv_heads, group_size, HD)
     scaled = (out_grad.astype(jnp.float32) * twist_weights[:, None, None]).astype(jnp.bfloat16)
+    scaled = scaled.reshape(particles_here, length, kv_heads, group_size, HD)
 
     own_kv = jnp.concatenate([prefix_keys, prefix_values], axis=2)
     every_kv = lax.all_to_all(
@@ -144,17 +139,43 @@
         tiled=True,
     )
     picked = jnp.take(every_kv, ancestors, axis=0)
-    pre_keys = picked[:, :, :width_kv]
-    pre_values = picked[:, :, width_kv:]
-
-    grad_q, grad_sk, grad_sv, grad_pk, grad_pv = attend(
-        queries.reshape(particles_here, length, kv_heads, group_size, HD),
-        scaled.reshape(particles_here, length, kv_heads, group_size, HD),
-        segment_keys.reshape(particles_here, length, kv_heads, HD),
-        segment_values.reshape(particles_here, length, kv_heads, HD),
-        pre_keys.reshape(particles_here, prefix, kv_heads, HD),
-        pre_values.reshape(particles_here, prefix, kv_heads, HD),
-    )
+    pre_keys = picked[:, :, :width_kv].reshape(particles_here, prefix, kv_heads, HD)
+    pre_values = picked[:, :, width_kv:].reshape(particles_here, prefix, kv_heads, HD)
+    seg_keys = segment_keys.reshape(particles_here, length, kv_heads, HD)
+    seg_values = segment_values.reshape(particles_here, length, kv_heads, HD)
+
+    halves = 2
+    per_half = group_size // halves
+    weight_parts = []
+    sums = None
+    for half in range(halves):
+        heads = slice(half * per_half, (half + 1) * per_half)
+        results = attend(
+            queries[:, :, :, heads],
+            scaled[:, :, :, heads],
+            seg_keys,
+            seg_values,
+            pre_keys,
+            pre_values,
+        )
+        grad_rows = results[0].reshape(particles_here * length, width_q // halves)
+        partial = jnp.einsum(
+            "ktd,tq->kdq", token_blocks, grad_rows, preferred_element_type=jnp.float32
+        ).astype(jnp.bfloat16)
+        if half + 1 < halves:
+            partial, queries, scaled = lax.optimization_barrier((partial, queries, scaled))
+        weight_parts.append(
+            lax.psum_scatter(
+                partial.reshape(blocks * width_in, width_q // halves),
+                "dom",
+                scatter_dimension=0,
+                tiled=True,
+            )
+        )
+        sums = results[1:] if sums is None else tuple(a + b for a, b in zip(sums, results[1:]))
+    grad_sk, grad_sv, grad_pk, grad_pv = sums
+    grad_weight = jnp.concatenate(weight_parts, axis=1)
+
     grad_pkv = jnp.concatenate(
         [
             grad_pk.reshape(particles_here, prefix, width_kv),
@@ -174,19 +195,8 @@
     grad_pre_keys = summed[None, :, :width_kv]
     grad_pre_values = summed[None, :, width_kv:]
 
-    grad_seg_keys = grad_sk.reshape(particles_here, length, width_kv)
-    grad_seg_values = grad_sv.reshape(particles_here, length, width_kv)
-    grad_rows = grad_q.reshape(particles_here * length, width_q)
-    partial = jnp.einsum(
-        "ktd,tq->kdq", token_blocks, grad_rows, preferred_element_type=jnp.float32
-    ).astype(jnp.bfloat16)
-    partial = jnp.take(partial, inverse, axis=0).reshape(blocks * width_in, width_q)
-    grad_weight = lax.psum_scatter(
-        partial,
-        "dom",
-        scatter_dimension=0,
-        tiled=True,
-    )
+    grad_seg_keys = grad_sk.astype(jnp.bfloat16).reshape(particles_here, length, width_kv)
+    grad_seg_values = grad_sv.astype(jnp.bfloat16).reshape(particles_here, length, width_kv)
     return (grad_weight, grad_seg_keys, grad_seg_values, grad_pre_keys, grad_pre_values)
 
 

time: 394 us -> 524 us (1.33)
  waiting for transfers between devices: 199 us -> 307 us
  between operations: 14.4 us -> 29.8 us
  local copies, waits for them, and re-layouts: 40.5 us -> 45.8 us
    reduce_scatter x1 -> x2, waiting for transfers between devices: 55.1 us -> 251 us  [local(): lax.psum_scatter(partial.reshape(blocks * width_in, width_q // halves), '...]
    all_to_all x1, waiting for transfers between devices: 68.9 us -> 0.01 us  [local(): lax.all_to_all(outgoing.astype(jnp.bfloat16), 'dom', split_axis=0, concat...]
    ppermute x4, waiting for transfers between devices: 73.8 us -> 54.4 us  [gather_ring(): moving = lax.ppermute(moving, 'tp', forward)]
    dynamic_update_slice x0 -> x8, local copies, waits for them, and re-layouts: none -> 13 us  [gather_ring(): stacked = lax.dynamic_update_index_in_dim(stacked, piece, order[slot], 0)]
    gather x3 -> x0, local copies, waits for them, and re-layouts: 10.6 us -> none  [the longest x1 5 us: local(): jnp.take(every_weight.reshape(blocks, width_in, width_q), order, axis=0)]
    unnamed x37 -> x64, local copies, waits for them, and re-layouts: 10.4 us -> 4.48 us
    dot_general x1 -> x2, matrix products: 9.48 us -> 13.7 us  [local(): jnp.einsum('ktd,tq->kdq', token_blocks, grad_rows, preferred_element_type...]
  transfers between devices with their start and end apart: 11 -> 12, of which waited for: 6 -> 5; matrix products, arithmetic and copies ran while one was open for 16% -> 9% of each run, Pallas kernels for 0% -> 0%
where the time goes in v4:
time: 524 us; the launch traced here: 523 us
  waiting for transfers between devices  307 us (59%)
  starting transfers between devices  83 us (16%)
  local copies, waits for them, and re-layouts  45.8 us (9%)
  matrix products  42.5 us (8%)
  between operations  29.8 us (6%)
  other arithmetic  14.5 us (3%)
    reduce_scatter x2, waiting for transfers between devices, local(): lax.psum_scatter(partial.reshape(blocks * width_in, width_q // halves), '...  251 us
    ppermute x3, starting transfers between devices, gather_ring(): moving = lax.ppermute(moving, 'tp', backward)  54.5 us
    ppermute x4, waiting for transfers between devices, gather_ring(): moving = lax.ppermute(moving, 'tp', forward)  54.4 us
    dot_general x2, matrix products, local(): jnp.einsum('ktd,tq->kdq', token_blocks, grad_rows, preferred_element_type...  13.7 us
    dynamic_update_slice x8, local copies, waits for them, and re-layouts, gather_ring(): stacked = lax.dynamic_update_index_in_dim(stacked, piece, order[slot], 0)  13 us
    all_to_all x1, starting transfers between devices, local(): lax.all_to_all(outgoing.astype(jnp.bfloat16), 'dom', split_axis=0, concat...  12.6 us
    all_to_all x1, starting transfers between devices, local(): lax.all_to_all(jnp.broadcast_to(own_kv, (owners,) + own_kv.shape[1:]), 'd...  11.8 us
  transfers between devices with their start and end apart: 12, of which 5 were waited for; matrix products, arithmetic and copies ran while one was open for 9% of the time, Pallas kernels for 0%

profile of v4, /device:TPU:2, one launch (start us, length us, event | category | flops | bytes accessed | tf_op | source)
XLA Modules:
  0.0 522.8 jit_solution(6021756438894266965)
XLA Ops:
  8.8 2.5 broadcast_in_dim.93
  11.4 11.8 %all-to-all-start = ((bf16[32,256,256]{2,1,0:T(8,128)(2,1)}), bf16[32,256,256]{2,1,0:T(8,128)(2,1)}, u32[]{:S(2)}, u32[]{:S(2)}) async-start(bf16[32,256,256]{2,1,0:T(8,128)(2,1)} %broadcast_in_dim.93), calls=%async_computation | async-start | bytes 8388608 | tf_op jit(solution)/shard_map/all_to_all | solution.py:134
  24.7 21.2 %collective-permute-done = bf16[14,64,512]{2,1,0:T(8,128)(2,1)S(1)} collective-permute-done((bf16[14,64,512]{2,1,0:T(8,128)(2,1)}, bf16[14,64,512]{2,1,0:T(8,128)(2,1)S(1)}, u32[]{:S(2)}, u32[]{:S(2)}) %collective-permute-start) | collective-permute-done | bytes 917536 | tf_op jit(solution)/shard_map/ppermute | solution.py:81
  47.4 17.9 %collective-permute-start.4 = (bf16[14,64,512]{2,1,0:T(8,128)(2,1)}, bf16[14,64,512]{2,1,0:T(8,128)(2,1)}, u32[]{:S(2)}, u32[]{:S(2)}) collective-permute-start(bf16[14,64,512]{2,1,0:T(8,128)(2,1)} %param.11), channel_id=1, source_target_pairs={{2,0},{4,2},{6,4},{7,6},{5,7},{3,5},{1,3},{0,1},{10,8},{12,10},{14... | collective-permute-start | bytes 2752520 | tf_op jit(solution)/shard_map/ppermute | solution.py:85
  67.2 18.5 %collective-permute-done.1 = bf16[14,64,512]{2,1,0:T(8,128)(2,1)} collective-permute-done((bf16[14,64,512]{2,1,0:T(8,128)(2,1)S(1)}, bf16[14,64,512]{2,1,0:T(8,128)(2,1)}, u32[]{:S(2)}, u32[]{:S(2)}) %collective-permute-start.1) | collective-permute-done | bytes 917536 | tf_op jit(solution)/shard_map/ppermute | solution.py:81
  86.7 35.5 %collective-permute-start.5 = (bf16[14,64,512]{2,1,0:T(8,128)(2,1)}, bf16[14,64,512]{2,1,0:T(8,128)(2,1)S(1)}, u32[]{:S(2)}, u32[]{:S(2)}) collective-permute-start(bf16[14,64,512]{2,1,0:T(8,128)(2,1)} %collective-permute-done.4), channel_id=1, source_target_pairs={{2,0},{4,2},{6,4},{7,6},{5,7},{3,5},{1,3},{0,1},{10,8},{12,10},{14... | collective-permute-start | bytes 2752520 | tf_op jit(solution)/shard_map/ppermute | solution.py:85
  139.1 3.9 broadcast_in_dim.80
  143.0 2.3 bitcast_dynamic-update-slice_fusion.7
  148.4 2.2 bitcast_dynamic-update-slice_fusion.5
  150.6 2.2 bitcast_dynamic-update-slice_fusion.4
  152.8 14.8 %collective-permute-done.3 = bf16[14,64,512]{2,1,0:T(8,128)(2,1)S(1)} collective-permute-done((bf16[14,64,512]{2,1,0:T(8,128)(2,1)}, bf16[14,64,512]{2,1,0:T(8,128)(2,1)S(1)}, u32[]{:S(2)}, u32[]{:S(2)}) %collective-permute-start.3) | collective-permute-done | bytes 917536 | tf_op jit(solution)/shard_map/ppermute | solution.py:81
  168.6 2.2 bitcast_dynamic-update-slice_fusion.2
  172.9 8.2 %bitcast_convert_fusion = bf16[896,512]{1,0:T(8,128)(2,1)S(1)} fusion(bf16[8,896,512]{2,1,0:T(8,128)(2,1)} %bitcast.17, bf16[8,512,512]{2,1,0:T(8,128)(2,1)} %bitcast.355), kind=kOutput, calls=%fused_computation.28 | convolution fusion | flops 3758555136 | bytes 12451840 | tf_op jit(solution)/shard_map/ktd,kdq->tq/dot_general | solution.py:123
  182.3 2.9 gather_fusion.1
  195.7 6.9 %convolution_convert_fusion.2 = bf16[8,512,256]{2,1,0:T(8,128)(2,1)} fusion(bf16[8,896,512]{2,1,0:T(8,128)(2,1)} %bitcast.17, bf16[896,256,1]{1,0,2:T(8,128)(2,1)} %reshape.330), kind=kOutput, calls=%fused_computation.6 | convolution fusion | flops 1880096768 | bytes 9895936 | tf_op jit(solution)/shard_map/ktd,tq->kdq/dot_general | solution.py:162
  214.0 2.2 pad_maximum_fusion
  216.2 5.4 %copy.51 = f32[14,256,256]{2,0,1:T(8,128)} copy(f32[14,256,256]{1,2,0:T(8,128)} %pad_maximum_fusion) | data formatting | bytes 7340032 | tf_op jit(solution)/shard_map/concatenate | solution.py:179
  221.6 5.6 %convolution_convert_fusion = bf16[32,256,256]{2,0,1:T(8,128)(2,1)S(1)} fusion(f32[14,256,256]{2,0,1:T(8,128)} %copy.51, s32[14]{0:T(128)S(1)} %copy-done.26), kind=kOutput, calls=%fused_computation.4 | convolution fusion | flops 354419136 | bytes 7864376 | tf_op jit(solution)/shard_map/ap,pjc->ajc/dot_general | solution.py:188
  227.2 4.5 copy.52
  231.7 12.6 %all-to-all-start.1 = ((bf16[32,256,256]{2,1,0:T(8,128)(2,1)}), bf16[32,256,256]{2,1,0:T(8,128)(2,1)}, u32[]{:S(2)}, u32[]{:S(2)}) async-start(bf16[32,256,256]{2,1,0:T(8,128)(2,1)} %copy.52), calls=%async_computation.3 | async-start | bytes 8388608 | tf_op jit(solution)/shard_map/all_to_all | solution.py:191
  247.9 6.8 %convolution_convert_fusion.1 = bf16[8,512,256]{2,1,0:T(8,128)(2,1)} fusion(bf16[8,896,512]{2,1,0:T(8,128)(2,1)} %bitcast.17, bf16[896,256,1]{1,0,2:T(8,128)(2,1)S(1)} %reshape.331), kind=kOutput, calls=%fused_computation.5 | convolution fusion | flops 1880096768 | bytes 9895936 | tf_op jit(solution)/shard_map/ktd,tq->kdq/dot_general | solution.py:162
  259.9 129.4 %reduce-scatter.5.cloned.1.call-done = bf16[128,256]{1,0:T(8,128)(2,1)} async-done(((bf16[4096,256]{1,0:T(8,128)(2,1)}), bf16[128,256]{1,0:T(8,128)(2,1)}) %reduce-scatter.5.cloned.1.call-update) | async-done | bytes 65552 | tf_op jit(solution)/shard_map/reduce_scatter | solution.py:168
  389.3 121.9 %reduce-scatter.3.cloned.1.call-done = bf16[128,256]{1,0:T(8,128)(2,1)} async-done(((bf16[4096,256]{1,0:T(8,128)(2,1)}), bf16[128,256]{1,0:T(8,128)(2,1)}) %reduce-scatter.3.cloned.1.call-update) | async-done | bytes 65552 | tf_op jit(solution)/shard_map/reduce_scatter | solution.py:168
  512.8 2.8 convert_reduce_fusion
  (144 shorter events, 49.0 us)
Async XLA Ops:
  7.2 178.7 %copy-start = (bf16[14,64,128]{2,1,0:T(8,128)(2,1)S(1)}, bf16[14,64,128]{2,1,0:T(8,128)(2,1)}, u32[]{:S(2)}) copy-start(bf16[14,64,128]{2,1,0:T(8,128)(2,1)} %param.13) | copy-start | bytes 688132
  7.2 165.7 %all-gather.2.cloned.1.call-start = ((), (), s32[]{:S(2)}) async-start(), calls=%async_computation.4 | async-start | bytes 4325376 | tf_op jit(solution)/shard_map/all_gather | solution.py:121
  11.3 53.9 %copy-start.31 = (s32[8]{0:T(128)S(1)}, s32[8]{0:T(128)}, u32[]{:S(2)}) copy-start(s32[8]{0:T(128)} %constant.85) | copy-start | bytes 100
  11.3 54.5 %copy-start.30 = (s32[8]{0:T(128)S(1)}, s32[8]{0:T(128)}, u32[]{:S(2)}) copy-start(s32[8]{0:T(128)} %constant.72.clone) | copy-start | bytes 100
  11.3 55.2 %copy-start.1 = (s32[8]{0:T(128)S(1)}, s32[8]{0:T(128)}, u32[]{:S(2)}) copy-start(s32[8]{0:T(128)} %constant.71.clone) | copy-start | bytes 100
  11.3 55.8 %copy-start.26 = (s32[14]{0:T(128)S(1)}, s32[14]{0:T(128)}, u32[]{:S(2)}) copy-start(s32[14]{0:T(128)} %param.17) | copy-start | bytes 172
  11.3 75.0 %copy-start.20 = (bf16[14,64,512]{2,1,0:T(8,128)(2,1)S(1)}, bf16[14,64,512]{2,1,0:T(8,128)(2,1)}, u32[]{:S(2)}) copy-start(bf16[14,64,512]{2,1,0:T(8,128)(2,1)} %param.19) | copy-start | bytes 2752516
  11.3 75.0 %copy-start.27 = (f32[14]{0:T(128)S(1)}, f32[14]{0:T(128)}, u32[]{:S(2)}) copy-start(f32[14]{0:T(128)} %param.18) | copy-start | bytes 172
  11.4 170.9 %all-to-all-start = ((bf16[32,256,256]{2,1,0:T(8,128)(2,1)}), bf16[32,256,256]{2,1,0:T(8,128)(2,1)}, u32[]{:S(2)}, u32[]{:S(2)}) async-start(bf16[32,256,256]{2,1,0:T(8,128)(2,1)} %broadcast_in_dim.93), calls=%async_computation | async-start | bytes 8388608 | tf_op jit(solution)/shard_map/all_to_all | solution.py:134
  23.1 22.7 %collective-permute-start = (bf16[14,64,512]{2,1,0:T(8,128)(2,1)}, bf16[14,64,512]{2,1,0:T(8,128)(2,1)S(1)}, u32[]{:S(2)}, u32[]{:S(2)}) collective-permute-start(bf16[14,64,512]{2,1,0:T(8,128)(2,1)} %param.11), channel_id=1, source_target_pairs={{0,2},{2,4},{4,6},{6,7},{7,5},{5,3},{3,1},{1,0},{8,10},{10,12},{12... | collective-permute-start | bytes 2752520 | tf_op jit(solution)/shard_map/ppermute | solution.py:81
  45.9 39.8 %copy-start.21 = (bf16[14,64,512]{2,1,0:T(8,128)(2,1)}, bf16[14,64,512]{2,1,0:T(8,128)(2,1)S(1)}, u32[]{:S(2)}) copy-start(bf16[14,64,512]{2,1,0:T(8,128)(2,1)S(1)} %collective-permute-done) | copy-start | bytes 2752516
  45.9 39.8 %collective-permute-start.1 = (bf16[14,64,512]{2,1,0:T(8,128)(2,1)S(1)}, bf16[14,64,512]{2,1,0:T(8,128)(2,1)}, u32[]{:S(2)}, u32[]{:S(2)}) collective-permute-start(bf16[14,64,512]{2,1,0:T(8,128)(2,1)S(1)} %collective-permute-done), channel_id=1, source_target_pairs={{0,2},{2,4},{4,6},{6,7},{7,5},{5,3},{3,1},{1,0},{8,10},{10,12},{12... | collective-permute-start | bytes 2752520 | tf_op jit(solution)/shard_map/ppermute | solution.py:81
  47.4 39.3 %collective-permute-start.4 = (bf16[14,64,512]{2,1,0:T(8,128)(2,1)}, bf16[14,64,512]{2,1,0:T(8,128)(2,1)}, u32[]{:S(2)}, u32[]{:S(2)}) collective-permute-start(bf16[14,64,512]{2,1,0:T(8,128)(2,1)} %param.11), channel_id=1, source_target_pairs={{2,0},{4,2},{6,4},{7,6},{5,7},{3,5},{1,3},{0,1},{10,8},{12,10},{14... | collective-permute-start | bytes 2752520 | tf_op jit(solution)/shard_map/ppermute | solution.py:85
  85.6 59.6 %collective-permute-start.2 = (bf16[14,64,512]{2,1,0:T(8,128)(2,1)}, bf16[14,64,512]{2,1,0:T(8,128)(2,1)}, u32[]{:S(2)}, u32[]{:S(2)}) collective-permute-start(bf16[14,64,512]{2,1,0:T(8,128)(2,1)} %collective-permute-done.1), channel_id=1, source_target_pairs={{0,2},{2,4},{4,6},{6,7},{7,5},{5,3},{3,1},{1,0},{8,10},{10,12},{12... | collective-permute-start | bytes 2752520 | tf_op jit(solution)/shard_map/ppermute | solution.py:81
  86.7 60.5 %collective-permute-start.5 = (bf16[14,64,512]{2,1,0:T(8,128)(2,1)}, bf16[14,64,512]{2,1,0:T(8,128)(2,1)S(1)}, u32[]{:S(2)}, u32[]{:S(2)}) collective-permute-start(bf16[14,64,512]{2,1,0:T(8,128)(2,1)} %collective-permute-done.4), channel_id=1, source_target_pairs={{2,0},{4,2},{6,4},{7,6},{5,7},{3,5},{1,3},{0,1},{10,8},{12,10},{14... | collective-permute-start | bytes 2752520 | tf_op jit(solution)/shard_map/ppermute | solution.py:85
  132.7 10.3 %copy-start.5 = (bf16[14,64,1,4,128]{4,3,1,0,2:T(4,128)(2,1)}, bf16[14,64,1,4,128]{4,3,1,0,2:T(4,128)(2,1)S(1)}, u32[]{:S(2)}) copy-start(bf16[14,64,1,4,128]{4,3,1,0,2:T(4,128)(2,1)S(1)} %reshape.287) | copy-start | bytes 2752516
  145.2 22.3 %collective-permute-start.3 = (bf16[14,64,512]{2,1,0:T(8,128)(2,1)}, bf16[14,64,512]{2,1,0:T(8,128)(2,1)S(1)}, u32[]{:S(2)}, u32[]{:S(2)}) collective-permute-start(bf16[14,64,512]{2,1,0:T(8,128)(2,1)} %collective-permute-done.2), channel_id=1, source_target_pairs={{0,2},{2,4},{4,6},{6,7},{7,5},{5,3},{3,1},{1,0},{8,10},{10,12},{12... | collective-permute-start | bytes 2752520 | tf_op jit(solution)/shard_map/ppermute | solution.py:81
  147.2 24.6 %collective-permute-start.6 = (bf16[14,64,512]{2,1,0:T(8,128)(2,1)S(1)}, bf16[14,64,512]{2,1,0:T(8,128)(2,1)S(1)}, u32[]{:S(2)}, u32[]{:S(2)}) collective-permute-start(bf16[14,64,512]{2,1,0:T(8,128)(2,1)S(1)} %collective-permute-done.5), channel_id=1, source_target_pairs={{2,0},{4,2},{6,4},{7,6},{5,7},{3,5},{1,3},{0,1},{10,8},{12,10},{14... | collective-permute-start | bytes 2752520 | tf_op jit(solution)/shard_map/ppermute | solution.py:85
  185.4 5.0 copy-start.2
  195.7 6.9 %copy-start.10 = (bf16[14,64,1,4,128]{4,3,1,0,2:T(4,128)(2,1)S(1)}, bf16[14,64,1,4,128]{4,3,1,0,2:T(4,128)(2,1)}, u32[]{:S(2)}) copy-start(bf16[14,64,1,4,128]{4,3,1,0,2:T(4,128)(2,1)} %copy-done.9) | copy-start | bytes 2752516
  204.1 9.4 %copy-start.7 = (bf16[14,64,1,4,128]{4,1,3,0,2:T(8,128)(2,1)}, bf16[14,64,1,4,128]{4,1,3,0,2:T(8,128)(2,1)S(1)}, u32[]{:S(2)}) copy-start(bf16[14,64,1,4,128]{4,1,3,0,2:T(8,128)(2,1)S(1)} %copy.46) | copy-start | bytes 2752516
  231.7 281.1 %all-to-all-start.1 = ((bf16[32,256,256]{2,1,0:T(8,128)(2,1)}), bf16[32,256,256]{2,1,0:T(8,128)(2,1)}, u32[]{:S(2)}, u32[]{:S(2)}) async-start(bf16[32,256,256]{2,1,0:T(8,128)(2,1)} %copy.52), calls=%async_computation.3 | async-start | bytes 8388608 | tf_op jit(solution)/shard_map/all_to_all | solution.py:191
  244.3 145.0 %reduce-scatter.5.cloned.1.call-start = ((), (), s32[]{:S(2)}) async-start(), calls=%async_computation.6 | async-start | bytes 2162688 | tf_op jit(solution)/shard_map/reduce_scatter | solution.py:168
  254.7 256.5 %reduce-scatter.3.cloned.1.call-start = ((), (), s32[]{:S(2)}) async-start(), calls=%async_computation.5 | async-start | bytes 2162688 | tf_op jit(solution)/shard_map/reduce_scatter | solution.py:168
  (20 other events, 38.1 us)
Sparse Core Ops, SparseCore 0:
  10.8 122.2 all-gather.1
  254.8 134.3 reduce-scatter.4
  393.4 117.7 reduce-scatter.2

commit v5 on v3

--- a/solution.py
+++ b/solution.py
@@ -4,6 +4,7 @@
 import jax.numpy as jnp
 from jax import lax
 from jax.sharding import PartitionSpec as P
+
 
 HD = 128
 
@@ -94,11 +95,10 @@
     place = jnp.zeros((size,), jnp.int32).at[ring].set(jnp.arange(size, dtype=jnp.int32))
     here = place[lax.axis_index("tp")]
     order = ring[(here + jnp.array(offsets, jnp.int32)) % size]
-    slot_of_offset = jnp.zeros((size,), jnp.int32).at[jnp.array(offsets, jnp.int32) % size].set(
-        jnp.arange(size, dtype=jnp.int32)
-    )
-    inverse = slot_of_offset[(place - here) % size]
-    return jnp.stack(pieces), order, inverse
+    stacked = jnp.zeros((size,) + block.shape, block.dtype)
+    for slot, piece in enumerate(pieces):
+        stacked = lax.dynamic_update_index_in_dim(stacked, piece, order[slot], 0)
+    return stacked
 
 
 def local(
@@ -115,7 +115,7 @@
     particles_here = hidden_in.shape[0]
     length = hidden_in.shape[1]
     owners = lax.axis_size("dom")
-    features, order, inverse = gather_ring(hidden_in)
+    features = gather_ring(hidden_in)
     blocks = features.shape[0]
     width_in = hidden_in.shape[2]
     token_blocks = features.reshape(blocks, particles_here * length, width_in)
@@ -125,7 +125,7 @@
     group_size = width_q // width_kv
     prefix = prefix_keys.shape[1]
     every_weight = lax.all_gather(query_weight, "dom", axis=0, tiled=True)
-    weight_blocks = jnp.take(every_weight.reshape(blocks, width_in, width_q), order, axis=0)
+    weight_blocks = every_weight.reshape(blocks, width_in, width_q)
     queries = jnp.einsum(
         "ktd,kdq->tq",
         token_blocks,
@@ -155,6 +155,16 @@
         pre_keys.reshape(particles_here, prefix, kv_heads, HD),
         pre_values.reshape(particles_here, prefix, kv_heads, HD),
     )
+    grad_rows = grad_q.reshape(particles_here * length, width_q)
+    partial = jnp.einsum(
+        "ktd,tq->kdq", token_blocks, grad_rows, preferred_element_type=jnp.float32
+    ).astype(jnp.bfloat16)
+    grad_weight = lax.psum_scatter(
+        partial.reshape(blocks * width_in, width_q),
+        "dom",
+        scatter_dimension=0,
+        tiled=True,
+    )
     grad_pkv = jnp.concatenate(
         [
             grad_pk.reshape(particles_here, prefix, width_kv),
@@ -173,20 +183,8 @@
     summed = jnp.sum(incoming.astype(jnp.float32), axis=0)
     grad_pre_keys = summed[None, :, :width_kv]
     grad_pre_values = summed[None, :, width_kv:]
-
     grad_seg_keys = grad_sk.reshape(particles_here, length, width_kv)
     grad_seg_values = grad_sv.reshape(particles_here, length, width_kv)
-    grad_rows = grad_q.reshape(particles_here * length, width_q)
-    partial = jnp.einsum(
-        "ktd,tq->kdq", token_blocks, grad_rows, preferred_element_type=jnp.float32
-    ).astype(jnp.bfloat16)
-    partial = jnp.take(partial, inverse, axis=0).reshape(blocks * width_in, width_q)
-    grad_weight = lax.psum_scatter(
-        partial,
-        "dom",
-        scatter_dimension=0,
-        tiled=True,
-    )
     return (grad_weight, grad_seg_keys, grad_seg_values, grad_pre_keys, grad_pre_values)
 
 

time: 394 us -> 389 us (0.987)
  between operations: 14.4 us -> 29.5 us
  waiting for transfers between devices: 199 us -> 187 us
  local copies, waits for them, and re-layouts: 40.5 us -> 35.5 us
  other arithmetic: 18 us -> 13.4 us
    ppermute x4, waiting for transfers between devices: 73.8 us -> 54.9 us  [gather_ring(): moving = lax.ppermute(moving, 'tp', forward)]
    dynamic_update_slice x0 -> x8, local copies, waits for them, and re-layouts: none -> 11.7 us  [gather_ring(): stacked = lax.dynamic_update_index_in_dim(stacked, piece, order[slot], 0)]
    all_to_all x1, waiting for transfers between devices: 68.9 us -> 79.8 us  [local(): lax.all_to_all(outgoing.astype(jnp.bfloat16), 'dom', split_axis=0, concat...]
    gather x3 -> x0, local copies, waits for them, and re-layouts: 10.6 us -> none  [the longest x1 5 us: local(): jnp.take(every_weight.reshape(blocks, width_in, width_q), order, axis=0)]
    unnamed x37 -> x28, local copies, waits for them, and re-layouts: 10.4 us -> 1.01 us
    select_n x4 -> x1, other arithmetic: 5.26 us -> 0.66 us  [gather_ring(): order = ring[(here + jnp.array(offsets, jnp.int32)) % size]]
  transfers between devices with their start and end apart: 11 -> 11, of which waited for: 6 -> 6; matrix products, arithmetic and copies ran while one was open for 16% -> 14% of each run, Pallas kernels for 0% -> 0%
where the time goes in v5:
time: 389 us; the launch traced here: 388 us
  waiting for transfers between devices  187 us (48%)
  starting transfers between devices  82.6 us (21%)
  matrix products  39.5 us (10%)
  local copies, waits for them, and re-layouts  35.5 us (9%)
  between operations  29.5 us (8%)
  other arithmetic  13.4 us (3%)
    all_to_all x1, waiting for transfers between devices, local(): lax.all_to_all(outgoing.astype(jnp.bfloat16), 'dom', split_axis=0, concat...  79.8 us
    ppermute x3, starting transfers between devices, gather_ring(): moving = lax.ppermute(moving, 'tp', backward)  55.4 us
    ppermute x4, waiting for transfers between devices, gather_ring(): moving = lax.ppermute(moving, 'tp', forward)  54.9 us
    reduce_scatter x1, waiting for transfers between devices, local(): lax.psum_scatter(partial.reshape(blocks * width_in, width_q), 'dom', scat...  52.1 us
    all_to_all x1, starting transfers between devices, local(): lax.all_to_all(jnp.broadcast_to(own_kv, (owners,) + own_kv.shape[1:]), 'd...  11.8 us
    dynamic_update_slice x8, local copies, waits for them, and re-layouts, gather_ring(): stacked = lax.dynamic_update_index_in_dim(stacked, piece, order[slot], 0)  11.7 us
    all_to_all x1, starting transfers between devices, local(): lax.all_to_all(outgoing.astype(jnp.bfloat16), 'dom', split_axis=0, concat...  11.1 us
    dot_general x1, matrix products, local(): jnp.einsum('ktd,tq->kdq', token_blocks, grad_rows, preferred_element_type...  9.48 us
  transfers between devices with their start and end apart: 11, of which 6 were waited for; matrix products, arithmetic and copies ran while one was open for 14% of the time, Pallas kernels for 0%

profile of v5, /device:TPU:2, one launch (start us, length us, event | category | flops | bytes accessed | tf_op | source)
XLA Modules:
  0.0 388.0 jit_solution(13041530654937421905)
XLA Ops:
  8.8 2.4 broadcast_in_dim.86
  11.2 11.8 %all-to-all-start = ((bf16[32,256,256]{2,1,0:T(8,128)(2,1)}), bf16[32,256,256]{2,1,0:T(8,128)(2,1)}, u32[]{:S(2)}, u32[]{:S(2)}) async-start(bf16[32,256,256]{2,1,0:T(8,128)(2,1)} %broadcast_in_dim.86), calls=%async_computation | async-start | bytes 8388608 | tf_op jit(solution)/shard_map/all_to_all | solution.py:139
  24.6 21.1 %collective-permute-done = bf16[14,64,512]{2,1,0:T(8,128)(2,1)} collective-permute-done((bf16[14,64,512]{2,1,0:T(8,128)(2,1)S(1)}, bf16[14,64,512]{2,1,0:T(8,128)(2,1)}, u32[]{:S(2)}, u32[]{:S(2)}) %collective-permute-start) | collective-permute-done | bytes 917536 | tf_op jit(solution)/shard_map/ppermute | solution.py:87
  47.2 18.1 %collective-permute-start.4 = (bf16[14,64,512]{2,1,0:T(8,128)(2,1)S(1)}, bf16[14,64,512]{2,1,0:T(8,128)(2,1)S(1)}, u32[]{:S(2)}, u32[]{:S(2)}) collective-permute-start(bf16[14,64,512]{2,1,0:T(8,128)(2,1)S(1)} %copy-done.7), channel_id=1, source_target_pairs={{2,0},{4,2},{6,4},{7,6},{5,7},{3,5},{1,3},{0,1},{10,8},{12,10},{14... | collective-permute-start | bytes 2752520 | tf_op jit(solution)/shard_map/ppermute | solution.py:91
  67.2 18.5 %collective-permute-done.1 = bf16[14,64,512]{2,1,0:T(8,128)(2,1)S(1)} collective-permute-done((bf16[14,64,512]{2,1,0:T(8,128)(2,1)}, bf16[14,64,512]{2,1,0:T(8,128)(2,1)S(1)}, u32[]{:S(2)}, u32[]{:S(2)}) %collective-permute-start.1) | collective-permute-done | bytes 917536 | tf_op jit(solution)/shard_map/ppermute | solution.py:87
  86.5 35.1 %collective-permute-start.5 = (bf16[14,64,512]{2,1,0:T(8,128)(2,1)S(1)}, bf16[14,64,512]{2,1,0:T(8,128)(2,1)}, u32[]{:S(2)}, u32[]{:S(2)}) collective-permute-start(bf16[14,64,512]{2,1,0:T(8,128)(2,1)S(1)} %collective-permute-done.4), channel_id=1, source_target_pairs={{2,0},{4,2},{6,4},{7,6},{5,7},{3,5},{1,3},{0,1},{10,8},{12,10},{14... | collective-permute-start | bytes 2752520 | tf_op jit(solution)/shard_map/ppermute | solution.py:91
  136.8 3.9 broadcast_in_dim.73
  150.3 15.2 %collective-permute-done.3 = bf16[14,64,512]{2,1,0:T(8,128)(2,1)S(1)} collective-permute-done((bf16[14,64,512]{2,1,0:T(8,128)(2,1)}, bf16[14,64,512]{2,1,0:T(8,128)(2,1)S(1)}, u32[]{:S(2)}, u32[]{:S(2)}) %collective-permute-start.3) | collective-permute-done | bytes 917536 | tf_op jit(solution)/shard_map/ppermute | solution.py:87
  170.9 8.2 %bitcast_convert_fusion = bf16[896,512]{1,0:T(8,128)(2,1)S(1)} fusion(bf16[8,896,512]{2,1,0:T(8,128)(2,1)} %bitcast.17, bf16[8,512,512]{2,1,0:T(8,128)(2,1)} %bitcast.230), kind=kOutput, calls=%fused_computation.30 | convolution fusion | flops 3758555136 | bytes 12451840 | tf_op jit(solution)/shard_map/ktd,kdq->tq/dot_general | solution.py:129
  179.3 2.9 gather_fusion.1
  186.1 2.7 fusion
  188.8 2.9 fusion.19
  191.8 2.4 fusion.12
  198.7 5.4 %copy.58 = f32[14,256,256]{2,0,1:T(8,128)} copy(f32[14,256,256]{1,2,0:T(8,128)} %pad_maximum_fusion) | data formatting | bytes 7340032 | tf_op jit(solution)/shard_map/concatenate | solution.py:168
  204.1 5.6 %convolution_convert_fusion = bf16[32,256,256]{2,0,1:T(8,128)(2,1)S(1)} fusion(f32[14,256,256]{2,0,1:T(8,128)} %copy.58, s32[14]{0:T(128)S(1)} %copy-done.8), kind=kOutput, calls=%fused_computation.14 | convolution fusion | flops 354419136 | bytes 7864376 | tf_op jit(solution)/shard_map/ap,pjc->ajc/dot_general | solution.py:177
  209.7 4.4 %copy.59 = bf16[32,256,256]{2,1,0:T(8,128)(2,1)} copy(bf16[32,256,256]{2,0,1:T(8,128)(2,1)S(1)} %convolution_convert_fusion) | data formatting | bytes 8388608 | tf_op jit(solution)/shard_map/convert_element_type | solution.py:181
  214.2 11.1 %all-to-all-start.1 = ((bf16[32,256,256]{2,1,0:T(8,128)(2,1)}), bf16[32,256,256]{2,1,0:T(8,128)(2,1)}, u32[]{:S(2)}, u32[]{:S(2)}) async-start(bf16[32,256,256]{2,1,0:T(8,128)(2,1)} %copy.59), calls=%async_computation.2 | async-start | bytes 8388608 | tf_op jit(solution)/shard_map/all_to_all | solution.py:180
  225.3 2.8 fusion.29
  231.3 9.5 %convolution_convert_fusion.1 = bf16[8,512,512]{2,1,0:T(8,128)(2,1)} fusion(bf16[8,896,512]{2,1,0:T(8,128)(2,1)} %bitcast.17, bf16[896,512,1]{1,0,2:T(8,128)(2,1)S(1)} %reshape.203), kind=kOutput, calls=%fused_computation.15 | convolution fusion | flops 3760193536 | bytes 12451840 | tf_op jit(solution)/shard_map/ktd,tq->kdq/dot_general | solution.py:159
  240.8 2.4 fusion.26
  243.2 2.5 fusion.27
  245.7 79.8 %all-to-all-done.1 = bf16[32,256,256]{2,1,0:T(8,128)(2,1)} async-done(((bf16[32,256,256]{2,1,0:T(8,128)(2,1)}), bf16[32,256,256]{2,1,0:T(8,128)(2,1)}, u32[]{:S(2)}, u32[]{:S(2)}) %all-to-all-start.1) | async-done | bytes 4194336 | tf_op jit(solution)/shard_map/all_to_all | solution.py:180
  325.5 2.8 convert_reduce_fusion
  329.0 52.1 %reduce-scatter.2.cloned.1.call-done = bf16[128,512]{1,0:T(8,128)(2,1)} async-done(((bf16[4096,512]{1,0:T(8,128)(2,1)}), bf16[128,512]{1,0:T(8,128)(2,1)}) %reduce-scatter.2.cloned.1.call-update) | async-done | bytes 131088 | tf_op jit(solution)/shard_map/reduce_scatter | solution.py:162
  (78 shorter events, 34.9 us)
Async XLA Ops:
  7.2 176.0 %copy-start = (bf16[14,64,128]{2,1,0:T(8,128)(2,1)S(1)}, bf16[14,64,128]{2,1,0:T(8,128)(2,1)}, u32[]{:S(2)}) copy-start(bf16[14,64,128]{2,1,0:T(8,128)(2,1)} %param.13) | copy-start | bytes 688132
  7.2 163.7 %all-gather.2.cloned.1.call-start = ((), (), s32[]{:S(2)}) async-start(), calls=%async_computation.3 | async-start | bytes 4325376 | tf_op jit(solution)/shard_map/all_gather | solution.py:127
  11.2 11.8 %copy-start.7 = (bf16[14,64,512]{2,1,0:T(8,128)(2,1)S(1)}, bf16[14,64,512]{2,1,0:T(8,128)(2,1)}, u32[]{:S(2)}) copy-start(bf16[14,64,512]{2,1,0:T(8,128)(2,1)} %param.11) | copy-start | bytes 2752516
  11.2 54.1 %copy-start.13 = (s32[8]{0:T(128)S(1)}, s32[8]{0:T(128)}, u32[]{:S(2)}) copy-start(s32[8]{0:T(128)} %constant.85) | copy-start | bytes 100
  11.2 54.6 %copy-start.12 = (s32[8]{0:T(128)S(1)}, s32[8]{0:T(128)}, u32[]{:S(2)}) copy-start(s32[8]{0:T(128)} %constant.72.clone) | copy-start | bytes 100
  11.2 55.3 %copy-start.1 = (s32[8]{0:T(128)S(1)}, s32[8]{0:T(128)}, u32[]{:S(2)}) copy-start(s32[8]{0:T(128)} %constant.71.clone) | copy-start | bytes 100
  11.2 75.2 %copy-start.8 = (s32[14]{0:T(128)S(1)}, s32[14]{0:T(128)}, u32[]{:S(2)}) copy-start(s32[14]{0:T(128)} %param.17) | copy-start | bytes 172
  11.2 168.0 %all-to-all-start = ((bf16[32,256,256]{2,1,0:T(8,128)(2,1)}), bf16[32,256,256]{2,1,0:T(8,128)(2,1)}, u32[]{:S(2)}, u32[]{:S(2)}) async-start(bf16[32,256,256]{2,1,0:T(8,128)(2,1)} %broadcast_in_dim.86), calls=%async_computation | async-start | bytes 8388608 | tf_op jit(solution)/shard_map/all_to_all | solution.py:139
  23.0 22.6 %collective-permute-start = (bf16[14,64,512]{2,1,0:T(8,128)(2,1)S(1)}, bf16[14,64,512]{2,1,0:T(8,128)(2,1)}, u32[]{:S(2)}, u32[]{:S(2)}) collective-permute-start(bf16[14,64,512]{2,1,0:T(8,128)(2,1)S(1)} %copy-done.7), channel_id=1, source_target_pairs={{0,2},{2,4},{4,6},{6,7},{7,5},{5,3},{3,1},{1,0},{8,10},{10,12},{12... | collective-permute-start | bytes 2752520 | tf_op jit(solution)/shard_map/ppermute | solution.py:87
  45.7 40.0 %collective-permute-start.1 = (bf16[14,64,512]{2,1,0:T(8,128)(2,1)}, bf16[14,64,512]{2,1,0:T(8,128)(2,1)S(1)}, u32[]{:S(2)}, u32[]{:S(2)}) collective-permute-start(bf16[14,64,512]{2,1,0:T(8,128)(2,1)} %collective-permute-done), channel_id=1, source_target_pairs={{0,2},{2,4},{4,6},{6,7},{7,5},{5,3},{3,1},{1,0},{8,10},{10,12},{12... | collective-permute-start | bytes 2752520 | tf_op jit(solution)/shard_map/ppermute | solution.py:87
  47.2 39.3 %collective-permute-start.4 = (bf16[14,64,512]{2,1,0:T(8,128)(2,1)S(1)}, bf16[14,64,512]{2,1,0:T(8,128)(2,1)S(1)}, u32[]{:S(2)}, u32[]{:S(2)}) collective-permute-start(bf16[14,64,512]{2,1,0:T(8,128)(2,1)S(1)} %copy-done.7), channel_id=1, source_target_pairs={{2,0},{4,2},{6,4},{7,6},{5,7},{3,5},{1,3},{0,1},{10,8},{12,10},{14... | collective-permute-start | bytes 2752520 | tf_op jit(solution)/shard_map/ppermute | solution.py:91
  85.7 56.0 %collective-permute-start.2 = (bf16[14,64,512]{2,1,0:T(8,128)(2,1)S(1)}, bf16[14,64,512]{2,1,0:T(8,128)(2,1)}, u32[]{:S(2)}, u32[]{:S(2)}) collective-permute-start(bf16[14,64,512]{2,1,0:T(8,128)(2,1)S(1)} %collective-permute-done.1), channel_id=1, source_target_pairs={{0,2},{2,4},{4,6},{6,7},{7,5},{5,3},{3,1},{1,0},{8,10},{10,12},{12... | collective-permute-start | bytes 2752520 | tf_op jit(solution)/shard_map/ppermute | solution.py:87
  86.5 58.4 %collective-permute-start.5 = (bf16[14,64,512]{2,1,0:T(8,128)(2,1)S(1)}, bf16[14,64,512]{2,1,0:T(8,128)(2,1)}, u32[]{:S(2)}, u32[]{:S(2)}) collective-permute-start(bf16[14,64,512]{2,1,0:T(8,128)(2,1)S(1)} %collective-permute-done.4), channel_id=1, source_target_pairs={{2,0},{4,2},{6,4},{7,6},{5,7},{3,5},{1,3},{0,1},{10,8},{12,10},{14... | collective-permute-start | bytes 2752520 | tf_op jit(solution)/shard_map/ppermute | solution.py:91
  141.7 23.9 %collective-permute-start.3 = (bf16[14,64,512]{2,1,0:T(8,128)(2,1)}, bf16[14,64,512]{2,1,0:T(8,128)(2,1)S(1)}, u32[]{:S(2)}, u32[]{:S(2)}) collective-permute-start(bf16[14,64,512]{2,1,0:T(8,128)(2,1)} %collective-permute-done.2), channel_id=1, source_target_pairs={{0,2},{2,4},{4,6},{6,7},{7,5},{5,3},{3,1},{1,0},{8,10},{10,12},{12... | collective-permute-start | bytes 2752520 | tf_op jit(solution)/shard_map/ppermute | solution.py:87
  144.9 24.9 %collective-permute-start.6 = (bf16[14,64,512]{2,1,0:T(8,128)(2,1)}, bf16[14,64,512]{2,1,0:T(8,128)(2,1)S(1)}, u32[]{:S(2)}, u32[]{:S(2)}) collective-permute-start(bf16[14,64,512]{2,1,0:T(8,128)(2,1)} %collective-permute-done.5), channel_id=1, source_target_pairs={{2,0},{4,2},{6,4},{7,6},{5,7},{3,5},{1,3},{0,1},{10,8},{12,10},{14... | collective-permute-start | bytes 2752520 | tf_op jit(solution)/shard_map/ppermute | solution.py:91
  182.4 3.7 copy-start.4
  184.2 7.6 %copy-start.2 = (f32[14,1,4,64,64]{3,4,2,0,1:T(8,128)}, f32[14,1,4,64,64]{3,4,2,0,1:T(8,128)S(1)}, u32[]{:S(2)}) copy-start(f32[14,1,4,64,64]{3,4,2,0,1:T(8,128)S(1)} %get-tuple-element.18) | copy-start | bytes 2752516
  184.2 1.9 copy-start.9
  184.2 1.9 copy-start.11
  188.8 3.0 copy-start.10
  214.2 111.3 %all-to-all-start.1 = ((bf16[32,256,256]{2,1,0:T(8,128)(2,1)}), bf16[32,256,256]{2,1,0:T(8,128)(2,1)}, u32[]{:S(2)}, u32[]{:S(2)}) async-start(bf16[32,256,256]{2,1,0:T(8,128)(2,1)} %copy.59), calls=%async_computation.2 | async-start | bytes 8388608 | tf_op jit(solution)/shard_map/all_to_all | solution.py:180
  225.2 155.9 %reduce-scatter.2.cloned.1.call-start = ((), (), s32[]{:S(2)}) async-start(), calls=%async_computation.4 | async-start | bytes 4325376 | tf_op jit(solution)/shard_map/reduce_scatter | solution.py:162
  225.3 4.3 %copy-start.5 = (bf16[14,256,256]{2,1,0:T(8,128)(2,1)S(1)}, bf16[14,256,256]{2,1,0:T(8,128)(2,1)}, u32[]{:S(2)}) copy-start(bf16[14,256,256]{2,1,0:T(8,128)(2,1)} %copy-done.4) | copy-start | bytes 5505028
  240.8 2.4 copy-start.3
  (1 other events, 1.0 us)
Sparse Core Ops, SparseCore 0:
  10.8 122.1 all-gather.1
  240.9 140.1 reduce-scatter.1

commit v6 on v5

--- a/solution.py
+++ b/solution.py
@@ -7,6 +7,7 @@
 
 
 HD = 128
+DOM = ("dh", "dc")
 
 
 def attend(queries, scaled, seg_keys, seg_values, pre_keys, pre_values):
@@ -101,6 +102,14 @@
     return stacked
 
 
+def pair_sum(block):
+    mine = lax.axis_index("dc")
+    kept = lax.dynamic_index_in_dim(block, mine, axis=1, keepdims=False)
+    sent = lax.dynamic_index_in_dim(block, 1 - mine, axis=1, keepdims=False)
+    other = lax.ppermute(sent, "dc", [(0, 1), (1, 0)])
+    return kept.astype(jnp.float32) + other.astype(jnp.float32)
+
+
 def local(
     hidden_in,
     query_weight,
@@ -114,7 +123,7 @@
 ):
     particles_here = hidden_in.shape[0]
     length = hidden_in.shape[1]
-    owners = lax.axis_size("dom")
+    owners = lax.axis_size(DOM)
     features = gather_ring(hidden_in)
     blocks = features.shape[0]
     width_in = hidden_in.shape[2]
@@ -124,7 +133,7 @@
     kv_heads = width_kv // HD
     group_size = width_q // width_kv
     prefix = prefix_keys.shape[1]
-    every_weight = lax.all_gather(query_weight, "dom", axis=0, tiled=True)
+    every_weight = lax.all_gather(query_weight, DOM, axis=0, tiled=True)
     weight_blocks = every_weight.reshape(blocks, width_in, width_q)
     queries = jnp.einsum(
         "ktd,kdq->tq",
@@ -138,7 +147,7 @@
     own_kv = jnp.concatenate([prefix_keys, prefix_values], axis=2)
     every_kv = lax.all_to_all(
         jnp.broadcast_to(own_kv, (owners,) + own_kv.shape[1:]),
-        "dom",
+        DOM,
         split_axis=0,
         concat_axis=0,
         tiled=True,
@@ -159,12 +168,17 @@
     partial = jnp.einsum(
         "ktd,tq->kdq", token_blocks, grad_rows, preferred_element_type=jnp.float32
     ).astype(jnp.bfloat16)
+    chips = lax.axis_size("dh")
+    cores = lax.axis_size("dc")
+    chip_sum = pair_sum(
+        partial.reshape(chips, cores, blocks * width_in // owners, width_q)
+    )
     grad_weight = lax.psum_scatter(
-        partial.reshape(blocks * width_in, width_q),
-        "dom",
+        chip_sum.reshape(chips * blocks * width_in // owners, width_q),
+        "dh",
         scatter_dimension=0,
         tiled=True,
-    )
+    ).astype(jnp.bfloat16)
     grad_pkv = jnp.concatenate(
         [
             grad_pk.reshape(particles_here, prefix, width_kv),
@@ -177,8 +191,13 @@
     outgoing = jnp.einsum(
         "ap,pjc->ajc", onehot, grad_pkv, precision=lax.Precision.HIGHEST
     )
+    on_chip = pair_sum(outgoing.reshape((chips, cores) + outgoing.shape[1:]))
     incoming = lax.all_to_all(
-        outgoing.astype(jnp.bfloat16), "dom", split_axis=0, concat_axis=0, tiled=True
+        on_chip.astype(jnp.bfloat16),
+        "dh",
+        split_axis=0,
+        concat_axis=0,
+        tiled=True,
     )
     summed = jnp.sum(incoming.astype(jnp.float32), axis=0)
     grad_pre_keys = summed[None, :, :width_kv]
@@ -189,26 +208,29 @@
 
 
 def solution(mesh):
+    split = jax.sharding.Mesh(
+        mesh.devices.reshape(mesh.shape["dom"] // 2, 2, mesh.shape["tp"]), ("dh", "dc", "tp")
+    )
     return jax.shard_map(
         local,
-        mesh=mesh,
+        mesh=split,
         in_specs=(
-            P("dom", None, "tp"),
-            P("dom", "tp"),
-            P("dom", None, "tp"),
-            P("dom", None, "tp"),
-            P("dom", None, "tp"),
-            P("dom", None, "tp"),
-            P("dom"),
-            P("dom"),
-            P("dom", None, "tp"),
+            P(DOM, None, "tp"),
+            P(DOM, "tp"),
+            P(DOM, None, "tp"),
+            P(DOM, None, "tp"),
+            P(DOM, None, "tp"),
+            P(DOM, None, "tp"),
+            P(DOM),
+            P(DOM),
+            P(DOM, None, "tp"),
         ),
         out_specs=(
-            P("dom", "tp"),
-            P("dom", None, "tp"),
-            P("dom", None, "tp"),
-            P("dom", None, "tp"),
-            P("dom", None, "tp"),
+            P(DOM, "tp"),
+            P(DOM, None, "tp"),
+            P(DOM, None, "tp"),
+            P(DOM, None, "tp"),
+            P(DOM, None, "tp"),
         ),
         check_vma=False,
     )

time: 389 us -> 507 us (1.30)
  waiting for transfers between devices: 187 us -> 270 us
  local copies, waits for them, and re-layouts: 35.5 us -> 63.1 us
  other arithmetic: 13.4 us -> 21.4 us
    reduce_scatter x1, waiting for transfers between devices: 52.1 us -> 154 us  [local(): lax.psum_scatter(chip_sum.reshape(chips * blocks * width_in // owners, wi...]
    all_to_all x2, waiting for transfers between devices: 79.8 us -> 57.1 us  [the longest x1 57.1 us: local(): lax.all_to_all(on_chip.astype(jnp.bfloat16), 'dh', split_axis=0, concat_a...]
    dynamic_slice x0 -> x2, local copies, waits for them, and re-layouts: none -> 16.6 us  [the longest x1 12.2 us: pair_sum(): kept = lax.dynamic_index_in_dim(block, mine, axis=1, keepdims=False)]
    reshape x0 -> x1, local copies, waits for them, and re-layouts: none -> 10.6 us  [local(): on_chip = pair_sum(outgoing.reshape((chips, cores) + outgoing.shape[1:]))]
    convert_element_type x0 -> x2, other arithmetic: none -> 8.75 us  [the longest x1 7.13 us: local(): on_chip.astype(jnp.bfloat16)]
  transfers between devices with their start and end apart: 11 -> 13, of which waited for: 6 -> 6; matrix products, arithmetic and copies ran while one was open for 14% -> 18% of each run, Pallas kernels for 0% -> 0%
where the time goes in v6:
time: 507 us; the launch traced here: 506 us
  waiting for transfers between devices  270 us (53%)
  starting transfers between devices  82.2 us (16%)
  local copies, waits for them, and re-layouts  63.1 us (12%)
  matrix products  39.3 us (8%)
  between operations  29.8 us (6%)
  other arithmetic  21.4 us (4%)
    reduce_scatter x1, waiting for transfers between devices, local(): lax.psum_scatter(chip_sum.reshape(chips * blocks * width_in // owners, wi...  154 us
    all_to_all x1, waiting for transfers between devices, local(): lax.all_to_all(on_chip.astype(jnp.bfloat16), 'dh', split_axis=0, concat_a...  57.1 us
    ppermute x3, starting transfers between devices, gather_ring(): moving = lax.ppermute(moving, 'tp', backward)  55 us
    ppermute x4, waiting for transfers between devices, gather_ring(): moving = lax.ppermute(moving, 'tp', forward)  54.8 us
    dynamic_slice x1, local copies, waits for them, and re-layouts, pair_sum(): kept = lax.dynamic_index_in_dim(block, mine, axis=1, keepdims=False)  12.2 us
    all_to_all x1, starting transfers between devices, local(): lax.all_to_all(jnp.broadcast_to(own_kv, (owners,) + own_kv.shape[1:]), DO...  11.8 us
    dynamic_update_slice x8, local copies, waits for them, and re-layouts, gather_ring(): stacked = lax.dynamic_update_index_in_dim(stacked, piece, order[slot], 0)  11.7 us
    all_to_all x1, starting transfers between devices, local(): lax.all_to_all(on_chip.astype(jnp.bfloat16), 'dh', split_axis=0, concat_a...  11 us
  transfers between devices with their start and end apart: 13, of which 6 were waited for; matrix products, arithmetic and copies ran while one was open for 18% of the time, Pallas kernels for 0%

profile of v6, /device:TPU:2, one launch (start us, length us, event | category | flops | bytes accessed | tf_op | source)
XLA Modules:
  0.0 505.5 jit_solution(46123100584410435)
XLA Ops:
  11.3 11.8 %all-to-all-start = ((bf16[32,256,256]{2,1,0:T(8,128)(2,1)}), bf16[32,256,256]{2,1,0:T(8,128)(2,1)}, u32[]{:S(2)}, u32[]{:S(2)}) async-start(bf16[32,256,256]{2,1,0:T(8,128)(2,1)} %broadcast_in_dim.86), calls=%async_computation | async-start | bytes 8388608 | tf_op jit(solution)/shard_map/all_to_all | solution.py:148
  24.7 21.1 %collective-permute-done = bf16[14,64,512]{2,1,0:T(8,128)(2,1)} collective-permute-done((bf16[14,64,512]{2,1,0:T(8,128)(2,1)S(1)}, bf16[14,64,512]{2,1,0:T(8,128)(2,1)}, u32[]{:S(2)}, u32[]{:S(2)}) %collective-permute-start) | collective-permute-done | bytes 917536 | tf_op jit(solution)/shard_map/ppermute | solution.py:88
  47.2 18.1 %collective-permute-start.4 = (bf16[14,64,512]{2,1,0:T(8,128)(2,1)S(1)}, bf16[14,64,512]{2,1,0:T(8,128)(2,1)S(1)}, u32[]{:S(2)}, u32[]{:S(2)}) collective-permute-start(bf16[14,64,512]{2,1,0:T(8,128)(2,1)S(1)} %copy-done.8), channel_id=1, source_target_pairs={{2,0},{4,2},{6,4},{7,6},{5,7},{3,5},{1,3},{0,1},{10,8},{12,10},{14... | collective-permute-start | bytes 2752520 | tf_op jit(solution)/shard_map/ppermute | solution.py:92
  67.2 18.5 %collective-permute-done.1 = bf16[14,64,512]{2,1,0:T(8,128)(2,1)S(1)} collective-permute-done((bf16[14,64,512]{2,1,0:T(8,128)(2,1)}, bf16[14,64,512]{2,1,0:T(8,128)(2,1)S(1)}, u32[]{:S(2)}, u32[]{:S(2)}) %collective-permute-start.1) | collective-permute-done | bytes 917536 | tf_op jit(solution)/shard_map/ppermute | solution.py:88
  86.5 35.1 %collective-permute-start.5 = (bf16[14,64,512]{2,1,0:T(8,128)(2,1)S(1)}, bf16[14,64,512]{2,1,0:T(8,128)(2,1)}, u32[]{:S(2)}, u32[]{:S(2)}) collective-permute-start(bf16[14,64,512]{2,1,0:T(8,128)(2,1)S(1)} %collective-permute-done.4), channel_id=1, source_target_pairs={{2,0},{4,2},{6,4},{7,6},{5,7},{3,5},{1,3},{0,1},{10,8},{12,10},{14... | collective-permute-start | bytes 2752520 | tf_op jit(solution)/shard_map/ppermute | solution.py:92
  137.1 3.9 broadcast_in_dim.73
  150.3 15.2 %collective-permute-done.3 = bf16[14,64,512]{2,1,0:T(8,128)(2,1)S(1)} collective-permute-done((bf16[14,64,512]{2,1,0:T(8,128)(2,1)}, bf16[14,64,512]{2,1,0:T(8,128)(2,1)S(1)}, u32[]{:S(2)}, u32[]{:S(2)}) %collective-permute-start.3) | collective-permute-done | bytes 917536 | tf_op jit(solution)/shard_map/ppermute | solution.py:88
  170.9 8.2 %bitcast_convert_fusion = bf16[896,512]{1,0:T(8,128)(2,1)S(1)} fusion(bf16[8,896,512]{2,1,0:T(8,128)(2,1)} %bitcast.17, bf16[8,512,512]{2,1,0:T(8,128)(2,1)} %bitcast.247), kind=kOutput, calls=%fused_computation.34 | convolution fusion | flops 3758555136 | bytes 12451840 | tf_op jit(solution)/shard_map/ktd,kdq->tq/dot_general | solution.py:138
  179.3 2.9 gather_fusion.1
  186.1 2.6 fusion.1
  188.8 3.3 fusion.20
  201.4 7.8 %convolution_convert_fusion = bf16[8,512,512]{2,1,0:T(8,128)(2,1)S(1)} fusion(bf16[8,896,512]{2,1,0:T(8,128)(2,1)} %bitcast.17, bf16[896,512,1]{1,0,2:T(8,128)(2,1)} %reshape.214), kind=kOutput, calls=%fused_computation.18 | convolution fusion | flops 3760193536 | bytes 12451840 | tf_op jit(solution)/shard_map/ktd,tq->kdq/dot_general | solution.py:168
  214.1 5.4 %copy.58 = f32[14,256,256]{2,0,1:T(8,128)} copy(f32[14,256,256]{1,2,0:T(8,128)} %pad_maximum_fusion) | data formatting | bytes 7340032 | tf_op jit(solution)/shard_map/concatenate | solution.py:182
  219.5 7.5 %fusion.53 = f32[32,256,256]{2,0,1:T(8,128)} fusion(f32[14,256,256]{2,0,1:T(8,128)} %copy.58, s32[14]{0:T(128)S(1)} %copy-done.9), kind=kOutput, calls=%fused_computation.89 | convolution fusion | flops 352321984 | bytes 12058680 | tf_op jit(solution)/shard_map/ap,pjc->ajc/dot_general | solution.py:191
  227.0 10.6 %reshape.189 = f32[16,2,256,256]{3,1,0,2:T(2,128)} reshape(f32[32,256,256]{2,0,1:T(8,128)} %fusion.53) | data formatting | bytes 16777216 | tf_op jit(solution)/shard_map/reshape | solution.py:194
  237.5 12.2 %constant_dynamic-slice_fusion.1 = (f32[16,1,256,256]{3,1,0,2:T(1,128)}, f32[16,1,256,256]{3,1,0,2:T(1,128)S(1)}) fusion(f32[16,2,256,256]{3,1,0,2:T(2,128)} %reshape.189, s32[]{:T(128)S(6)} %select_n.79, s32[]{:T(128)S(6)} %select_n.80), kind=kLoop, calls=%fused_computation.94 | loop fusion | bytes 16777224 | tf_op jit(solution)/shard_map/jit(dynamic_index_in_dim)/dynamic_slice | solution.py:107
  249.7 4.4 copy.106
  254.1 4.2 convert_add_fusion
  258.4 3.2 collective-permute-done.8
  261.6 7.1 %fusion = bf16[16,256,256]{2,1,0:T(8,128)(2,1)} fusion(f32[16,256,256]{2,1,0:T(8,128)} %collective-permute-done.8, f32[16,1,256,256]{3,1,0,2:T(1,128)} %get-tuple-element.5), kind=kLoop, calls=%fused_computation.4 | loop fusion | flops 2097152 | bytes 10485760 | tf_op jit(solution)/shard_map/convert_element_type | solution.py:196
  268.7 11.0 %all-to-all-start.1 = ((bf16[16,256,256]{2,1,0:T(8,128)(2,1)}), bf16[16,256,256]{2,1,0:T(8,128)(2,1)S(1)}, u32[]{:S(2)}, u32[]{:S(2)}) async-start(bf16[16,256,256]{2,1,0:T(8,128)(2,1)} %fusion), calls=%async_computation.2 | async-start | bytes 4194304 | tf_op jit(solution)/shard_map/all_to_all | solution.py:195
  282.0 3.1 fusion.28
  285.1 57.1 %all-to-all-done.1 = bf16[16,256,256]{2,1,0:T(8,128)(2,1)S(1)} async-done(((bf16[16,256,256]{2,1,0:T(8,128)(2,1)}), bf16[16,256,256]{2,1,0:T(8,128)(2,1)S(1)}, u32[]{:S(2)}, u32[]{:S(2)}) %all-to-all-start.1) | async-done | bytes 2097184 | tf_op jit(solution)/shard_map/all_to_all | solution.py:195
  343.2 153.9 %reduce-scatter.2.cloned.1.call-done = f32[128,512]{1,0:T(8,128)} async-done(((f32[2048,512]{1,0:T(8,128)}), f32[128,512]{1,0:T(8,128)}) %reduce-scatter.2.cloned.1.call-update) | async-done | bytes 262160 | tf_op jit(solution)/shard_map/reduce_scatter | solution.py:176
  (90 shorter events, 47.6 us)
Async XLA Ops:
  7.2 176.0 %copy-start = (bf16[14,64,128]{2,1,0:T(8,128)(2,1)S(1)}, bf16[14,64,128]{2,1,0:T(8,128)(2,1)}, u32[]{:S(2)}) copy-start(bf16[14,64,128]{2,1,0:T(8,128)(2,1)} %param.13) | copy-start | bytes 688132
  7.2 163.7 %all-gather.2.cloned.1.call-start = ((), (), s32[]{:S(2)}) async-start(), calls=%async_computation.3 | async-start | bytes 4325376 | tf_op jit(solution)/shard_map/all_gather | solution.py:136
  11.2 11.8 %copy-start.8 = (bf16[14,64,512]{2,1,0:T(8,128)(2,1)S(1)}, bf16[14,64,512]{2,1,0:T(8,128)(2,1)}, u32[]{:S(2)}) copy-start(bf16[14,64,512]{2,1,0:T(8,128)(2,1)} %param.11) | copy-start | bytes 2752516
  11.2 54.0 %copy-start.14 = (s32[8]{0:T(128)S(1)}, s32[8]{0:T(128)}, u32[]{:S(2)}) copy-start(s32[8]{0:T(128)} %constant.107) | copy-start | bytes 100
  11.2 54.6 %copy-start.13 = (s32[8]{0:T(128)S(1)}, s32[8]{0:T(128)}, u32[]{:S(2)}) copy-start(s32[8]{0:T(128)} %constant.94.clone) | copy-start | bytes 100
  11.3 55.3 %copy-start.2 = (s32[8]{0:T(128)S(1)}, s32[8]{0:T(128)}, u32[]{:S(2)}) copy-start(s32[8]{0:T(128)} %constant.93.clone) | copy-start | bytes 100
  11.3 75.3 %copy-start.9 = (s32[14]{0:T(128)S(1)}, s32[14]{0:T(128)}, u32[]{:S(2)}) copy-start(s32[14]{0:T(128)} %param.17) | copy-start | bytes 172
  11.3 168.1 %all-to-all-start = ((bf16[32,256,256]{2,1,0:T(8,128)(2,1)}), bf16[32,256,256]{2,1,0:T(8,128)(2,1)}, u32[]{:S(2)}, u32[]{:S(2)}) async-start(bf16[32,256,256]{2,1,0:T(8,128)(2,1)} %broadcast_in_dim.86), calls=%async_computation | async-start | bytes 8388608 | tf_op jit(solution)/shard_map/all_to_all | solution.py:148
  23.0 474.0 %reduce-scatter.2.cloned.1.call-start = ((), (), s32[]{:S(2)}) async-start(), calls=%async_computation.4 | async-start | bytes 4456448 | tf_op jit(solution)/shard_map/reduce_scatter | solution.py:176
  23.1 22.6 %collective-permute-start = (bf16[14,64,512]{2,1,0:T(8,128)(2,1)S(1)}, bf16[14,64,512]{2,1,0:T(8,128)(2,1)}, u32[]{:S(2)}, u32[]{:S(2)}) collective-permute-start(bf16[14,64,512]{2,1,0:T(8,128)(2,1)S(1)} %copy-done.8), channel_id=1, source_target_pairs={{0,2},{2,4},{4,6},{6,7},{7,5},{5,3},{3,1},{1,0},{8,10},{10,12},{12... | collective-permute-start | bytes 2752520 | tf_op jit(solution)/shard_map/ppermute | solution.py:88
  45.7 40.0 %collective-permute-start.1 = (bf16[14,64,512]{2,1,0:T(8,128)(2,1)}, bf16[14,64,512]{2,1,0:T(8,128)(2,1)S(1)}, u32[]{:S(2)}, u32[]{:S(2)}) collective-permute-start(bf16[14,64,512]{2,1,0:T(8,128)(2,1)} %collective-permute-done), channel_id=1, source_target_pairs={{0,2},{2,4},{4,6},{6,7},{7,5},{5,3},{3,1},{1,0},{8,10},{10,12},{12... | collective-permute-start | bytes 2752520 | tf_op jit(solution)/shard_map/ppermute | solution.py:88
  47.2 39.3 %collective-permute-start.4 = (bf16[14,64,512]{2,1,0:T(8,128)(2,1)S(1)}, bf16[14,64,512]{2,1,0:T(8,128)(2,1)S(1)}, u32[]{:S(2)}, u32[]{:S(2)}) collective-permute-start(bf16[14,64,512]{2,1,0:T(8,128)(2,1)S(1)} %copy-done.8), channel_id=1, source_target_pairs={{2,0},{4,2},{6,4},{7,6},{5,7},{3,5},{1,3},{0,1},{10,8},{12,10},{14... | collective-permute-start | bytes 2752520 | tf_op jit(solution)/shard_map/ppermute | solution.py:92
  85.7 56.3 %collective-permute-start.2 = (bf16[14,64,512]{2,1,0:T(8,128)(2,1)S(1)}, bf16[14,64,512]{2,1,0:T(8,128)(2,1)}, u32[]{:S(2)}, u32[]{:S(2)}) collective-permute-start(bf16[14,64,512]{2,1,0:T(8,128)(2,1)S(1)} %collective-permute-done.1), channel_id=1, source_target_pairs={{0,2},{2,4},{4,6},{6,7},{7,5},{5,3},{3,1},{1,0},{8,10},{10,12},{12... | collective-permute-start | bytes 2752520 | tf_op jit(solution)/shard_map/ppermute | solution.py:88
  86.5 58.8 %collective-permute-start.5 = (bf16[14,64,512]{2,1,0:T(8,128)(2,1)S(1)}, bf16[14,64,512]{2,1,0:T(8,128)(2,1)}, u32[]{:S(2)}, u32[]{:S(2)}) collective-permute-start(bf16[14,64,512]{2,1,0:T(8,128)(2,1)S(1)} %collective-permute-done.4), channel_id=1, source_target_pairs={{2,0},{4,2},{6,4},{7,6},{5,7},{3,5},{1,3},{0,1},{10,8},{12,10},{14... | collective-permute-start | bytes 2752520 | tf_op jit(solution)/shard_map/ppermute | solution.py:92
  142.0 23.6 %collective-permute-start.3 = (bf16[14,64,512]{2,1,0:T(8,128)(2,1)}, bf16[14,64,512]{2,1,0:T(8,128)(2,1)S(1)}, u32[]{:S(2)}, u32[]{:S(2)}) collective-permute-start(bf16[14,64,512]{2,1,0:T(8,128)(2,1)} %collective-permute-done.2), channel_id=1, source_target_pairs={{0,2},{2,4},{4,6},{6,7},{7,5},{5,3},{3,1},{1,0},{8,10},{10,12},{12... | collective-permute-start | bytes 2752520 | tf_op jit(solution)/shard_map/ppermute | solution.py:88
  145.3 24.5 %collective-permute-start.6 = (bf16[14,64,512]{2,1,0:T(8,128)(2,1)}, bf16[14,64,512]{2,1,0:T(8,128)(2,1)S(1)}, u32[]{:S(2)}, u32[]{:S(2)}) collective-permute-start(bf16[14,64,512]{2,1,0:T(8,128)(2,1)} %collective-permute-done.5), channel_id=1, source_target_pairs={{2,0},{4,2},{6,4},{7,6},{5,7},{3,5},{1,3},{0,1},{10,8},{12,10},{14... | collective-permute-start | bytes 2752520 | tf_op jit(solution)/shard_map/ppermute | solution.py:92
  184.2 9.0 %copy-start.3 = (f32[14,1,4,64,64]{3,4,2,0,1:T(8,128)}, f32[14,1,4,64,64]{3,4,2,0,1:T(8,128)S(1)}, u32[]{:S(2)}) copy-start(f32[14,1,4,64,64]{3,4,2,0,1:T(8,128)S(1)} %get-tuple-element.20) | copy-start | bytes 2752516
  188.8 3.3 copy-start.11
  209.2 2.8 copy-start.7
  210.8 43.3 %collective-permute-start.7 = (bf16[16,128,512]{2,1,0:T(8,128)(2,1)}, bf16[16,128,512]{2,1,0:T(8,128)(2,1)}, u32[]{:S(2)}, u32[]{:S(2)}) collective-permute-start(bf16[16,128,512]{2,1,0:T(8,128)(2,1)} %dynamic-slice_bitcast_fusion), channel_id=1, source_target_pairs={{0,8},{8,0},{1,9},{9,1},{2,10},{10,2},{3,11},{11,3},{4,12},{12,4},... | collective-permute-start | bytes 6291464 | tf_op jit(solution)/shard_map/ppermute | solution.py:109
  249.7 4.4 copy-start.5
  254.1 7.5 %collective-permute-start.8 = (f32[16,256,256]{2,1,0:T(8,128)}, f32[16,256,256]{2,1,0:T(8,128)}, u32[]{:S(2)}, u32[]{:S(2)}) collective-permute-start(f32[16,256,256]{2,1,0:T(8,128)} %bitcast.243), channel_id=1, source_target_pairs={{0,8},{8,0},{1,9},{9,1},{2,10},{10,2},{3,11},{11,3},{4,12},{12,4},... | collective-permute-start | bytes 12582920 | tf_op jit(solution)/shard_map/ppermute | solution.py:109
  268.7 73.4 %all-to-all-start.1 = ((bf16[16,256,256]{2,1,0:T(8,128)(2,1)}), bf16[16,256,256]{2,1,0:T(8,128)(2,1)S(1)}, u32[]{:S(2)}, u32[]{:S(2)}) async-start(bf16[16,256,256]{2,1,0:T(8,128)(2,1)} %fusion), calls=%async_computation.2 | async-start | bytes 4194304 | tf_op jit(solution)/shard_map/all_to_all | solution.py:195
  282.0 216.7 %copy-start.1 = (bf16[14,64,128]{2,1,0:T(8,128)(2,1)S(1)}, bf16[14,64,128]{2,1,0:T(8,128)(2,1)}, u32[]{:S(2)}) copy-start(bf16[14,64,128]{2,1,0:T(8,128)(2,1)} %param.13) | copy-start | bytes 688132
  (4 other events, 7.4 us)
Sparse Core Ops, SparseCore 0:
  10.8 122.1 all-gather.1
  258.5 238.5 reduce-scatter.1

commit v7 on v6

--- a/solution.py
+++ b/solution.py
@@ -144,15 +144,23 @@
     queries = queries.reshape(particles_here, length, width_q)
     scaled = (out_grad.astype(jnp.float32) * twist_weights[:, None, None]).astype(jnp.bfloat16)
 
+    chips = lax.axis_size("dh")
+    cores = lax.axis_size("dc")
     own_kv = jnp.concatenate([prefix_keys, prefix_values], axis=2)
-    every_kv = lax.all_to_all(
-        jnp.broadcast_to(own_kv, (owners,) + own_kv.shape[1:]),
-        DOM,
+    half_kv = lax.all_to_all(
+        jnp.broadcast_to(own_kv, (chips,) + own_kv.shape[1:]),
+        "dh",
         split_axis=0,
         concat_axis=0,
         tiled=True,
     )
-    picked = jnp.take(every_kv, ancestors, axis=0)
+    other_kv = lax.ppermute(half_kv, "dc", [(0, 1), (1, 0)])
+    on_this_core = (ancestors % cores == lax.axis_index("dc"))[:, None, None]
+    picked = jnp.where(
+        on_this_core,
+        jnp.take(half_kv, ancestors // cores, axis=0),
+        jnp.take(other_kv, ancestors // cores, axis=0),
+    )
     pre_keys = picked[:, :, :width_kv]
     pre_values = picked[:, :, width_kv:]
 
@@ -168,17 +176,12 @@
     partial = jnp.einsum(
         "ktd,tq->kdq", token_blocks, grad_rows, preferred_element_type=jnp.float32
     ).astype(jnp.bfloat16)
-    chips = lax.axis_size("dh")
-    cores = lax.axis_size("dc")
-    chip_sum = pair_sum(
-        partial.reshape(chips, cores, blocks * width_in // owners, width_q)
-    )
     grad_weight = lax.psum_scatter(
-        chip_sum.reshape(chips * blocks * width_in // owners, width_q),
-        "dh",
+        partial.reshape(blocks * width_in, width_q),
+        DOM,
         scatter_dimension=0,
         tiled=True,
-    ).astype(jnp.bfloat16)
+    )
     grad_pkv = jnp.concatenate(
         [
             grad_pk.reshape(particles_here, prefix, width_kv),

time: 507 us -> 388 us (0.77)
  waiting for transfers between devices: 270 us -> 171 us
  starting transfers between devices: 82.2 us -> 60.5 us
    reduce_scatter x1, waiting for transfers between devices: 154 us -> 63.9 us  [local(): lax.psum_scatter(partial.reshape(blocks * width_in, width_q), DOM, scatte...]
    ppermute x3, starting transfers between devices: 55 us -> 32.7 us  [gather_ring(): moving = lax.ppermute(moving, 'tp', backward)]
    ppermute x3, waiting for transfers between devices: 0.01 us -> 14.6 us  [gather_ring(): moving = lax.ppermute(moving, 'tp', backward)]
    ppermute x4, waiting for transfers between devices: 54.8 us -> 43.2 us  [gather_ring(): moving = lax.ppermute(moving, 'tp', forward)]
    all_to_all x1, waiting for transfers between devices: 57.1 us -> 48.8 us  [local(): lax.all_to_all(on_chip.astype(jnp.bfloat16), 'dh', split_axis=0, concat_a...]
  transfers between devices with their start and end apart: 13 -> 13, of which waited for: 6 -> 7; matrix products, arithmetic and copies ran while one was open for 18% -> 14% of each run, Pallas kernels for 0% -> 0%
where the time goes in v7:
time: 388 us; the launch traced here: 387 us
  waiting for transfers between devices  171 us (44%)
  local copies, waits for them, and re-layouts  65.2 us (17%)
  starting transfers between devices  60.5 us (16%)
  matrix products  42.8 us (11%)
  between operations  29.8 us (8%)
  other arithmetic  17.6 us (5%)
    reduce_scatter x1, waiting for transfers between devices, local(): lax.psum_scatter(partial.reshape(blocks * width_in, width_q), DOM, scatte...  63.9 us
    all_to_all x1, waiting for transfers between devices, local(): lax.all_to_all(on_chip.astype(jnp.bfloat16), 'dh', split_axis=0, concat_a...  48.8 us
    ppermute x4, waiting for transfers between devices, gather_ring(): moving = lax.ppermute(moving, 'tp', forward)  43.2 us
    ppermute x3, starting transfers between devices, gather_ring(): moving = lax.ppermute(moving, 'tp', backward)  32.7 us
    ppermute x3, waiting for transfers between devices, gather_ring(): moving = lax.ppermute(moving, 'tp', backward)  14.6 us
    dynamic_update_slice x8, local copies, waits for them, and re-layouts, gather_ring(): stacked = lax.dynamic_update_index_in_dim(stacked, piece, order[slot], 0)  14 us
    dynamic_slice x1, local copies, waits for them, and re-layouts, pair_sum(): kept = lax.dynamic_index_in_dim(block, mine, axis=1, keepdims=False)  12.3 us
    all_to_all x1, starting transfers between devices, local(): lax.all_to_all(jnp.broadcast_to(own_kv, (chips,) + own_kv.shape[1:]), 'dh...  11.3 us
  transfers between devices with their start and end apart: 13, of which 7 were waited for; matrix products, arithmetic and copies ran while one was open for 14% of the time, Pallas kernels for 0%

profile of v7, /device:TPU:2, one launch (start us, length us, event | category | flops | bytes accessed | tf_op | source)
XLA Modules:
  0.0 387.2 jit_solution(9941151199643536396)
XLA Ops:
  10.4 11.3 %all-to-all-start = ((bf16[16,256,256]{2,1,0:T(8,128)(2,1)}), bf16[16,256,256]{2,1,0:T(8,128)(2,1)S(1)}, u32[]{:S(2)}, u32[]{:S(2)}) async-start(bf16[16,256,256]{2,1,0:T(8,128)(2,1)} %broadcast_in_dim.92), calls=%async_computation | async-start | bytes 4194304 | tf_op jit(solution)/shard_map/all_to_all | solution.py:150
  23.4 20.4 %collective-permute-done = bf16[14,64,512]{2,1,0:T(8,128)(2,1)} collective-permute-done((bf16[14,64,512]{2,1,0:T(8,128)(2,1)S(1)}, bf16[14,64,512]{2,1,0:T(8,128)(2,1)}, u32[]{:S(2)}, u32[]{:S(2)}) %collective-permute-start) | collective-permute-done | bytes 917536 | tf_op jit(solution)/shard_map/ppermute | solution.py:88
  45.3 18.7 %collective-permute-start.4 = (bf16[14,64,512]{2,1,0:T(8,128)(2,1)S(1)}, bf16[14,64,512]{2,1,0:T(8,128)(2,1)}, u32[]{:S(2)}, u32[]{:S(2)}) collective-permute-start(bf16[14,64,512]{2,1,0:T(8,128)(2,1)S(1)} %copy-done.9), channel_id=1, source_target_pairs={{2,0},{4,2},{6,4},{7,6},{5,7},{3,5},{1,3},{0,1},{10,8},{12,10},{14... | collective-permute-start | bytes 2752520 | tf_op jit(solution)/shard_map/ppermute | solution.py:92
  64.6 19.0 %collective-permute-done.1 = bf16[14,64,512]{2,1,0:T(8,128)(2,1)} collective-permute-done((bf16[14,64,512]{2,1,0:T(8,128)(2,1)}, bf16[14,64,512]{2,1,0:T(8,128)(2,1)}, u32[]{:S(2)}, u32[]{:S(2)}) %collective-permute-start.1) | collective-permute-done | bytes 917536 | tf_op jit(solution)/shard_map/ppermute | solution.py:88
  101.0 13.7 %collective-permute-start.5 = (bf16[14,64,512]{2,1,0:T(8,128)(2,1)}, bf16[14,64,512]{2,1,0:T(8,128)(2,1)}, u32[]{:S(2)}, u32[]{:S(2)}) collective-permute-start(bf16[14,64,512]{2,1,0:T(8,128)(2,1)} %collective-permute-done.4), channel_id=1, source_target_pairs={{2,0},{4,2},{6,4},{7,6},{5,7},{3,5},{1,3},{0,1},{10,8},{12,10},{14... | collective-permute-start | bytes 2752520 | tf_op jit(solution)/shard_map/ppermute | solution.py:92
  114.7 3.9 broadcast_in_dim.79
  123.9 10.6 %collective-permute-done.5 = bf16[14,64,512]{2,1,0:T(8,128)(2,1)} collective-permute-done((bf16[14,64,512]{2,1,0:T(8,128)(2,1)}, bf16[14,64,512]{2,1,0:T(8,128)(2,1)}, u32[]{:S(2)}, u32[]{:S(2)}) %collective-permute-start.5) | collective-permute-done | bytes 917536 | tf_op jit(solution)/shard_map/ppermute | solution.py:92
  139.2 3.8 collective-permute-done.3
  148.4 4.0 %collective-permute-done.6 = bf16[14,64,512]{2,1,0:T(8,128)(2,1)S(1)} collective-permute-done((bf16[14,64,512]{2,1,0:T(8,128)(2,1)}, bf16[14,64,512]{2,1,0:T(8,128)(2,1)S(1)}, u32[]{:S(2)}, u32[]{:S(2)}) %collective-permute-start.6) | collective-permute-done | bytes 917536 | tf_op jit(solution)/shard_map/ppermute | solution.py:92
  155.4 3.5 gather_fusion.2
  161.4 9.8 %bitcast_convert_fusion = bf16[896,512]{1,0:T(8,128)(2,1)} fusion(bf16[8,896,512]{2,1,0:T(8,128)(2,1)} %bitcast.17, bf16[8,512,512]{2,1,0:T(8,128)(2,1)} %bitcast.239), kind=kOutput, calls=%fused_computation.33 | convolution fusion | flops 3758555136 | bytes 12451840 | tf_op jit(solution)/shard_map/ktd,kdq->tq/dot_general | solution.py:138
  176.7 2.6 fusion.1
  179.3 2.9 fusion.20
  189.1 5.4 %copy.58 = f32[14,256,256]{2,0,1:T(8,128)} copy(f32[14,256,256]{1,2,0:T(8,128)} %pad_maximum_fusion) | data formatting | bytes 7340032 | tf_op jit(solution)/shard_map/concatenate | solution.py:185
  194.5 7.5 %fusion.53 = f32[32,256,256]{2,0,1:T(8,128)} fusion(f32[14,256,256]{2,0,1:T(8,128)} %copy.58, s32[14]{0:T(128)S(1)} %copy-done.10), kind=kOutput, calls=%fused_computation.88 | convolution fusion | flops 352321984 | bytes 12058680 | tf_op jit(solution)/shard_map/ap,pjc->ajc/dot_general | solution.py:194
  201.9 10.6 %reshape.184 = f32[16,2,256,256]{3,1,0,2:T(2,128)} reshape(f32[32,256,256]{2,0,1:T(8,128)} %fusion.53) | data formatting | bytes 16777216 | tf_op jit(solution)/shard_map/reshape | solution.py:197
  212.5 12.3 %constant_dynamic-slice_fusion.1 = (f32[16,1,256,256]{3,1,0,2:T(1,128)}, f32[16,1,256,256]{3,1,0,2:T(1,128)S(1)}) fusion(f32[16,2,256,256]{3,1,0,2:T(2,128)} %reshape.184, s32[]{:T(128)S(6)} %select_n.90, s32[]{:T(128)S(6)} %select_n.91), kind=kLoop, calls=%fused_computation.95 | loop fusion | bytes 16777224 | tf_op jit(solution)/shard_map/jit(dynamic_index_in_dim)/dynamic_slice | solution.py:107
  224.8 4.4 %copy.106 = f32[16,1,256,256]{3,2,0,1:T(8,128)} copy(f32[16,1,256,256]{3,1,0,2:T(1,128)S(1)} %get-tuple-element.9) | data formatting | bytes 8388608 | tf_op jit(solution)/shard_map/jit(dynamic_index_in_dim)/dynamic_slice | solution.py:108
  233.9 9.3 %convolution_convert_fusion = bf16[8,512,512]{2,1,0:T(8,128)(2,1)} fusion(bf16[8,896,512]{2,1,0:T(8,128)(2,1)} %bitcast.17, bf16[896,512,1]{1,0,2:T(8,128)(2,1)S(1)} %reshape.221), kind=kOutput, calls=%fused_computation.18 | convolution fusion | flops 3760193536 | bytes 12451840 | tf_op jit(solution)/shard_map/ktd,tq->kdq/dot_general | solution.py:176
  243.3 7.1 %fusion = bf16[16,256,256]{2,1,0:T(8,128)(2,1)} fusion(f32[16,256,256]{2,1,0:T(8,128)} %collective-permute-done.8, f32[16,1,256,256]{3,1,0,2:T(1,128)} %get-tuple-element.8), kind=kLoop, calls=%fused_computation.4 | loop fusion | flops 2097152 | bytes 10485760 | tf_op jit(solution)/shard_map/convert_element_type | solution.py:199
  250.4 11.2 %all-to-all-start.1 = ((bf16[16,256,256]{2,1,0:T(8,128)(2,1)}), bf16[16,256,256]{2,1,0:T(8,128)(2,1)S(1)}, u32[]{:S(2)}, u32[]{:S(2)}) async-start(bf16[16,256,256]{2,1,0:T(8,128)(2,1)} %fusion), calls=%async_computation.2 | async-start | bytes 4194304 | tf_op jit(solution)/shard_map/all_to_all | solution.py:198
  264.1 2.5 fusion.28
  266.6 48.8 %all-to-all-done.1 = bf16[16,256,256]{2,1,0:T(8,128)(2,1)S(1)} async-done(((bf16[16,256,256]{2,1,0:T(8,128)(2,1)}), bf16[16,256,256]{2,1,0:T(8,128)(2,1)S(1)}, u32[]{:S(2)}, u32[]{:S(2)}) %all-to-all-start.1) | async-done | bytes 2097184 | tf_op jit(solution)/shard_map/all_to_all | solution.py:198
  316.4 63.9 %reduce-scatter.2.cloned.1.call-done = bf16[128,512]{1,0:T(8,128)(2,1)} async-done(((bf16[4096,512]{1,0:T(8,128)(2,1)}), bf16[128,512]{1,0:T(8,128)(2,1)}) %reduce-scatter.2.cloned.1.call-update) | async-done | bytes 131088 | tf_op jit(solution)/shard_map/reduce_scatter | solution.py:179
  (89 shorter events, 50.2 us)
Async XLA Ops:
  7.2 166.6 %copy-start = (bf16[14,64,128]{2,1,0:T(8,128)(2,1)S(1)}, bf16[14,64,128]{2,1,0:T(8,128)(2,1)}, u32[]{:S(2)}) copy-start(bf16[14,64,128]{2,1,0:T(8,128)(2,1)} %param.15) | copy-start | bytes 688132
  7.2 154.2 %all-gather.2.cloned.1.call-start = ((), (), s32[]{:S(2)}) async-start(), calls=%async_computation.3 | async-start | bytes 4325376 | tf_op jit(solution)/shard_map/all_gather | solution.py:136
  10.4 11.4 %copy-start.9 = (bf16[14,64,512]{2,1,0:T(8,128)(2,1)S(1)}, bf16[14,64,512]{2,1,0:T(8,128)(2,1)}, u32[]{:S(2)}) copy-start(bf16[14,64,512]{2,1,0:T(8,128)(2,1)} %param.13) | copy-start | bytes 2752516
  10.4 53.6 %copy-start.15 = (s32[8]{0:T(128)S(1)}, s32[8]{0:T(128)}, u32[]{:S(2)}) copy-start(s32[8]{0:T(128)} %constant.121) | copy-start | bytes 100
  10.4 73.2 %copy-start.14 = (s32[8]{0:T(128)S(1)}, s32[8]{0:T(128)}, u32[]{:S(2)}) copy-start(s32[8]{0:T(128)} %constant.108.clone) | copy-start | bytes 100
  10.4 73.8 %copy-start.1 = (s32[8]{0:T(128)S(1)}, s32[8]{0:T(128)}, u32[]{:S(2)}) copy-start(s32[8]{0:T(128)} %constant.107.clone) | copy-start | bytes 100
  10.4 104.3 %copy-start.10 = (s32[14]{0:T(128)S(1)}, s32[14]{0:T(128)}, u32[]{:S(2)}) copy-start(s32[14]{0:T(128)} %param.19) | copy-start | bytes 172
  10.4 109.2 %all-to-all-start = ((bf16[16,256,256]{2,1,0:T(8,128)(2,1)}), bf16[16,256,256]{2,1,0:T(8,128)(2,1)S(1)}, u32[]{:S(2)}, u32[]{:S(2)}) async-start(bf16[16,256,256]{2,1,0:T(8,128)(2,1)} %broadcast_in_dim.92), calls=%async_computation | async-start | bytes 4194304 | tf_op jit(solution)/shard_map/all_to_all | solution.py:150
  21.7 358.6 %reduce-scatter.2.cloned.1.call-start = ((), (), s32[]{:S(2)}) async-start(), calls=%async_computation.4 | async-start | bytes 4325376 | tf_op jit(solution)/shard_map/reduce_scatter | solution.py:179
  21.8 22.0 %collective-permute-start = (bf16[14,64,512]{2,1,0:T(8,128)(2,1)S(1)}, bf16[14,64,512]{2,1,0:T(8,128)(2,1)}, u32[]{:S(2)}, u32[]{:S(2)}) collective-permute-start(bf16[14,64,512]{2,1,0:T(8,128)(2,1)S(1)} %copy-done.9), channel_id=1, source_target_pairs={{0,2},{2,4},{4,6},{6,7},{7,5},{5,3},{3,1},{1,0},{8,10},{10,12},{12... | collective-permute-start | bytes 2752520 | tf_op jit(solution)/shard_map/ppermute | solution.py:88
  43.8 39.7 %collective-permute-start.1 = (bf16[14,64,512]{2,1,0:T(8,128)(2,1)}, bf16[14,64,512]{2,1,0:T(8,128)(2,1)}, u32[]{:S(2)}, u32[]{:S(2)}) collective-permute-start(bf16[14,64,512]{2,1,0:T(8,128)(2,1)} %collective-permute-done), channel_id=1, source_target_pairs={{0,2},{2,4},{4,6},{6,7},{7,5},{5,3},{3,1},{1,0},{8,10},{10,12},{12... | collective-permute-start | bytes 2752520 | tf_op jit(solution)/shard_map/ppermute | solution.py:88
  45.3 55.7 %collective-permute-start.4 = (bf16[14,64,512]{2,1,0:T(8,128)(2,1)S(1)}, bf16[14,64,512]{2,1,0:T(8,128)(2,1)}, u32[]{:S(2)}, u32[]{:S(2)}) collective-permute-start(bf16[14,64,512]{2,1,0:T(8,128)(2,1)S(1)} %copy-done.9), channel_id=1, source_target_pairs={{2,0},{4,2},{6,4},{7,6},{5,7},{3,5},{1,3},{0,1},{10,8},{12,10},{14... | collective-permute-start | bytes 2752520 | tf_op jit(solution)/shard_map/ppermute | solution.py:92
  83.5 36.1 %collective-permute-start.2 = (bf16[14,64,512]{2,1,0:T(8,128)(2,1)}, bf16[14,64,512]{2,1,0:T(8,128)(2,1)}, u32[]{:S(2)}, u32[]{:S(2)}) collective-permute-start(bf16[14,64,512]{2,1,0:T(8,128)(2,1)} %collective-permute-done.1), channel_id=1, source_target_pairs={{0,2},{2,4},{4,6},{6,7},{7,5},{5,3},{3,1},{1,0},{8,10},{10,12},{12... | collective-permute-start | bytes 2752520 | tf_op jit(solution)/shard_map/ppermute | solution.py:88
  101.0 33.5 %collective-permute-start.5 = (bf16[14,64,512]{2,1,0:T(8,128)(2,1)}, bf16[14,64,512]{2,1,0:T(8,128)(2,1)}, u32[]{:S(2)}, u32[]{:S(2)}) collective-permute-start(bf16[14,64,512]{2,1,0:T(8,128)(2,1)} %collective-permute-done.4), channel_id=1, source_target_pairs={{2,0},{4,2},{6,4},{7,6},{5,7},{3,5},{1,3},{0,1},{10,8},{12,10},{14... | collective-permute-start | bytes 2752520 | tf_op jit(solution)/shard_map/ppermute | solution.py:92
  119.6 35.8 %collective-permute-start.7 = (bf16[16,256,256]{2,1,0:T(8,128)(2,1)S(1)}, bf16[16,256,256]{2,1,0:T(8,128)(2,1)}, u32[]{:S(2)}, u32[]{:S(2)}) collective-permute-start(bf16[16,256,256]{2,1,0:T(8,128)(2,1)S(1)} %all-to-all-done), channel_id=1, source_target_pairs={{0,8},{8,0},{1,9},{9,1},{2,10},{10,2},{3,11},{11,3},{4,12},{12,4},... | collective-permute-start | bytes 6291464 | tf_op jit(solution)/shard_map/ppermute | solution.py:157
  119.6 23.3 %collective-permute-start.3 = (bf16[14,64,512]{2,1,0:T(8,128)(2,1)}, bf16[14,64,512]{2,1,0:T(8,128)(2,1)S(1)}, u32[]{:S(2)}, u32[]{:S(2)}) collective-permute-start(bf16[14,64,512]{2,1,0:T(8,128)(2,1)} %collective-permute-done.2), channel_id=1, source_target_pairs={{0,2},{2,4},{4,6},{6,7},{7,5},{5,3},{3,1},{1,0},{8,10},{10,12},{12... | collective-permute-start | bytes 2752520 | tf_op jit(solution)/shard_map/ppermute | solution.py:88
  134.5 17.9 %collective-permute-start.6 = (bf16[14,64,512]{2,1,0:T(8,128)(2,1)}, bf16[14,64,512]{2,1,0:T(8,128)(2,1)S(1)}, u32[]{:S(2)}, u32[]{:S(2)}) collective-permute-start(bf16[14,64,512]{2,1,0:T(8,128)(2,1)} %collective-permute-done.5), channel_id=1, source_target_pairs={{2,0},{4,2},{6,4},{7,6},{5,7},{3,5},{1,3},{0,1},{10,8},{12,10},{14... | collective-permute-start | bytes 2752520 | tf_op jit(solution)/shard_map/ppermute | solution.py:92
  161.3 15.2 %copy-start.5 = (bf16[14,256,256]{2,1,0:T(8,128)(2,1)}, bf16[14,256,256]{2,1,0:T(8,128)(2,1)S(1)}, u32[]{:S(2)}) copy-start(bf16[14,256,256]{2,1,0:T(8,128)(2,1)S(1)} %select_select_fusion) | copy-start | bytes 5505028
  174.8 7.4 %copy-start.2 = (f32[14,1,4,64,64]{3,4,2,0,1:T(8,128)}, f32[14,1,4,64,64]{3,4,2,0,1:T(8,128)S(1)}, u32[]{:S(2)}) copy-start(f32[14,1,4,64,64]{3,4,2,0,1:T(8,128)S(1)} %get-tuple-element.24) | copy-start | bytes 2752516
  179.3 2.9 copy-start.12
  224.8 4.4 %copy-start.3 = (f32[14,1,4,64,64]{3,4,2,0,1:T(8,128)S(1)}, f32[14,1,4,64,64]{3,4,2,0,1:T(8,128)}, u32[]{:S(2)}) copy-start(f32[14,1,4,64,64]{3,4,2,0,1:T(8,128)} %copy-done.2) | copy-start | bytes 2752516
  224.8 4.4 %copy-start.8 = (f32[14,64,4,64]{1,3,2,0:T(8,128)S(1)}, f32[14,64,4,64]{1,3,2,0:T(8,128)}, u32[]{:S(2)}) copy-start(f32[14,64,4,64]{1,3,2,0:T(8,128)} %get-tuple-element.28) | copy-start | bytes 2752516
  229.1 14.1 %collective-permute-start.8 = (f32[16,256,256]{2,1,0:T(8,128)}, f32[16,256,256]{2,1,0:T(8,128)}, u32[]{:S(2)}, u32[]{:S(2)}) collective-permute-start(f32[16,256,256]{2,1,0:T(8,128)} %bitcast.237), channel_id=1, source_target_pairs={{0,8},{8,0},{1,9},{9,1},{2,10},{10,2},{3,11},{11,3},{4,12},{12,4},... | collective-permute-start | bytes 12582920 | tf_op jit(solution)/shard_map/ppermute | solution.py:109
  250.4 65.0 %all-to-all-start.1 = ((bf16[16,256,256]{2,1,0:T(8,128)(2,1)}), bf16[16,256,256]{2,1,0:T(8,128)(2,1)S(1)}, u32[]{:S(2)}, u32[]{:S(2)}) async-start(bf16[16,256,256]{2,1,0:T(8,128)(2,1)} %fusion), calls=%async_computation.2 | async-start | bytes 4194304 | tf_op jit(solution)/shard_map/all_to_all | solution.py:198
  (5 other events, 8.5 us)
Sparse Core Ops, SparseCore 0:
  10.8 104.4 all-gather.1
  243.4 136.9 reduce-scatter.1

commit v8 on v7

--- a/solution.py
+++ b/solution.py
@@ -104,8 +104,8 @@
 
 def pair_sum(block):
     mine = lax.axis_index("dc")
-    kept = lax.dynamic_index_in_dim(block, mine, axis=1, keepdims=False)
-    sent = lax.dynamic_index_in_dim(block, 1 - mine, axis=1, keepdims=False)
+    kept = lax.dynamic_index_in_dim(block, mine, axis=0, keepdims=False)
+    sent = lax.dynamic_index_in_dim(block, 1 - mine, axis=0, keepdims=False)
     other = lax.ppermute(sent, "dc", [(0, 1), (1, 0)])
     return kept.astype(jnp.float32) + other.astype(jnp.float32)
 
@@ -189,12 +189,12 @@
         ],
         axis=2,
     )
-    owner_ids = jnp.arange(owners, dtype=jnp.int32)
-    onehot = (owner_ids[:, None] == ancestors[None, :]).astype(jnp.float32)
+    core_major = jnp.arange(owners, dtype=jnp.int32).reshape(chips, cores).T.reshape(owners)
+    onehot = (core_major[:, None] == ancestors[None, :]).astype(jnp.float32)
     outgoing = jnp.einsum(
         "ap,pjc->ajc", onehot, grad_pkv, precision=lax.Precision.HIGHEST
     )
-    on_chip = pair_sum(outgoing.reshape((chips, cores) + outgoing.shape[1:]))
+    on_chip = pair_sum(outgoing.astype(jnp.bfloat16).reshape((cores, chips) + outgoing.shape[1:]))
     incoming = lax.all_to_all(
         on_chip.astype(jnp.bfloat16),
         "dh",

time: 388 us -> 363 us (0.936)
  local copies, waits for them, and re-layouts: 65.2 us -> 42.7 us
    dynamic_slice x2, local copies, waits for them, and re-layouts: 16.6 us -> 2.61 us  [the longest x1 2.09 us: pair_sum(): sent = lax.dynamic_index_in_dim(block, 1 - mine, axis=0, keepdims=False)]
    reshape x1, local copies, waits for them, and re-layouts: 10.6 us -> 0.08 us  [local(): jnp.arange(owners, dtype=jnp.int32).reshape(chips, cores).T.reshape(owners)]
where the time goes in v8:
time: 363 us; the launch traced here: 362 us
  waiting for transfers between devices  172 us (47%)
  starting transfers between devices  60.8 us (17%)
  local copies, waits for them, and re-layouts  42.7 us (12%)
  matrix products  40.2 us (11%)
  between operations  29.9 us (8%)
  other arithmetic  15.9 us (4%)
    reduce_scatter x1, waiting for transfers between devices, local(): lax.psum_scatter(partial.reshape(blocks * width_in, width_q), DOM, scatte...  66.4 us
    all_to_all x1, waiting for transfers between devices, local(): lax.all_to_all(on_chip.astype(jnp.bfloat16), 'dh', split_axis=0, concat_a...  48.6 us
    ppermute x4, waiting for transfers between devices, gather_ring(): moving = lax.ppermute(moving, 'tp', forward)  42 us
    ppermute x3, starting transfers between devices, gather_ring(): moving = lax.ppermute(moving, 'tp', backward)  32.8 us
    ppermute x3, waiting for transfers between devices, gather_ring(): moving = lax.ppermute(moving, 'tp', backward)  14.5 us
    dynamic_update_slice x8, local copies, waits for them, and re-layouts, gather_ring(): stacked = lax.dynamic_update_index_in_dim(stacked, piece, order[slot], 0)  14 us
    all_to_all x1, starting transfers between devices, local(): lax.all_to_all(jnp.broadcast_to(own_kv, (chips,) + own_kv.shape[1:]), 'dh...  11.3 us
    all_to_all x1, starting transfers between devices, local(): lax.all_to_all(on_chip.astype(jnp.bfloat16), 'dh', split_axis=0, concat_a...  11.3 us
  transfers between devices with their start and end apart: 13, of which 7 were waited for; matrix products, arithmetic and copies ran while one was open for 14% of the time, Pallas kernels for 0%

profile of v8, /device:TPU:2, one launch (start us, length us, event | category | flops | bytes accessed | tf_op | source)
XLA Modules:
  0.0 361.8 jit_solution(10515564579800302928)
XLA Ops:
  10.4 11.3 %all-to-all-start = ((bf16[16,256,256]{2,1,0:T(8,128)(2,1)}), bf16[16,256,256]{2,1,0:T(8,128)(2,1)S(1)}, u32[]{:S(2)}, u32[]{:S(2)}) async-start(bf16[16,256,256]{2,1,0:T(8,128)(2,1)} %broadcast_in_dim.91), calls=%async_computation | async-start | bytes 4194304 | tf_op jit(solution)/shard_map/all_to_all | solution.py:150
  23.3 20.4 %collective-permute-done = bf16[14,64,512]{2,1,0:T(8,128)(2,1)} collective-permute-done((bf16[14,64,512]{2,1,0:T(8,128)(2,1)S(1)}, bf16[14,64,512]{2,1,0:T(8,128)(2,1)}, u32[]{:S(2)}, u32[]{:S(2)}) %collective-permute-start) | collective-permute-done | bytes 917536 | tf_op jit(solution)/shard_map/ppermute | solution.py:88
  45.3 18.7 %collective-permute-start.4 = (bf16[14,64,512]{2,1,0:T(8,128)(2,1)S(1)}, bf16[14,64,512]{2,1,0:T(8,128)(2,1)}, u32[]{:S(2)}, u32[]{:S(2)}) collective-permute-start(bf16[14,64,512]{2,1,0:T(8,128)(2,1)S(1)} %copy-done.9), channel_id=1, source_target_pairs={{2,0},{4,2},{6,4},{7,6},{5,7},{3,5},{1,3},{0,1},{10,8},{12,10},{14... | collective-permute-start | bytes 2752520 | tf_op jit(solution)/shard_map/ppermute | solution.py:92
  65.2 18.3 %collective-permute-done.1 = bf16[14,64,512]{2,1,0:T(8,128)(2,1)} collective-permute-done((bf16[14,64,512]{2,1,0:T(8,128)(2,1)}, bf16[14,64,512]{2,1,0:T(8,128)(2,1)}, u32[]{:S(2)}, u32[]{:S(2)}) %collective-permute-start.1) | collective-permute-done | bytes 917536 | tf_op jit(solution)/shard_map/ppermute | solution.py:88
  100.5 13.4 %collective-permute-start.5 = (bf16[14,64,512]{2,1,0:T(8,128)(2,1)}, bf16[14,64,512]{2,1,0:T(8,128)(2,1)}, u32[]{:S(2)}, u32[]{:S(2)}) collective-permute-start(bf16[14,64,512]{2,1,0:T(8,128)(2,1)} %collective-permute-done.4), channel_id=1, source_target_pairs={{2,0},{4,2},{6,4},{7,6},{5,7},{3,5},{1,3},{0,1},{10,8},{12,10},{14... | collective-permute-start | bytes 2752520 | tf_op jit(solution)/shard_map/ppermute | solution.py:92
  114.0 3.9 %broadcast_in_dim.78 = bf16[8,14,64,512]{3,2,1,0:T(8,128)(2,1)} broadcast(bf16[]{:T(256)} %constant.94.clone.1), dimensions={} | broadcast | bytes 7340034 | tf_op jit(solution)/shard_map/broadcast_in_dim | solution.py:99
  123.1 10.6 %collective-permute-done.5 = bf16[14,64,512]{2,1,0:T(8,128)(2,1)} collective-permute-done((bf16[14,64,512]{2,1,0:T(8,128)(2,1)}, bf16[14,64,512]{2,1,0:T(8,128)(2,1)}, u32[]{:S(2)}, u32[]{:S(2)}) %collective-permute-start.5) | collective-permute-done | bytes 917536 | tf_op jit(solution)/shard_map/ppermute | solution.py:92
  138.8 3.3 collective-permute-done.3
  147.6 3.9 %collective-permute-done.6 = bf16[14,64,512]{2,1,0:T(8,128)(2,1)S(1)} collective-permute-done((bf16[14,64,512]{2,1,0:T(8,128)(2,1)}, bf16[14,64,512]{2,1,0:T(8,128)(2,1)S(1)}, u32[]{:S(2)}, u32[]{:S(2)}) %collective-permute-start.6) | collective-permute-done | bytes 917536 | tf_op jit(solution)/shard_map/ppermute | solution.py:92
  154.5 3.5 gather_fusion.2
  160.4 9.8 %bitcast_convert_fusion = bf16[896,512]{1,0:T(8,128)(2,1)} fusion(bf16[8,896,512]{2,1,0:T(8,128)(2,1)} %bitcast.17, bf16[8,512,512]{2,1,0:T(8,128)(2,1)} %bitcast.240), kind=kOutput, calls=%fused_computation.35 | convolution fusion | flops 3758555136 | bytes 12451840 | tf_op jit(solution)/shard_map/ktd,kdq->tq/dot_general | solution.py:138
  175.8 2.6 fusion.1
  178.4 3.2 fusion.20
  189.6 2.5 reshape.254
  192.0 3.6 %pad_maximum_fusion = f32[14,256,256]{1,2,0:T(8,128)} fusion(f32[14,256,128]{1,2,0:T(8,128)} %fusion.20, f32[14,256,128]{1,2,0:T(8,128)S(1)} %fusion.10), kind=kLoop, calls=%fused_computation.6 | loop fusion | flops 917504 | bytes 7340032 | tf_op jit(solution)/shard_map/concatenate | solution.py:185
  195.7 5.3 %copy.58 = f32[14,256,256]{2,0,1:T(8,128)} copy(f32[14,256,256]{1,2,0:T(8,128)} %pad_maximum_fusion) | data formatting | bytes 7340032 | tf_op jit(solution)/shard_map/concatenate | solution.py:185
  201.0 5.8 %convolution_convert_fusion = bf16[32,256,256]{2,0,1:T(8,128)(2,1)S(1)} fusion(f32[14,256,256]{2,0,1:T(8,128)} %copy.58, s32[32]{0:T(128)S(1)} %reshape.212, s32[14]{0:T(128)S(1)} %copy-done.10), kind=kOutput, calls=%fused_computation.17 | convolution fusion | flops 354419136 | bytes 7864504 | tf_op jit(solution)/shard_map/ap,pjc->ajc/dot_general | solution.py:194
  209.5 9.3 %convolution_convert_fusion.1 = bf16[8,512,512]{2,1,0:T(8,128)(2,1)} fusion(bf16[8,896,512]{2,1,0:T(8,128)(2,1)} %bitcast.17, bf16[896,512,1]{1,0,2:T(8,128)(2,1)S(1)} %copy-done.8), kind=kOutput, calls=%fused_computation.18 | convolution fusion | flops 3760193536 | bytes 12451840 | tf_op jit(solution)/shard_map/ktd,tq->kdq/dot_general | solution.py:176
  218.8 3.8 %fusion = bf16[16,256,256]{2,1,0:T(8,128)(2,1)} fusion(bf16[16,256,256]{2,1,0:T(8,128)(2,1)} %collective-permute-done.8, bf16[1,16,256,256]{3,1,0,2:T(8,128)(2,1)S(1)} %get-tuple-element.8), kind=kLoop, calls=%fused_computation.4 | loop fusion | flops 4194304 | bytes 6291456 | tf_op jit(solution)/shard_map/convert_element_type | solution.py:199
  222.6 11.3 %all-to-all-start.1 = ((bf16[16,256,256]{2,1,0:T(8,128)(2,1)}), bf16[16,256,256]{2,1,0:T(8,128)(2,1)S(1)}, u32[]{:S(2)}, u32[]{:S(2)}) async-start(bf16[16,256,256]{2,1,0:T(8,128)(2,1)} %fusion), calls=%async_computation.2 | async-start | bytes 4194304 | tf_op jit(solution)/shard_map/all_to_all | solution.py:198
  233.9 2.4 fusion.27
  236.3 2.6 fusion.28
  238.9 48.6 %all-to-all-done.1 = bf16[16,256,256]{2,1,0:T(8,128)(2,1)S(1)} async-done(((bf16[16,256,256]{2,1,0:T(8,128)(2,1)}), bf16[16,256,256]{2,1,0:T(8,128)(2,1)S(1)}, u32[]{:S(2)}, u32[]{:S(2)}) %all-to-all-start.1) | async-done | bytes 2097184 | tf_op jit(solution)/shard_map/all_to_all | solution.py:198
  288.6 66.4 %reduce-scatter.2.cloned.1.call-done = bf16[128,512]{1,0:T(8,128)(2,1)} async-done(((bf16[4096,512]{1,0:T(8,128)(2,1)}), bf16[128,512]{1,0:T(8,128)(2,1)}) %reduce-scatter.2.cloned.1.call-update) | async-done | bytes 131088 | tf_op jit(solution)/shard_map/reduce_scatter | solution.py:179
  (90 shorter events, 47.1 us)
Async XLA Ops:
  7.2 165.7 %copy-start = (bf16[14,64,128]{2,1,0:T(8,128)(2,1)S(1)}, bf16[14,64,128]{2,1,0:T(8,128)(2,1)}, u32[]{:S(2)}) copy-start(bf16[14,64,128]{2,1,0:T(8,128)(2,1)} %param.15) | copy-start | bytes 688132
  7.2 153.3 %all-gather.2.cloned.1.call-start = ((), (), s32[]{:S(2)}) async-start(), calls=%async_computation.3 | async-start | bytes 4325376 | tf_op jit(solution)/shard_map/all_gather | solution.py:136
  10.3 11.4 %copy-start.9 = (bf16[14,64,512]{2,1,0:T(8,128)(2,1)S(1)}, bf16[14,64,512]{2,1,0:T(8,128)(2,1)}, u32[]{:S(2)}) copy-start(bf16[14,64,512]{2,1,0:T(8,128)(2,1)} %param.13) | copy-start | bytes 2752516
  10.3 53.6 %copy-start.15 = (s32[8]{0:T(128)S(1)}, s32[8]{0:T(128)}, u32[]{:S(2)}) copy-start(s32[8]{0:T(128)} %constant.122) | copy-start | bytes 100
  10.3 54.2 %copy-start.14 = (s32[8]{0:T(128)S(1)}, s32[8]{0:T(128)}, u32[]{:S(2)}) copy-start(s32[8]{0:T(128)} %constant.109.clone) | copy-start | bytes 100
  10.3 73.2 %copy-start.2 = (s32[8]{0:T(128)S(1)}, s32[8]{0:T(128)}, u32[]{:S(2)}) copy-start(s32[8]{0:T(128)} %constant.108.clone) | copy-start | bytes 100
  10.3 103.6 %copy-start.10 = (s32[14]{0:T(128)S(1)}, s32[14]{0:T(128)}, u32[]{:S(2)}) copy-start(s32[14]{0:T(128)} %param.19) | copy-start | bytes 172
  10.4 108.5 %all-to-all-start = ((bf16[16,256,256]{2,1,0:T(8,128)(2,1)}), bf16[16,256,256]{2,1,0:T(8,128)(2,1)S(1)}, u32[]{:S(2)}, u32[]{:S(2)}) async-start(bf16[16,256,256]{2,1,0:T(8,128)(2,1)} %broadcast_in_dim.91), calls=%async_computation | async-start | bytes 4194304 | tf_op jit(solution)/shard_map/all_to_all | solution.py:150
  21.7 333.3 %reduce-scatter.2.cloned.1.call-start = ((), (), s32[]{:S(2)}) async-start(), calls=%async_computation.4 | async-start | bytes 4325376 | tf_op jit(solution)/shard_map/reduce_scatter | solution.py:179
  21.8 22.0 %collective-permute-start = (bf16[14,64,512]{2,1,0:T(8,128)(2,1)S(1)}, bf16[14,64,512]{2,1,0:T(8,128)(2,1)}, u32[]{:S(2)}, u32[]{:S(2)}) collective-permute-start(bf16[14,64,512]{2,1,0:T(8,128)(2,1)S(1)} %copy-done.9), channel_id=1, source_target_pairs={{0,2},{2,4},{4,6},{6,7},{7,5},{5,3},{3,1},{1,0},{8,10},{10,12},{12... | collective-permute-start | bytes 2752520 | tf_op jit(solution)/shard_map/ppermute | solution.py:88
  43.8 39.7 %collective-permute-start.1 = (bf16[14,64,512]{2,1,0:T(8,128)(2,1)}, bf16[14,64,512]{2,1,0:T(8,128)(2,1)}, u32[]{:S(2)}, u32[]{:S(2)}) collective-permute-start(bf16[14,64,512]{2,1,0:T(8,128)(2,1)} %collective-permute-done), channel_id=1, source_target_pairs={{0,2},{2,4},{4,6},{6,7},{7,5},{5,3},{3,1},{1,0},{8,10},{10,12},{12... | collective-permute-start | bytes 2752520 | tf_op jit(solution)/shard_map/ppermute | solution.py:88
  45.3 55.3 %collective-permute-start.4 = (bf16[14,64,512]{2,1,0:T(8,128)(2,1)S(1)}, bf16[14,64,512]{2,1,0:T(8,128)(2,1)}, u32[]{:S(2)}, u32[]{:S(2)}) collective-permute-start(bf16[14,64,512]{2,1,0:T(8,128)(2,1)S(1)} %copy-done.9), channel_id=1, source_target_pairs={{2,0},{4,2},{6,4},{7,6},{5,7},{3,5},{1,3},{0,1},{10,8},{12,10},{14... | collective-permute-start | bytes 2752520 | tf_op jit(solution)/shard_map/ppermute | solution.py:92
  83.5 35.3 %collective-permute-start.2 = (bf16[14,64,512]{2,1,0:T(8,128)(2,1)}, bf16[14,64,512]{2,1,0:T(8,128)(2,1)}, u32[]{:S(2)}, u32[]{:S(2)}) collective-permute-start(bf16[14,64,512]{2,1,0:T(8,128)(2,1)} %collective-permute-done.1), channel_id=1, source_target_pairs={{0,2},{2,4},{4,6},{6,7},{7,5},{5,3},{3,1},{1,0},{8,10},{10,12},{12... | collective-permute-start | bytes 2752520 | tf_op jit(solution)/shard_map/ppermute | solution.py:88
  100.5 33.2 %collective-permute-start.5 = (bf16[14,64,512]{2,1,0:T(8,128)(2,1)}, bf16[14,64,512]{2,1,0:T(8,128)(2,1)}, u32[]{:S(2)}, u32[]{:S(2)}) collective-permute-start(bf16[14,64,512]{2,1,0:T(8,128)(2,1)} %collective-permute-done.4), channel_id=1, source_target_pairs={{2,0},{4,2},{6,4},{7,6},{5,7},{3,5},{1,3},{0,1},{10,8},{12,10},{14... | collective-permute-start | bytes 2752520 | tf_op jit(solution)/shard_map/ppermute | solution.py:92
  118.8 35.6 %collective-permute-start.7 = (bf16[16,256,256]{2,1,0:T(8,128)(2,1)S(1)}, bf16[16,256,256]{2,1,0:T(8,128)(2,1)}, u32[]{:S(2)}, u32[]{:S(2)}) collective-permute-start(bf16[16,256,256]{2,1,0:T(8,128)(2,1)S(1)} %all-to-all-done), channel_id=1, source_target_pairs={{0,8},{8,0},{1,9},{9,1},{2,10},{10,2},{3,11},{11,3},{4,12},{12,4},... | collective-permute-start | bytes 6291464 | tf_op jit(solution)/shard_map/ppermute | solution.py:157
  118.8 23.3 %collective-permute-start.3 = (bf16[14,64,512]{2,1,0:T(8,128)(2,1)}, bf16[14,64,512]{2,1,0:T(8,128)(2,1)S(1)}, u32[]{:S(2)}, u32[]{:S(2)}) collective-permute-start(bf16[14,64,512]{2,1,0:T(8,128)(2,1)} %collective-permute-done.2), channel_id=1, source_target_pairs={{0,2},{2,4},{4,6},{6,7},{7,5},{5,3},{3,1},{1,0},{8,10},{10,12},{12... | collective-permute-start | bytes 2752520 | tf_op jit(solution)/shard_map/ppermute | solution.py:88
  133.7 17.8 %collective-permute-start.6 = (bf16[14,64,512]{2,1,0:T(8,128)(2,1)}, bf16[14,64,512]{2,1,0:T(8,128)(2,1)S(1)}, u32[]{:S(2)}, u32[]{:S(2)}) collective-permute-start(bf16[14,64,512]{2,1,0:T(8,128)(2,1)} %collective-permute-done.5), channel_id=1, source_target_pairs={{2,0},{4,2},{6,4},{7,6},{5,7},{3,5},{1,3},{0,1},{10,8},{12,10},{14... | collective-permute-start | bytes 2752520 | tf_op jit(solution)/shard_map/ppermute | solution.py:92
  160.4 15.2 %copy-start.5 = (bf16[14,256,256]{2,1,0:T(8,128)(2,1)}, bf16[14,256,256]{2,1,0:T(8,128)(2,1)S(1)}, u32[]{:S(2)}) copy-start(bf16[14,256,256]{2,1,0:T(8,128)(2,1)S(1)} %select_select_fusion) | copy-start | bytes 5505028
  173.9 8.9 %copy-start.3 = (f32[14,1,4,64,64]{3,4,2,0,1:T(8,128)}, f32[14,1,4,64,64]{3,4,2,0,1:T(8,128)S(1)}, u32[]{:S(2)}) copy-start(f32[14,1,4,64,64]{3,4,2,0,1:T(8,128)S(1)} %get-tuple-element.24) | copy-start | bytes 2752516
  178.4 3.2 copy-start.12
  209.5 9.3 %collective-permute-start.8 = (bf16[16,256,256]{2,1,0:T(8,128)(2,1)}, bf16[16,256,256]{2,1,0:T(8,128)(2,1)}, u32[]{:S(2)}, u32[]{:S(2)}) collective-permute-start(bf16[16,256,256]{2,1,0:T(8,128)(2,1)} %bitcast.237), channel_id=1, source_target_pairs={{0,8},{8,0},{1,9},{9,1},{2,10},{10,2},{3,11},{11,3},{4,12},{12,4},... | collective-permute-start | bytes 6291464 | tf_op jit(solution)/shard_map/ppermute | solution.py:109
  222.6 65.0 %all-to-all-start.1 = ((bf16[16,256,256]{2,1,0:T(8,128)(2,1)}), bf16[16,256,256]{2,1,0:T(8,128)(2,1)S(1)}, u32[]{:S(2)}, u32[]{:S(2)}) async-start(bf16[16,256,256]{2,1,0:T(8,128)(2,1)} %fusion), calls=%async_computation.2 | async-start | bytes 4194304 | tf_op jit(solution)/shard_map/all_to_all | solution.py:198
  233.9 2.4 copy-start.4
  236.3 118.7 %copy-start.1 = (bf16[14,64,128]{2,1,0:T(8,128)(2,1)S(1)}, bf16[14,64,128]{2,1,0:T(8,128)(2,1)}, u32[]{:S(2)}) copy-start(bf16[14,64,128]{2,1,0:T(8,128)(2,1)} %param.15) | copy-start | bytes 688132
  (5 other events, 9.5 us)
Sparse Core Ops, SparseCore 0:
  10.8 104.7 all-gather.1
  218.9 136.0 reduce-scatter.1
